TPU v7x, 128 devices: a whole 4x4x4 slice. The times are simulated.
128 devices in a mesh: rad: 8 (over y, core), mode: 16 (over z, x).
Axes of the slice: x: 4, y: 4, z: 4, core: 2. Of those that a mesh axis runs over, the one named last changes fastest.
Arguments:
- spectra: bfloat16 [2, 256, 1024, 1024], P(None, 'mode', 'rad'), may hold values from -6 to 6
- diffusivity: float32 [1024], replicated, may hold values from 0.1 to 1
- eigenvalues: float32 [1024], replicated, may hold values from 0.3 to 3
- radial_basis: bfloat16 [1024, 1024], replicated, may hold values from -0.1875 to 0.1875
- dual_basis: bfloat16 [1024, 1024], replicated, may hold values from -0.1875 to 0.1875
- degree_count: int32 [256], replicated, may hold values from 1 to 1024, as said below
- order_slot: int32 [256], replicated, may hold values from 0 to 255, as said below
Outputs:
- stepped: bfloat16 [2, 256, 1024, 1024], P(None, 'mode', 'rad')
Inputs may be any that keep to these rules, and one draw needn't show every extreme that they name: `degree_count`: row i holds order m_i = floor(i * 2); at most 1024 - m_i of its slots are live, and row 0 has all 1024. `order_slot`: A permutation of the rows. Output row d * 16 + s + k takes an input row of block s, that is one of s * 16 to (s + 1) * 16 - 1.
All inputs are finite; a program needn't handle non-finite values.
Results may differ from a plain program's by a relative error of at most 0.0065.
Values may be sent and summed in bfloat16 or wider, within the bound.
No kernel may reach another device: no remote copies, remote signals or barrier semaphores. Data moves between devices by JAX's collectives and lax.ppermute only.
A program may use at most 192 MiB of HBM per device.

v0:
```python
import jax
import jax.numpy as jnp
from jax import lax
from jax.sharding import PartitionSpec as P


def extended(shard, sides, width):
    for axis, dim in sides:
        count, length = (lax.axis_size(axis), shard.shape[dim])
        up = [(i, (i + 1) % count) for i in range(count - 1)]
        down = [(j, i) for i, j in up]
        last = lax.slice_in_dim(shard, length - width, length, axis=dim)
        first = lax.slice_in_dim(shard, 0, width, axis=dim)
        before = lax.ppermute(last, axis, up)
        after = lax.ppermute(first, axis, down)
        shard = jnp.concatenate([before, shard, after], axis=dim)
    return shard


def degree_table(
    counts, order_start, order_rows, slot_start, slot_width, slots_total, orders_total
):
    row_ids = order_start + jnp.arange(order_rows, dtype=jnp.int32)
    orders = row_ids * slots_total // (2 * orders_total)
    slot_ids = slot_start + jnp.arange(slot_width, dtype=jnp.int32)
    degree = (orders[:, None] + slot_ids[None, :]).astype(jnp.float32)
    limits = lax.dynamic_slice_in_dim(counts, order_start, order_rows)
    live_mask = slot_ids[None, :] < limits[:, None]
    return (degree, live_mask)


def explicit(padded, kappa_rows, radius_start, degree, live_mask, shells_total):
    center = padded[:, :, 2:-2]
    shell_rows = center.shape[2]
    second = (
        -padded[:, :, :-4]
        + 16.0 * padded[:, :, 1:-3]
        - 30.0 * center
        + 16.0 * padded[:, :, 3:-1]
        - padded[:, :, 4:]
    ) / 12.0
    radius = (
        1.2
        + (radius_start + jnp.arange(shell_rows, dtype=jnp.int32)).astype(jnp.float32)
        / shells_total
    )
    damping = (degree * (degree + 1.0))[None, :, None, :] / ((shells_total * radius) ** 2)[
        None, None, :, None
    ]
    updated = center + 0.5 * kappa_rows[None, None, :, None] * (second - damping * center)
    return jnp.where(live_mask[None, :, None, :], updated, 0.0).astype(jnp.bfloat16)


def on_device(
    spectra, diffusivity, eigenvalues, radial_basis, dual_basis, degree_count, order_slot
):
    orders_here = spectra.shape[1]
    shells_here = spectra.shape[2]
    slots_total = spectra.shape[3]
    shells_total = diffusivity.shape[0]
    orders_total = degree_count.shape[0]
    groups = lax.axis_size("mode")
    shell_groups = lax.axis_size("rad")
    per_group = orders_here // groups
    window = slots_total // shell_groups
    group_index = lax.axis_index("mode")
    order_start = group_index * orders_here
    slot_start = lax.axis_index("rad") * window
    degree_win, live_win = degree_table(
        degree_count, order_start, orders_here, slot_start, window, slots_total, orders_total
    )
    degree_all, live_all = degree_table(
        degree_count, order_start, orders_here, 0, slots_total, slots_total, orders_total
    )
    padded = extended(spectra, (("rad", 2),), 2).astype(jnp.float32)
    radius_start = lax.axis_index("rad") * shells_here
    kappa_rows = lax.dynamic_slice_in_dim(diffusivity, radius_start, shells_here)
    updated = explicit(padded, kappa_rows, radius_start, degree_all, live_all, shells_total)
    relaid = lax.all_to_all(updated, "rad", split_axis=3, concat_axis=2, tiled=True)
    identity = jnp.eye(shells_total, dtype=jnp.float32)
    basis_full = (identity + radial_basis.astype(jnp.float32)).astype(jnp.bfloat16)
    dual_full = (identity + dual_basis.astype(jnp.float32)).astype(jnp.bfloat16)
    projected = jnp.einsum("kr,cirj->cikj", dual_full, relaid, preferred_element_type=jnp.float32)
    divisor = eigenvalues[None, None, :, None] + 0.5 * (degree_win * (degree_win + 1.0))[
        None, :, None, :
    ] / (shells_total * shells_total)
    scaled = (projected / divisor).astype(jnp.bfloat16)
    restored = jnp.einsum("kr,cirj->cikj", basis_full, scaled, preferred_element_type=jnp.float32)
    solved = jnp.where(live_win[None, :, None, :], restored, 0.0).astype(jnp.bfloat16)
    targets = lax.dynamic_slice_in_dim(
        order_slot.reshape(groups, orders_here), group_index * per_group, per_group, 1
    )
    picked_rows = targets.reshape(orders_here) - order_start
    sendable = jnp.take(solved, picked_rows, axis=1)
    stepped = lax.all_to_all(
        lax.all_to_all(sendable, "rad", split_axis=2, concat_axis=3, tiled=True),
        "mode",
        split_axis=1,
        concat_axis=1,
        tiled=True,
    )
    return stepped


def solution(mesh):
    placed = (P(None, "mode", "rad", None), P(), P(), P(), P(), P(), P())
    return jax.shard_map(
        on_device,
        mesh=mesh,
        in_specs=placed,
        out_specs=P(None, "mode", "rad", None),
        check_vma=False,
    )
```

profile of v0, /device:TPU:1, one launch (start us, length us, event | category | flops | bytes accessed | tf_op | source)
XLA Modules:
  0.0 482.7 jit_solution(1554725865413892524)
XLA Ops:
  0.0 1.4 fusion.26
  1.4 4.6 collective-permute-start
  6.0 1.9 collective-permute-start.1
  8.0 0.1 add_multiply_fusion
  8.1 0.8 dynamic_slice.11
  8.8 4.5 broadcast_divide_fusion
  13.3 0.1 iota_compare_fusion.1
  13.4 0.8 dynamic-slice_multiply_fusion
  14.2 0.0 collective-permute-done
  14.2 0.0 collective-permute-done.1
  14.2 10.6 %maximum_convert_fusion = f32[2,16,132,1024]{3,2,1,0:T(8,128)} fusion(bf16[2,16,2,1024]{3,2,1,0:T(2,128)(2,1)S(1)} %collective-permute-done.1, bf16[2,16,128,1024]{3,2,1,0:T(8,128)(2,1)} %param.7, bf16[2,16,2,1024]{3,2,1,0:T(2,128)(2,1)S(1)} %collective-permute-done), kind=kLoop, calls=%fused_computation.17 | loop fusion | flops 25952256 | bytes 25952256 | tf_op jit(solution)/shard_map/convert_element_type | solution.py:75
  24.9 36.2 %fusion.5 = bf16[2,16,128,1024]{3,2,1,0:T(8,128)(2,1)} fusion(f32[2,16,132,1024]{3,2,1,0:T(8,128)} %maximum_convert_fusion, f32[16,128,1024]{2,1,0:T(8,128)} %broadcast_divide_fusion, f32[128]{0:T(128)S(1)} %dynamic-slice_multiply_fusion, pred[16,1024]{1,0:T(8,128)(4,1)S(1)} %iota_compare_fusion.1), kind=kLoop, calls=%fused_computation.7 | loop fusion | flops 62914560 | bytes 100680192 | tf_op jit(solution)/shard_map/convert_element_type | solution.py:51
  61.0 12.5 %copy.19 = bf16[2,16,128,1024]{2,1,0,3:T(8,128)(2,1)} copy(bf16[2,16,128,1024]{3,2,1,0:T(8,128)(2,1)} %fusion.5) | data formatting | bytes 16777216 | tf_op jit(solution)/shard_map/convert_element_type | solution.py:51
  73.5 0.0 copy-start.1
  73.5 0.0 copy-start
  73.5 5.3 %all-to-all-start = ((bf16[2,16,128,1024]{2,1,0,3:T(8,128)(2,1)}), bf16[2,16,128,1024]{2,1,0,3:T(8,128)(2,1)}, u32[]{:S(2)}, u32[]{:S(2)}) async-start(bf16[2,16,128,1024]{2,1,0,3:T(8,128)(2,1)} %copy.19), calls=%async_computation | async-start | bytes 16777216 | tf_op jit(solution)/shard_map/all_to_all | solution.py:79
  78.8 0.0 copy-done.1
  78.8 0.1 reshape.151
  78.9 0.2 fusion.25
  79.0 0.2 and_reduce_fusion
  79.3 0.1 broadcast_compare_fusion
  79.3 0.1 fusion.24
  79.4 0.0 copy-done
  79.4 4.0 broadcast_add_fusion
  83.4 88.7 %all-to-all-done = bf16[2,16,128,1024]{2,1,0,3:T(8,128)(2,1)} async-done(((bf16[2,16,128,1024]{2,1,0,3:T(8,128)(2,1)}), bf16[2,16,128,1024]{2,1,0,3:T(8,128)(2,1)}, u32[]{:S(2)}, u32[]{:S(2)}) %all-to-all-start) | async-done | bytes 8388640 | tf_op jit(solution)/shard_map/all_to_all | solution.py:79
  172.2 0.0 copy-start.2
  172.2 12.3 %copy.21 = bf16[2,16,8,128,128]{4,3,2,1,0:T(8,128)(2,1)} copy(bf16[2,16,8,128,128]{3,1,0,4,2:T(8,128)(2,1)} %bitcast.2) | data formatting | bytes 16777216 | tf_op jit(solution)/shard_map/all_to_all | solution.py:79
  184.5 0.0 copy-done.2
  184.5 24.4 %fusion.10 = bf16[2,16,1024,128]{2,3,1,0:T(8,128)(2,1)} fusion(pred[16,128]{1,0:T(8,128)(4,1)S(1)} %broadcast_compare_fusion, f32[16,1024,128]{1,2,0:T(8,128)} %broadcast_add_fusion, bf16[2,16,1024,128]{3,2,1,0:T(8,128)(2,1)} %bitcast.35, bf16[1024,1024]{1,0:T(8,128)(2,1)S(1)} %copy-done.2, bf16[1024,1024]{1,0:T(8,128)(2,1)} %param.11), kind=kOutput, calls=%fused_computation.18 | convolution fusion | flops 17207132160 | bytes 29362176 | tf_op jit(solution)/shard_map/kr,cirj->cikj/dot_general | solution.py:88
  208.8 8.3 %gather_fusion = bf16[16,2,1024,128]{2,3,1,0:T(8,128)(2,1)} fusion(bf16[2,16,1024,128]{2,3,1,0:T(8,128)(2,1)} %fusion.10, s32[1024]{0:T(1024)S(1)} %pad_clamp_fusion), kind=kCustom, calls=%fused_computation | custom fusion | bytes 16777280 | tf_op jit(solution)/shard_map/jit(_take)/gather | solution.py:94
  217.1 7.6 %select_bitcast_fusion = bf16[2,16,1024,128]{2,3,0,1:T(8,128)(2,1)} fusion(bf16[16,2,1024,128]{2,3,1,0:T(8,128)(2,1)} %gather_fusion, pred[16]{0:T(512)(128)(4,1)S(1)} %and_reduce_fusion), kind=kLoop, calls=%fused_computation.19 | loop fusion | flops 4194304 | bytes 16777232 | tf_op jit(solution)/shard_map/jit(_take)/select_n | solution.py:94
  224.8 21.2 %copy.23 = bf16[2,16,1024,128]{3,0,1,2:T(2,128)(2,1)} copy(bf16[2,16,1024,128]{2,3,0,1:T(8,128)(2,1)} %select_bitcast_fusion) | data formatting | bytes 16777216 | tf_op jit(solution)/shard_map/jit(_take)/select_n | solution.py:94
  246.0 100.5 %all_to_all.41 = bf16[2,16,1024,128]{3,0,1,2:T(2,128)(2,1)} all-to-all(bf16[2,16,1024,128]{3,0,1,2:T(2,128)(2,1)} %copy.23), channel_id=1, replica_groups=mesh['rad'=8,'mode'=16] {'rad'}, dimensions={2} | all-to-all | bytes 16777216 | tf_op jit(solution)/shard_map/all_to_all | solution.py:96
  346.5 12.2 %copy.24 = bf16[2,16,128,8,128]{4,3,2,0,1:T(8,128)(2,1)} copy(bf16[2,16,128,8,128]{4,0,1,2,3:T(2,128)(2,1)} %bitcast.34) | data formatting | bytes 16777216 | tf_op jit(solution)/shard_map/all_to_all | solution.py:96
  358.7 13.3 %all_to_all.36 = bf16[2,16,128,1024]{3,2,0,1:T(8,128)(2,1)} reshape(bf16[2,16,128,8,128]{4,3,2,0,1:T(8,128)(2,1)} %copy.24) | data formatting | bytes 16777216 | tf_op jit(solution)/shard_map/all_to_all | solution.py:96
  372.0 102.3 %all_to_all.42 = bf16[2,16,128,1024]{3,2,0,1:T(8,128)(2,1)} all-to-all(bf16[2,16,128,1024]{3,2,0,1:T(8,128)(2,1)} %all_to_all.36), channel_id=1, replica_groups=mesh['rad'=8,'mode'=16] {'mode'}, dimensions={1} | all-to-all | bytes 16777216 | tf_op jit(solution)/shard_map/all_to_all | solution.py:95
  474.3 8.4 %copy.25 = bf16[2,16,128,1024]{3,2,1,0:T(8,128)(2,1)} copy(bf16[2,16,128,1024]{3,2,0,1:T(8,128)(2,1)} %all_to_all.42) | data formatting | bytes 16777216 | tf_op jit(solution)/shard_map/all_to_all | solution.py:95
  (4 shorter events, 0.0 us)
Async XLA Ops:
  1.4 12.8 %collective-permute-start = (bf16[2,16,2,1024]{3,2,1,0:T(2,128)(2,1)S(1)}, bf16[2,16,2,1024]{3,2,1,0:T(2,128)(2,1)S(1)}, u32[]{:S(2)}, u32[]{:S(2)}) collective-permute-start(bf16[2,16,2,1024]{3,2,1,0:T(2,128)(2,1)S(1)} %get-tuple-element.5), channel_id=1, source_target_pairs={{0,16},{16,32},{32,48},{48,64},{64,80},{80,96},{96,112},{1,17},{17... | collective-permute-start | bytes 393224 | tf_op jit(solution)/shard_map/ppermute | solution.py:14
  6.0 8.2 %collective-permute-start.1 = (bf16[2,16,2,1024]{3,2,1,0:T(2,128)(2,1)S(1)}, bf16[2,16,2,1024]{3,2,1,0:T(2,128)(2,1)S(1)}, u32[]{:S(2)}, u32[]{:S(2)}) collective-permute-start(bf16[2,16,2,1024]{3,2,1,0:T(2,128)(2,1)S(1)} %get-tuple-element.6), channel_id=1, source_target_pairs={{16,0},{32,16},{48,32},{64,48},{80,64},{96,80},{112,96},{17,1},{33... | collective-permute-start | bytes 393224 | tf_op jit(solution)/shard_map/ppermute | solution.py:15
  73.5 5.3 %copy-start.1 = (s32[256]{0:T(256)S(1)}, s32[256]{0:T(256)}, u32[]{:S(2)}) copy-start(s32[256]{0:T(256)} %param.13) | copy-start | bytes 3076
  73.5 5.9 %copy-start = (f32[1024]{0:T(1024)S(1)}, f32[1024]{0:T(1024)}, u32[]{:S(2)}) copy-start(f32[1024]{0:T(1024)} %param.9) | copy-start | bytes 12292
  73.5 98.7 %all-to-all-start = ((bf16[2,16,128,1024]{2,1,0,3:T(8,128)(2,1)}), bf16[2,16,128,1024]{2,1,0,3:T(8,128)(2,1)}, u32[]{:S(2)}, u32[]{:S(2)}) async-start(bf16[2,16,128,1024]{2,1,0,3:T(8,128)(2,1)} %copy.19), calls=%async_computation | async-start | bytes 16777216 | tf_op jit(solution)/shard_map/all_to_all | solution.py:79
  172.2 12.3 %copy-start.2 = (bf16[1024,1024]{1,0:T(8,128)(2,1)S(1)}, bf16[1024,1024]{1,0:T(8,128)(2,1)}, u32[]{:S(2)}) copy-start(bf16[1024,1024]{1,0:T(8,128)(2,1)} %param.10) | copy-start | bytes 6291460
where the time goes:
time: 485 us; the launch traced here: 483 us
  blocking collectives  203 us (42%)
  local copies, waits for them, and re-layouts  90.4 us (19%)
  waiting for transfers between devices  88.7 us (18%)
  other arithmetic  64.5 us (13%)
  matrix products  24.4 us (5%)
  starting transfers between devices  11.8 us (2%)
    all_to_all x1, blocking collectives, on_device(): lax.all_to_all(lax.all_to_all(sendable, 'rad', split_axis=2, concat_axis=...  102 us
    all_to_all x1, blocking collectives, on_device(): lax.all_to_all(sendable, 'rad', split_axis=2, concat_axis=3, tiled=True)  101 us
    all_to_all x1, waiting for transfers between devices, on_device(): lax.all_to_all(updated, 'rad', split_axis=3, concat_axis=2, tiled=True)  88.7 us
    convert_element_type x1, other arithmetic, explicit(): jnp.where(live_mask[None, :, None, :], updated, 0.0).astype(jnp.bfloat16)  36.2 us
    all_to_all x2, local copies, waits for them, and re-layouts, on_device(): lax.all_to_all(sendable, 'rad', split_axis=2, concat_axis=3, tiled=True)  25.5 us
    dot_general x1, matrix products, on_device(): jnp.einsum('kr,cirj->cikj', basis_full, scaled, preferred_element_type=jn...  24.4 us
    select_n x1, local copies, waits for them, and re-layouts, on_device(): sendable = jnp.take(solved, picked_rows, axis=1)  21.2 us
    convert_element_type x1, local copies, waits for them, and re-layouts, explicit(): jnp.where(live_mask[None, :, None, :], updated, 0.0).astype(jnp.bfloat16)  12.5 us
  transfers between devices with their start and end apart: 3, of which 1 were waited for; matrix products, arithmetic and copies ran while one was open for 2% of the time, Pallas kernels for 0%

commit v1 on v0

v1 whole, which is shorter than its diff:
```python
import jax
import jax.numpy as jnp
from jax import lax
from jax.sharding import PartitionSpec as P


def explicit(padded, kappa_rows, radius_start, degree, live_mask, shells_total):
    center = padded[:, :, 2:-2]
    shell_rows = center.shape[2]
    second = (
        -padded[:, :, :-4]
        + 16.0 * padded[:, :, 1:-3]
        - 30.0 * center
        + 16.0 * padded[:, :, 3:-1]
        - padded[:, :, 4:]
    ) / 12.0
    radius = (
        1.2
        + (radius_start + jnp.arange(shell_rows, dtype=jnp.int32)).astype(jnp.float32)
        / shells_total
    )
    damping = (degree * (degree + 1.0))[None, :, None, :] / ((shells_total * radius) ** 2)[
        None, None, :, None
    ]
    updated = center + 0.5 * kappa_rows[None, None, :, None] * (second - damping * center)
    return jnp.where(live_mask[None, :, None, :], updated, 0.0).astype(jnp.bfloat16)


def on_device(
    spectra, diffusivity, eigenvalues, radial_basis, dual_basis, degree_count, order_slot
):
    comps, rows_here, shells_here, slots_total = spectra.shape
    shells_total = diffusivity.shape[0]
    orders_total = degree_count.shape[0]
    groups = lax.axis_size("mode")
    nrad = lax.axis_size("rad")
    per_group = rows_here // groups
    window = slots_total // nrad
    me_mode = lax.axis_index("mode")
    me_rad = lax.axis_index("rad")

    picks = (
        lax.dynamic_slice_in_dim(
            order_slot.reshape(groups, groups, per_group), me_mode, 1, 1
        ).reshape(groups * per_group)
        - me_mode * rows_here
    )
    chosen = jnp.take(spectra, picks, axis=1)
    send = chosen.reshape(comps, groups, per_group, shells_here, nrad, window)
    send = send.transpose(1, 4, 0, 2, 3, 5).reshape(
        groups * nrad, comps, per_group, shells_here, window
    )
    recv = lax.all_to_all(send, ("mode", "rad"), 0, 0, tiled=True)
    local = recv.reshape(groups, nrad, comps, per_group, shells_here, window)
    local = local.transpose(2, 0, 3, 1, 4, 5).reshape(comps, rows_here, shells_total, window)

    out_rows = me_mode * rows_here + jnp.arange(rows_here, dtype=jnp.int32)
    in_rows = jnp.take(order_slot, out_rows)
    orders = in_rows * slots_total // (2 * orders_total)
    slot_ids = me_rad * window + jnp.arange(window, dtype=jnp.int32)
    degree = (orders[:, None] + slot_ids[None, :]).astype(jnp.float32)
    live = slot_ids[None, :] < jnp.take(degree_count, in_rows)[:, None]

    padded = jnp.pad(local.astype(jnp.float32), ((0, 0), (0, 0), (2, 2), (0, 0)))
    updated = explicit(padded, diffusivity, 0, degree, live, shells_total)

    identity = jnp.eye(shells_total, dtype=jnp.float32)
    basis_full = (identity + radial_basis.astype(jnp.float32)).astype(jnp.bfloat16)
    dual_full = (identity + dual_basis.astype(jnp.float32)).astype(jnp.bfloat16)
    projected = jnp.einsum("kr,cirj->cikj", dual_full, updated, preferred_element_type=jnp.float32)
    divisor = eigenvalues[None, None, :, None] + 0.5 * (degree * (degree + 1.0))[
        None, :, None, :
    ] / (shells_total * shells_total)
    scaled = (projected / divisor).astype(jnp.bfloat16)
    restored = jnp.einsum("kr,cirj->cikj", basis_full, scaled, preferred_element_type=jnp.float32)
    solved = jnp.where(live[None, :, None, :], restored, 0.0).astype(jnp.bfloat16)

    back = solved.reshape(comps, rows_here, nrad, shells_here, window).transpose(2, 0, 1, 3, 4)
    got = lax.all_to_all(back, "rad", 0, 0, tiled=True)
    return got.transpose(1, 2, 3, 0, 4).reshape(comps, rows_here, shells_here, slots_total)


def solution(mesh):
    placed = (P(None, "mode", "rad", None), P(), P(), P(), P(), P(), P())
    return jax.shard_map(
        on_device,
        mesh=mesh,
        in_specs=placed,
        out_specs=P(None, "mode", "rad", None),
        check_vma=False,
    )
```

time: 485 us -> 353 us (0.73)
  blocking collectives: 203 us -> 101 us
  other arithmetic: 64.5 us -> 16.2 us
  matrix products: 24.4 us -> 57.6 us
  local copies, waits for them, and re-layouts: 90.4 us -> 76.7 us
    all_to_all x2 -> x1, blocking collectives: 203 us -> 101 us  [on_device(): got = lax.all_to_all(back, 'rad', 0, 0, tiled=True)]
    convert_element_type x2 -> x0, other arithmetic: 46.8 us -> none  [the longest x1 36.2 us: explicit(): jnp.where(live_mask[None, :, None, :], updated, 0.0).astype(jnp.bfloat16)]
    dot_general x0 -> x1, matrix products: none -> 40.9 us  [on_device(): jnp.einsum('kr,cirj->cikj', dual_full, updated, preferred_element_type=jn...]
    all_to_all x4 -> x1, local copies, waits for them, and re-layouts: 46.2 us -> 10.3 us  [on_device(): got = lax.all_to_all(back, 'rad', 0, 0, tiled=True)]
    reshape x1 -> x4, local copies, waits for them, and re-layouts: 0.08 us -> 33.6 us  [the longest x1 12 us: on_device(): send.transpose(1, 4, 0, 2, 3, 5)]
    select_n x1 -> x0, local copies, waits for them, and re-layouts: 21.2 us -> none  [on_device(): sendable = jnp.take(solved, picked_rows, axis=1)]
    gather x1 -> x4, local copies, waits for them, and re-layouts: 8.31 us -> 21.5 us  [the longest x2 20.2 us: on_device(): chosen = jnp.take(spectra, picks, axis=1)]
    dot_general x1, matrix products: 24.4 us -> 16.7 us  [on_device(): jnp.einsum('kr,cirj->cikj', basis_full, scaled, preferred_element_type=jn...]
  transfers between devices with their start and end apart: 3 -> 1, of which waited for: 1 -> 1; matrix products, arithmetic and copies ran while one was open for 2% -> 3% of each run, Pallas kernels for 0% -> 0%
where the time goes in v1:
time: 353 us; the launch traced here: 352 us
  blocking collectives  101 us (29%)
  waiting for transfers between devices  88.2 us (25%)
  local copies, waits for them, and re-layouts  76.7 us (22%)
  matrix products  57.6 us (16%)
  other arithmetic  16.2 us (5%)
  starting transfers between devices  12 us (3%)
    all_to_all x1, blocking collectives, on_device(): got = lax.all_to_all(back, 'rad', 0, 0, tiled=True)  101 us
    all_to_all x1, waiting for transfers between devices, on_device(): recv = lax.all_to_all(send, ('mode', 'rad'), 0, 0, tiled=True)  88.2 us
    dot_general x1, matrix products, on_device(): jnp.einsum('kr,cirj->cikj', dual_full, updated, preferred_element_type=jn...  40.9 us
    gather x2, local copies, waits for them, and re-layouts, on_device(): chosen = jnp.take(spectra, picks, axis=1)  20.2 us
    dot_general x1, matrix products, on_device(): jnp.einsum('kr,cirj->cikj', basis_full, scaled, preferred_element_type=jn...  16.7 us
    reshape x1, local copies, waits for them, and re-layouts, on_device(): send.transpose(1, 4, 0, 2, 3, 5)  12 us
    all_to_all x1, starting transfers between devices, on_device(): recv = lax.all_to_all(send, ('mode', 'rad'), 0, 0, tiled=True)  12 us
    reshape x1, local copies, waits for them, and re-layouts, on_device(): got.transpose(1, 2, 3, 0, 4)  11.8 us
  transfers between devices with their start and end apart: 1, of which 1 were waited for; matrix products, arithmetic and copies ran while one was open for 3% of the time, Pallas kernels for 0%

profile of v1, /device:TPU:1, one launch (start us, length us, event | category | flops | bytes accessed | tf_op | source)
XLA Modules:
  0.0 351.7 jit_solution(17975685433454107822)
XLA Ops:
  0.0 0.0 copy-start
  0.0 0.8 reshape.172
  0.8 0.2 subtract_reduce_fusion
  1.0 8.3 %gather_fusion = bf16[16,2,128,1024]{3,2,1,0:T(8,128)(2,1)} fusion(bf16[2,16,128,1024]{3,2,1,0:T(8,128)(2,1)} %param.9, s32[1024]{0:T(1024)S(1)} %pad_clamp_fusion), kind=kCustom, calls=%fused_computation.2 | custom fusion | bytes 16777280 | tf_op jit(solution)/shard_map/jit(_take)/gather | solution.py:48
  9.3 11.9 %copy.25 = bf16[2,16,128,1024]{2,3,1,0:T(8,128)(2,1)} copy(bf16[2,16,128,1024]{3,2,0,1:T(8,128)(2,1)} %bitcast.45) | data formatting | bytes 16777216 | tf_op jit(solution)/shard_map/jit(_take)/gather | solution.py:48
  21.2 7.6 %broadcast_select_fusion = bf16[2,16,1,128,8,128]{3,5,4,1,0,2:T(8,128)(2,1)} fusion(bf16[2,16,1,128,8,128]{3,5,4,1,0,2:T(8,128)(2,1)} %bitcast.43, pred[16]{0:T(512)(128)(4,1)S(1)} %compare_and_fusion), kind=kLoop, calls=%fused_computation.16 | loop fusion | flops 4194304 | bytes 16777232 | tf_op jit(solution)/shard_map/jit(_take)/select_n | solution.py:48
  28.9 12.0 %copy.27 = bf16[128,2,1,128,128]{4,3,1,2,0:T(8,128)(2,1)} copy(bf16[128,2,1,128,128]{3,4,0,1,2:T(8,128)(2,1)} %bitcast.44) | data formatting | bytes 16777216 | tf_op jit(solution)/shard_map/reshape | solution.py:50
  40.8 0.0 copy-start.2
  40.8 0.0 copy-start.4
  40.8 0.0 copy-start.3
  40.8 12.0 %all-to-all-start = ((bf16[128,2,1,128,128]{4,3,1,2,0:T(8,128)(2,1)}), bf16[128,2,1,128,128]{4,3,1,2,0:T(8,128)(2,1)}, u32[]{:S(2)}, u32[]{:S(2)}) async-start(bf16[128,2,1,128,128]{4,3,1,2,0:T(8,128)(2,1)} %copy.27), calls=%async_computation | async-start | bytes 16777216 | tf_op jit(solution)/shard_map/all_to_all | solution.py:53
  52.8 0.0 copy-done.2
  52.8 0.7 gather_fusion.1
  53.5 0.0 copy-done
  53.5 0.7 gather_fusion.2
  54.2 0.1 broadcast_compare_fusion
  54.3 0.0 copy-done.4
  54.3 0.1 broadcast_multiply_fusion
  54.4 0.0 copy-done.3
  54.4 3.8 %broadcast_add_fusion = f32[16,1024,128]{1,2,0:T(8,128)} fusion(f32[16,128]{1,0:T(8,128)S(1)} %get-tuple-element.8, f32[1024]{0:T(1024)S(1)} %copy-done.3), kind=kLoop, calls=%fused_computation.22 | loop fusion | flops 2097152 | bytes 8400896 | tf_op jit(solution)/shard_map/add | solution.py:71
  58.2 4.3 %broadcast_divide_fusion = f32[16,1024,128]{2,1,0:T(8,128)} fusion(f32[1024]{0:T(1024)S(1)} %multiply_multiply_fusion, f32[16,128]{1,0:T(8,128)S(1)} %get-tuple-element.9), kind=kLoop, calls=%fused_computation.24 | loop fusion | flops 2097152 | bytes 8400896 | tf_op jit(solution)/shard_map/div | solution.py:22
  62.6 0.0 copy-start.5
  62.6 88.2 %all-to-all-done = bf16[128,2,1,128,128]{4,3,1,2,0:T(8,128)(2,1)} async-done(((bf16[128,2,1,128,128]{4,3,1,2,0:T(8,128)(2,1)}), bf16[128,2,1,128,128]{4,3,1,2,0:T(8,128)(2,1)}, u32[]{:S(2)}, u32[]{:S(2)}) %all-to-all-start) | async-done | bytes 8388640 | tf_op jit(solution)/shard_map/all_to_all | solution.py:53
  150.8 11.2 %copy.28 = f32[128,2,1,128,128]{4,3,0,1,2:T(8,128)} copy(bf16[128,2,1,128,128]{4,3,1,2,0:T(8,128)(2,1)} %all-to-all-done) | data formatting | bytes 25165824 | tf_op jit(solution)/shard_map/convert_element_type | solution.py:64
  162.0 0.0 copy-done.5
  162.0 40.9 %fusion.8 = f32[2,16,128,1024]{3,2,1,0:T(8,128)} fusion(f32[2,16,1024,128]{3,2,1,0:T(8,128)} %bitcast.48, f32[16,1024,128]{2,1,0:T(8,128)} %broadcast_divide_fusion, f32[1024]{0:T(1024)S(1)} %broadcast_multiply_fusion.1, pred[16,128]{1,0:T(8,128)(4,1)S(1)} %broadcast_compare_fusion, bf16[1024,1024]{1,0:T(8,128)(2,1)S(1)} %copy-done.5), kind=kOutput, calls=%fused_computation.17 | convolution fusion | flops 8658092032 | bytes 44046336 | tf_op jit(solution)/shard_map/kr,cirj->cikj/dot_general | solution.py:70
  202.9 16.7 %fusion.5 = bf16[2,16,16,8,8,128]{5,4,3,2,1,0:T(8,128)(2,1)} fusion(pred[16,128]{1,0:T(8,128)(4,1)S(1)} %broadcast_compare_fusion, f32[2,16,128,1024]{3,2,1,0:T(8,128)} %fusion.8, f32[16,1024,128]{1,2,0:T(8,128)} %broadcast_add_fusion, bf16[1024,1024]{1,0:T(8,128)(2,1)} %param.12), kind=kOutput, calls=%fused_computation.13 | convolution fusion | flops 8611954688 | bytes 35653632 | tf_op jit(solution)/shard_map/kr,cirj->cikj/dot_general | solution.py:75
  219.6 9.0 %copy.40 = bf16[2,16,16,8,8,128]{5,4,2,1,0,3:T(8,128)(2,1)} copy(bf16[2,16,16,8,8,128]{5,4,3,2,1,0:T(8,128)(2,1)} %fusion.5) | data formatting | bytes 16777216 | tf_op jit(solution)/shard_map/reshape | solution.py:78
  228.6 100.9 %all_to_all.10 = bf16[8,2,16,128,128]{3,4,2,1,0:T(8,128)(2,1)} all-to-all(bf16[8,2,16,128,128]{3,4,2,1,0:T(8,128)(2,1)} %bitcast.46), channel_id=1, replica_groups=mesh['rad'=8,'mode'=16] {'rad'}, dimensions={0} | all-to-all | bytes 16777216 | tf_op jit(solution)/shard_map/all_to_all | solution.py:79
  329.5 10.3 %copy.31 = bf16[8,2,16,128,128]{3,4,0,2,1:T(8,128)(2,1)} copy(bf16[8,2,16,128,128]{3,4,2,1,0:T(8,128)(2,1)} %all_to_all.10) | data formatting | bytes 16777216 | tf_op jit(solution)/shard_map/all_to_all | solution.py:79
  339.8 0.0 copy-start.1
  339.8 11.8 %copy.32 = bf16[2,16,128,1024]{3,2,1,0:T(8,128)(2,1)} copy(bf16[2,16,128,1024]{2,3,1,0:T(8,128)(2,1)} %bitcast.47) | data formatting | bytes 16777216 | tf_op jit(solution)/shard_map/reshape | solution.py:80
  351.7 0.0 copy-done.1
  (12 shorter events, 0.1 us)
Async XLA Ops:
  0.0 53.5 %copy-start = (s32[256]{0:T(256)S(1)}, s32[256]{0:T(256)}, u32[]{:S(2)}) copy-start(s32[256]{0:T(256)} %param.14) | copy-start | bytes 3076
  40.8 12.0 %copy-start.2 = (s32[256]{0:T(256)S(1)}, s32[256]{0:T(256)}, u32[]{:S(2)}) copy-start(s32[256]{0:T(256)} %param.15) | copy-start | bytes 3076
  40.8 13.5 %copy-start.4 = (f32[1024]{0:T(1024)S(1)}, f32[1024]{0:T(1024)}, u32[]{:S(2)}) copy-start(f32[1024]{0:T(1024)} %param.10) | copy-start | bytes 12292
  40.8 13.6 %copy-start.3 = (f32[1024]{0:T(1024)S(1)}, f32[1024]{0:T(1024)}, u32[]{:S(2)}) copy-start(f32[1024]{0:T(1024)} %param.11) | copy-start | bytes 12292
  40.8 109.9 %all-to-all-start = ((bf16[128,2,1,128,128]{4,3,1,2,0:T(8,128)(2,1)}), bf16[128,2,1,128,128]{4,3,1,2,0:T(8,128)(2,1)}, u32[]{:S(2)}, u32[]{:S(2)}) async-start(bf16[128,2,1,128,128]{4,3,1,2,0:T(8,128)(2,1)} %copy.27), calls=%async_computation | async-start | bytes 16777216 | tf_op jit(solution)/shard_map/all_to_all | solution.py:53
  62.6 99.4 %copy-start.5 = (bf16[1024,1024]{1,0:T(8,128)(2,1)S(1)}, bf16[1024,1024]{1,0:T(8,128)(2,1)}, u32[]{:S(2)}) copy-start(bf16[1024,1024]{1,0:T(8,128)(2,1)} %param.13) | copy-start | bytes 6291460
  339.8 11.8 %copy-start.1 = (s32[256]{0:T(256)S(1)}, s32[256]{0:T(256)}, u32[]{:S(2)}) copy-start(s32[256]{0:T(256)} %param.14) | copy-start | bytes 3076

commit v2 on v1

v2 whole, which is shorter than its diff:
```python
import functools

import jax
import jax.numpy as jnp
from jax import lax
from jax.experimental import pallas as pl
from jax.experimental.pallas import tpu as pltpu
from jax.sharding import PartitionSpec as P

PAD = 8


def pack_kernel(picks_ref, x_ref, o_ref):
    nrad, window = o_ref.shape[0], o_ref.shape[-1]
    for w in range(nrad):
        o_ref[w, 0, 0] = x_ref[0, 0, :, w * window:(w + 1) * window]


def pack(spectra, picks, groups, nrad, per_group):
    comps, rows_here, shells_here, slots_total = spectra.shape
    window = slots_total // nrad
    return pl.pallas_call(
        pack_kernel,
        out_shape=jax.ShapeDtypeStruct(
            (groups * nrad, comps, per_group, shells_here, window), spectra.dtype
        ),
        grid_spec=pltpu.PrefetchScalarGridSpec(
            num_scalar_prefetch=1,
            grid=(groups * per_group, comps),
            in_specs=[
                pl.BlockSpec(
                    (1, 1, shells_here, slots_total), lambda q, c, p: (c, p[q], 0, 0)
                )
            ],
            out_specs=pl.BlockSpec(
                (nrad, 1, 1, shells_here, window),
                lambda q, c, p: (q // per_group, c, q % per_group, 0, 0),
            ),
        ),
    )(picks, spectra)


def solve_kernel(x_ref, info_ref, kappa_ref, invden_ref, eig_ref, d_ref, b_ref, o_ref, pad_ref):
    nrad, comps = x_ref.shape[1], x_ref.shape[2]
    sh, window = x_ref.shape[4], x_ref.shape[5]
    nr = nrad * sh
    cols = [x_ref[0, :, c, 0].reshape(nr, window) for c in range(comps)]
    f = jnp.concatenate(cols, axis=1).astype(jnp.float32)
    width = f.shape[1]
    pad_ref[0:PAD, :] = jnp.zeros((PAD, width), jnp.float32)
    pad_ref[PAD + nr:PAD + nr + PAD, :] = jnp.zeros((PAD, width), jnp.float32)
    pad_ref[PAD:PAD + nr, :] = f
    m2 = pad_ref[PAD - 2:PAD - 2 + nr, :]
    m1 = pad_ref[PAD - 1:PAD - 1 + nr, :]
    p1 = pad_ref[PAD + 1:PAD + 1 + nr, :]
    p2 = pad_ref[PAD + 2:PAD + 2 + nr, :]
    second = (-m2 + 16.0 * m1 - 30.0 * f + 16.0 * p1 - p2) / 12.0
    deg = info_ref[0, 0:1, :]
    live = info_ref[0, 1:2, :] > 0.5
    lterm = deg * (deg + 1.0)
    damping = lterm * invden_ref[...]
    updated = f + 0.5 * kappa_ref[...] * (second - damping * f)
    updated = jnp.where(live, updated, 0.0).astype(jnp.bfloat16)
    projected = jnp.dot(d_ref[...], updated, preferred_element_type=jnp.float32)
    divisor = eig_ref[...] + 0.5 * lterm / float(nr * nr)
    scaled = (projected / divisor).astype(jnp.bfloat16)
    restored = jnp.dot(b_ref[...], scaled, preferred_element_type=jnp.float32)
    solved = jnp.where(live, restored, 0.0).astype(jnp.bfloat16)
    for c in range(comps):
        o_ref[:, c, 0] = solved[:, c * window:(c + 1) * window].reshape(nrad, sh, window)


def solve(recv, info, kappa, invden, eig, dual_full, basis_full, groups, nrad, per_group):
    _, comps, _, sh, window = recv.shape
    nr = nrad * sh
    rows_here = groups * per_group
    x = recv.reshape(groups, nrad, comps, per_group, sh, window)
    width = comps * window
    flops = 2 * 2 * nr * nr * width * rows_here
    return pl.pallas_call(
        solve_kernel,
        out_shape=jax.ShapeDtypeStruct((nrad, comps, rows_here, sh, window), jnp.bfloat16),
        grid=(rows_here,),
        in_specs=[
            pl.BlockSpec(
                (1, nrad, comps, 1, sh, window),
                lambda q: (q // per_group, 0, 0, q % per_group, 0, 0),
            ),
            pl.BlockSpec((1, 8, width), lambda q: (q, 0, 0)),
            pl.BlockSpec((nr, 1), lambda q: (0, 0)),
            pl.BlockSpec((nr, 1), lambda q: (0, 0)),
            pl.BlockSpec((nr, 1), lambda q: (0, 0)),
            pl.BlockSpec((nr, nr), lambda q: (0, 0)),
            pl.BlockSpec((nr, nr), lambda q: (0, 0)),
        ],
        out_specs=pl.BlockSpec((nrad, comps, 1, sh, window), lambda q: (0, 0, q, 0, 0)),
        scratch_shapes=[pltpu.VMEM((nr + 2 * PAD, width), jnp.float32)],
        compiler_params=pltpu.CompilerParams(vmem_limit_bytes=48 * 1024 * 1024),
        cost_estimate=pl.CostEstimate(
            flops=flops, transcendentals=0, bytes_accessed=4 * recv.size + 4 * nr * nr
        ),
    )(x, info, kappa, invden, eig, dual_full, basis_full)


def unpack_kernel(x_ref, o_ref):
    nrad, window = x_ref.shape[0], x_ref.shape[-1]
    for w in range(nrad):
        o_ref[0, 0, :, w * window:(w + 1) * window] = x_ref[w, 0, 0]


def unpack(got):
    nrad, comps, rows_here, sh, window = got.shape
    return pl.pallas_call(
        unpack_kernel,
        out_shape=jax.ShapeDtypeStruct((comps, rows_here, sh, nrad * window), got.dtype),
        grid=(comps, rows_here),
        in_specs=[pl.BlockSpec((nrad, 1, 1, sh, window), lambda c, r: (0, c, r, 0, 0))],
        out_specs=pl.BlockSpec((1, 1, sh, nrad * window), lambda c, r: (c, r, 0, 0)),
    )(got)


def on_device(
    spectra, diffusivity, eigenvalues, radial_basis, dual_basis, degree_count, order_slot
):
    comps, rows_here, shells_here, slots_total = spectra.shape
    shells_total = diffusivity.shape[0]
    orders_total = degree_count.shape[0]
    groups = lax.axis_size("mode")
    nrad = lax.axis_size("rad")
    per_group = rows_here // groups
    window = slots_total // nrad
    me_mode = lax.axis_index("mode")
    me_rad = lax.axis_index("rad")

    picks = (
        lax.dynamic_slice_in_dim(
            order_slot.reshape(groups, groups, per_group), me_mode, 1, 1
        ).reshape(groups * per_group)
        - me_mode * rows_here
    )
    send = pack(spectra, picks, groups, nrad, per_group)
    recv = lax.all_to_all(send, ("mode", "rad"), 0, 0, tiled=True)

    out_rows = me_mode * rows_here + jnp.arange(rows_here, dtype=jnp.int32)
    in_rows = jnp.take(order_slot, out_rows)
    orders = in_rows * slots_total // (2 * orders_total)
    slot_ids = me_rad * window + jnp.arange(window, dtype=jnp.int32)
    degree = (orders[:, None] + slot_ids[None, :]).astype(jnp.float32)
    live = (slot_ids[None, :] < jnp.take(degree_count, in_rows)[:, None]).astype(jnp.float32)
    info = jnp.zeros((rows_here, 8, comps * window), jnp.float32)
    info = info.at[:, 0, :].set(jnp.tile(degree, (1, comps)))
    info = info.at[:, 1, :].set(jnp.tile(live, (1, comps)))

    radius = 1.2 + jnp.arange(shells_total, dtype=jnp.int32).astype(jnp.float32) / shells_total
    invden = (1.0 / ((shells_total * radius) ** 2)).reshape(shells_total, 1)
    kappa = diffusivity.reshape(shells_total, 1)
    eig = eigenvalues.reshape(shells_total, 1)

    identity = jnp.eye(shells_total, dtype=jnp.float32)
    basis_full = (identity + radial_basis.astype(jnp.float32)).astype(jnp.bfloat16)
    dual_full = (identity + dual_basis.astype(jnp.float32)).astype(jnp.bfloat16)
    back = solve(recv, info, kappa, invden, eig, dual_full, basis_full, groups, nrad, per_group)
    got = lax.all_to_all(back, "rad", 0, 0, tiled=True)
    return unpack(got)


def solution(mesh):
    placed = (P(None, "mode", "rad", None), P(), P(), P(), P(), P(), P())
    return jax.shard_map(
        on_device,
        mesh=mesh,
        in_specs=placed,
        out_specs=P(None, "mode", "rad", None),
        check_vma=False,
    )
```

time: 353 us -> 304 us (0.86)
  Pallas kernels: 0 us -> 87.6 us
  local copies, waits for them, and re-layouts: 76.7 us -> 5.3 us
  matrix products: 57.6 us -> 0 us
  other arithmetic: 16.2 us -> 6.22 us
    pallas_call x0 -> x3, Pallas kernels: none -> 87.6 us  [the longest x1 47.7 us: solve(): pl.pallas_call(solve_kernel, out_shape=jax.ShapeDtypeStruct((nrad, comps,...]
    dot_general x2 -> x0, matrix products: 57.6 us -> none  [the longest x1 40.9 us: on_device(): jnp.einsum('kr,cirj->cikj', dual_full, updated, preferred_element_type=jn...]
    reshape x3 -> x2, local copies, waits for them, and re-layouts: 32.8 us -> 0.44 us  [the longest x1 0.22 us: on_device(): kappa = diffusivity.reshape(shells_total, 1)]
    gather x3 -> x1, local copies, waits for them, and re-layouts: 20.9 us -> 0.66 us  [on_device(): jnp.take(degree_count, in_rows)[:, None]]
    convert_element_type x1 -> x0, local copies, waits for them, and re-layouts: 11.2 us -> none  [on_device(): local.astype(jnp.float32)]
    all_to_all x1 -> x0, local copies, waits for them, and re-layouts: 10.3 us -> none  [on_device(): got = lax.all_to_all(back, 'rad', 0, 0, tiled=True)]
    select_n x5 -> x2, other arithmetic: 7.68 us -> 0.02 us  [on_device(): jnp.take(degree_count, in_rows)[:, None]]
    convert_element_type x0 -> x3, other arithmetic: none -> 4.46 us  [the longest x1 4.31 us: on_device(): dual_full = (identity + dual_basis.astype(jnp.float32)).astype(jnp.bfloat16)]
  transfers between devices with their start and end apart: 1 -> 1, of which waited for: 1 -> 1; matrix products, arithmetic and copies ran while one was open for 3% -> 2% of each run, Pallas kernels for 0% -> 0%
where the time goes in v2:
time: 304 us; the launch traced here: 302 us
  blocking collectives  101 us (33%)
  waiting for transfers between devices  90.5 us (30%)
  Pallas kernels  87.6 us (29%)
  starting transfers between devices  11.9 us (4%)
  other arithmetic  6.22 us (2%)
  local copies, waits for them, and re-layouts  5.3 us (2%)
    all_to_all x1, blocking collectives, on_device(): got = lax.all_to_all(back, 'rad', 0, 0, tiled=True)  101 us
    all_to_all x1, waiting for transfers between devices, on_device(): recv = lax.all_to_all(send, ('mode', 'rad'), 0, 0, tiled=True)  90.5 us
    pallas_call x1, Pallas kernels, solve(): pl.pallas_call(solve_kernel, out_shape=jax.ShapeDtypeStruct((nrad, comps,...  47.7 us
    pallas_call x1, Pallas kernels, pack(): pl.pallas_call(pack_kernel, out_shape=jax.ShapeDtypeStruct((groups * nrad...  20.2 us
    pallas_call x1, Pallas kernels, unpack(): pl.pallas_call(unpack_kernel, out_shape=jax.ShapeDtypeStruct((comps, rows...  19.7 us
    all_to_all x1, starting transfers between devices, on_device(): recv = lax.all_to_all(send, ('mode', 'rad'), 0, 0, tiled=True)  11.9 us
  transfers between devices with their start and end apart: 1, of which 1 were waited for; matrix products, arithmetic and copies ran while one was open for 2% of the time, Pallas kernels for 0%

profile of v2, /device:TPU:1, one launch (start us, length us, event | category | flops | bytes accessed | tf_op | source)
XLA Modules:
  0.0 302.5 jit_solution(3458928428705617557)
XLA Ops:
  0.0 0.0 copy-start
  0.0 0.8 reshape.172
  0.8 0.8 subtract_reduce_fusion.picks_ref
  1.5 20.2 %shard_map.73 = bf16[128,2,1,128,128]{4,3,2,1,0:T(8,128)(2,1)} custom-call(s32[16]{0:T(128)} %subtract_reduce_fusion.picks_ref, bf16[2,16,128,1024]{3,2,1,0:T(8,128)(2,1)} %x_ref.1), custom_call_target="tpu_custom_call" | custom-call | tf_op jit(solution)/shard_map/pallas_call | solution.py:22
  21.7 0.0 copy-start.3
  21.7 0.0 copy-start.4
  21.7 0.0 copy-start.5
  21.7 11.9 %all-to-all-start = ((bf16[128,2,1,128,128]{4,3,2,1,0:T(8,128)(2,1)}), bf16[128,2,1,128,128]{4,3,2,1,0:T(8,128)(2,1)}, u32[]{:S(2)}, u32[]{:S(2)}) async-start(bf16[128,2,1,128,128]{4,3,2,1,0:T(8,128)(2,1)} %shard_map.73), calls=%async_computation | async-start | bytes 16777216 | tf_op jit(solution)/shard_map/all_to_all | solution.py:142
  33.7 0.0 copy-done.3
  33.7 0.7 gather_fusion
  34.4 0.0 copy-done.4
  34.4 0.2 copy.13.kappa_ref
  34.6 0.0 copy-done.5
  34.6 0.2 copy.14.eig_ref
  34.9 0.0 copy-done
  34.9 0.7 gather_fusion.1
  35.6 0.1 add_convert_fusion
  35.7 0.1 compare_convert_fusion
  35.8 0.1 scatter.9.info_ref
  35.9 0.9 multiply_divide_fusion.invden_ref
  36.8 4.3 %fusion = (bf16[1024,1024]{1,0:T(8,128)(2,1)S(1)}, bf16[1024,1024]{1,0:T(8,128)(2,1)}) fusion(bf16[1024,1024]{1,0:T(8,128)(2,1)} %param.17, bf16[1024,1024]{1,0:T(8,128)(2,1)} %param.16), kind=kLoop, calls=%fused_computation.4 | loop fusion | flops 8388608 | bytes 8388608 | tf_op jit(solution)/shard_map/convert_element_type | solution.py:161
  41.1 90.5 %all-to-all-done = bf16[128,2,1,128,128]{4,3,2,1,0:T(8,128)(2,1)} async-done(((bf16[128,2,1,128,128]{4,3,2,1,0:T(8,128)(2,1)}), bf16[128,2,1,128,128]{4,3,2,1,0:T(8,128)(2,1)}, u32[]{:S(2)}, u32[]{:S(2)}) %all-to-all-start) | async-done | bytes 8388640 | tf_op jit(solution)/shard_map/all_to_all | solution.py:142
  131.6 0.0 copy-start.1
  131.6 1.6 copy-done.1
  133.2 0.0 copy-start.2
  133.2 1.0 copy-done.2
  134.3 47.7 %shard_map.74 = bf16[8,2,16,128,128]{4,3,2,1,0:T(8,128)(2,1)} custom-call(bf16[16,8,2,1,128,128]{5,4,3,2,1,0:T(8,128)(2,1)} %bitcast.x_ref, f32[16,8,256]{2,1,0:T(8,128)S(1)} %scatter.9.info_ref, f32[1024,1]{1,0:T(8,128)S(1)} %copy.13.kappa_ref, f32[1024,1]{1,0:T(8,128)S(1)} %copy-done.2, f32[1024,1]{1,0:T(8,128)S(1)} %copy.14.eig_ref, ...), custom_call_target="tpu_custom_call" | custom-call | flops 17179869184 | bytes 20971520 | tf_op jit(solution)/shard_map/pallas_call | solution.py:80
  181.9 100.8 %all_to_all.10.x_ref = bf16[8,2,16,128,128]{4,3,2,1,0:T(8,128)(2,1)} all-to-all(bf16[8,2,16,128,128]{4,3,2,1,0:T(8,128)(2,1)} %shard_map.74), channel_id=1, replica_groups=mesh['rad'=8,'mode'=16] {'rad'}, dimensions={0} | all-to-all | bytes 16777216 | tf_op jit(solution)/shard_map/all_to_all | solution.py:163
  282.8 19.7 %shard_map.75 = bf16[2,16,128,1024]{3,2,1,0:T(8,128)(2,1)} custom-call(bf16[8,2,16,128,128]{4,3,2,1,0:T(8,128)(2,1)} %all_to_all.10.x_ref), custom_call_target="tpu_custom_call" | custom-call | tf_op jit(solution)/shard_map/pallas_call | solution.py:113
  (9 shorter events, 0.1 us)
Async XLA Ops:
  0.0 34.9 %copy-start = (s32[256]{0:T(256)S(1)}, s32[256]{0:T(256)}, u32[]{:S(2)}) copy-start(s32[256]{0:T(256)} %param.18) | copy-start | bytes 3076
  21.7 12.0 %copy-start.3 = (s32[256]{0:T(256)S(1)}, s32[256]{0:T(256)}, u32[]{:S(2)}) copy-start(s32[256]{0:T(256)} %param.19) | copy-start | bytes 3076
  21.7 12.7 %copy-start.4 = (f32[1024]{0:T(1024)S(1)}, f32[1024]{0:T(1024)}, u32[]{:S(2)}) copy-start(f32[1024]{0:T(1024)} %param.14) | copy-start | bytes 12292
  21.7 12.9 %copy-start.5 = (f32[1024]{0:T(1024)S(1)}, f32[1024]{0:T(1024)}, u32[]{:S(2)}) copy-start(f32[1024]{0:T(1024)} %param.15) | copy-start | bytes 12292
  21.7 109.9 %all-to-all-start = ((bf16[128,2,1,128,128]{4,3,2,1,0:T(8,128)(2,1)}), bf16[128,2,1,128,128]{4,3,2,1,0:T(8,128)(2,1)}, u32[]{:S(2)}, u32[]{:S(2)}) async-start(bf16[128,2,1,128,128]{4,3,2,1,0:T(8,128)(2,1)} %shard_map.73), calls=%async_computation | async-start | bytes 16777216 | tf_op jit(solution)/shard_map/all_to_all | solution.py:142
  131.6 1.6 copy-start.1
  133.2 1.0 copy-start.2

commit v3 on v2

--- a/solution.py
+++ b/solution.py
@@ -10,15 +10,26 @@
 PAD = 8
 
 
-def pack_kernel(picks_ref, x_ref, o_ref):
-    nrad, window = o_ref.shape[0], o_ref.shape[-1]
-    for w in range(nrad):
-        o_ref[w, 0, 0] = x_ref[0, 0, :, w * window:(w + 1) * window]
+def pack_kernel(picks_ref, *refs):
+    x_refs, o_ref = refs[:-1], refs[-1]
+    nrad, window = o_ref.shape[0] // len(x_refs), o_ref.shape[-1]
+    for i, x_ref in enumerate(x_refs):
+        for w in range(nrad):
+            o_ref[i * nrad + w] = x_ref[:, 0:1, :, w * window:(w + 1) * window]
 
 
-def pack(spectra, picks, groups, nrad, per_group):
+def pack(spectra, picks, groups, nrad, per_group, step=4):
     comps, rows_here, shells_here, slots_total = spectra.shape
     window = slots_total // nrad
+    picks_total = groups * per_group
+
+    def in_map(i):
+        return lambda q, p: (0, p[q * step + i], 0, 0)
+
+    def out_map(q, p):
+        return (q, 0, 0, 0, 0)
+
+    assert per_group == 1 and picks_total % step == 0
     return pl.pallas_call(
         pack_kernel,
         out_shape=jax.ShapeDtypeStruct(
@@ -26,18 +37,16 @@
         ),
         grid_spec=pltpu.PrefetchScalarGridSpec(
             num_scalar_prefetch=1,
-            grid=(groups * per_group, comps),
+            grid=(picks_total // step,),
             in_specs=[
-                pl.BlockSpec(
-                    (1, 1, shells_here, slots_total), lambda q, c, p: (c, p[q], 0, 0)
-                )
+                pl.BlockSpec((comps, 1, shells_here, slots_total), in_map(i))
+                for i in range(step)
             ],
             out_specs=pl.BlockSpec(
-                (nrad, 1, 1, shells_here, window),
-                lambda q, c, p: (q // per_group, c, q % per_group, 0, 0),
+                (step * nrad, comps, per_group, shells_here, window), out_map
             ),
         ),
-    )(picks, spectra)
+    )(picks, *([spectra] * step))
 
 
 def solve_kernel(x_ref, info_ref, kappa_ref, invden_ref, eig_ref, d_ref, b_ref, o_ref, pad_ref):
@@ -105,17 +114,17 @@
 def unpack_kernel(x_ref, o_ref):
     nrad, window = x_ref.shape[0], x_ref.shape[-1]
     for w in range(nrad):
-        o_ref[0, 0, :, w * window:(w + 1) * window] = x_ref[w, 0, 0]
+        o_ref[:, :, :, w * window:(w + 1) * window] = x_ref[w]
 
 
-def unpack(got):
+def unpack(got, step=4):
     nrad, comps, rows_here, sh, window = got.shape
     return pl.pallas_call(
         unpack_kernel,
         out_shape=jax.ShapeDtypeStruct((comps, rows_here, sh, nrad * window), got.dtype),
-        grid=(comps, rows_here),
-        in_specs=[pl.BlockSpec((nrad, 1, 1, sh, window), lambda c, r: (0, c, r, 0, 0))],
-        out_specs=pl.BlockSpec((1, 1, sh, nrad * window), lambda c, r: (c, r, 0, 0)),
+        grid=(rows_here // step,),
+        in_specs=[pl.BlockSpec((nrad, comps, step, sh, window), lambda r: (0, 0, r, 0, 0))],
+        out_specs=pl.BlockSpec((comps, step, sh, nrad * window), lambda r: (0, r, 0, 0)),
     )(got)
 
 

time: 304 us -> 279 us (0.918)
  Pallas kernels: 87.6 us -> 63.7 us
    pallas_call x1, Pallas kernels: 20.2 us -> 8.06 us  [pack(): pl.pallas_call(pack_kernel, out_shape=jax.ShapeDtypeStruct((groups * nrad...]
    pallas_call x1, Pallas kernels: 19.7 us -> 7.93 us  [unpack(): pl.pallas_call(unpack_kernel, out_shape=jax.ShapeDtypeStruct((comps, rows...]
  transfers between devices with their start and end apart: 1 -> 1, of which waited for: 1 -> 1; matrix products, arithmetic and copies ran while one was open for 2% -> 3% of each run, Pallas kernels for 0% -> 0%
where the time goes in v3:
time: 279 us
  blocking collectives  101 us (36%)
  waiting for transfers between devices  90.5 us (32%)
  Pallas kernels  63.7 us (23%)
  starting transfers between devices  12 us (4%)
  other arithmetic  6.22 us (2%)
  local copies, waits for them, and re-layouts  5.3 us (2%)
    all_to_all x1, blocking collectives, on_device(): got = lax.all_to_all(back, 'rad', 0, 0, tiled=True)  101 us
    all_to_all x1, waiting for transfers between devices, on_device(): recv = lax.all_to_all(send, ('mode', 'rad'), 0, 0, tiled=True)  90.5 us
    pallas_call x1, Pallas kernels, solve(): pl.pallas_call(solve_kernel, out_shape=jax.ShapeDtypeStruct((nrad, comps,...  47.7 us
    all_to_all x1, starting transfers between devices, on_device(): recv = lax.all_to_all(send, ('mode', 'rad'), 0, 0, tiled=True)  12 us
    pallas_call x1, Pallas kernels, pack(): pl.pallas_call(pack_kernel, out_shape=jax.ShapeDtypeStruct((groups * nrad...  8.06 us
    pallas_call x1, Pallas kernels, unpack(): pl.pallas_call(unpack_kernel, out_shape=jax.ShapeDtypeStruct((comps, rows...  7.93 us
  transfers between devices with their start and end apart: 1, of which 1 were waited for; matrix products, arithmetic and copies ran while one was open for 3% of the time, Pallas kernels for 0%

profile of v3, /device:TPU:1, one launch (start us, length us, event | category | flops | bytes accessed | tf_op | source)
XLA Modules:
  0.0 278.6 jit_solution(12274578891005920946)
XLA Ops:
  0.0 0.0 copy-start
  0.0 0.8 reshape.172
  0.8 0.8 subtract_reduce_fusion.picks_ref
  1.5 8.1 %shard_map.73 = bf16[128,2,1,128,128]{4,3,2,1,0:T(8,128)(2,1)} custom-call(s32[16]{0:T(128)} %subtract_reduce_fusion.picks_ref, bf16[2,16,128,1024]{3,2,1,0:T(8,128)(2,1)} %refs_3_.1, bf16[2,16,128,1024]{3,2,1,0:T(8,128)(2,1)} %refs_3_.1, bf16[2,16,128,1024]{3,2,1,0:T(8,128)(2,1)} %refs_3_.1, bf16[2,16,128,1024]{3,2,1,0:T(8,128)(2,1)} %refs_3_.1), custom_call_target="tpu_custom_call" | custom-call | tf_op jit(solution)/shard_map/pallas_call | solution.py:33
  9.6 0.0 copy-start.3
  9.6 0.0 copy-start.4
  9.6 0.0 copy-start.5
  9.6 12.0 %all-to-all-start = ((bf16[128,2,1,128,128]{4,3,2,1,0:T(8,128)(2,1)}), bf16[128,2,1,128,128]{4,3,2,1,0:T(8,128)(2,1)}, u32[]{:S(2)}, u32[]{:S(2)}) async-start(bf16[128,2,1,128,128]{4,3,2,1,0:T(8,128)(2,1)} %shard_map.73), calls=%async_computation | async-start | bytes 16777216 | tf_op jit(solution)/shard_map/all_to_all | solution.py:151
  21.6 0.0 copy-done.3
  21.6 0.7 gather_fusion
  22.3 0.0 copy-done.4
  22.3 0.2 copy.13.kappa_ref
  22.5 0.0 copy-done.5
  22.5 0.2 copy.14.eig_ref
  22.8 0.0 copy-done
  22.8 0.7 gather_fusion.1
  23.5 0.1 add_convert_fusion
  23.6 0.1 compare_convert_fusion
  23.7 0.1 scatter.9.info_ref
  23.8 0.9 multiply_divide_fusion.invden_ref
  24.7 4.3 %fusion = (bf16[1024,1024]{1,0:T(8,128)(2,1)S(1)}, bf16[1024,1024]{1,0:T(8,128)(2,1)}) fusion(bf16[1024,1024]{1,0:T(8,128)(2,1)} %param.17, bf16[1024,1024]{1,0:T(8,128)(2,1)} %param.16), kind=kLoop, calls=%fused_computation.4 | loop fusion | flops 8388608 | bytes 8388608 | tf_op jit(solution)/shard_map/convert_element_type | solution.py:170
  29.0 90.5 %all-to-all-done = bf16[128,2,1,128,128]{4,3,2,1,0:T(8,128)(2,1)} async-done(((bf16[128,2,1,128,128]{4,3,2,1,0:T(8,128)(2,1)}), bf16[128,2,1,128,128]{4,3,2,1,0:T(8,128)(2,1)}, u32[]{:S(2)}, u32[]{:S(2)}) %all-to-all-start) | async-done | bytes 8388640 | tf_op jit(solution)/shard_map/all_to_all | solution.py:151
  119.5 0.0 copy-start.1
  119.5 1.6 copy-done.1
  121.1 0.0 copy-start.2
  121.1 1.0 copy-done.2
  122.2 47.7 %shard_map.74 = bf16[8,2,16,128,128]{4,3,2,1,0:T(8,128)(2,1)} custom-call(bf16[16,8,2,1,128,128]{5,4,3,2,1,0:T(8,128)(2,1)} %bitcast.x_ref, f32[16,8,256]{2,1,0:T(8,128)S(1)} %scatter.9.info_ref, f32[1024,1]{1,0:T(8,128)S(1)} %copy.13.kappa_ref, f32[1024,1]{1,0:T(8,128)S(1)} %copy-done.2, f32[1024,1]{1,0:T(8,128)S(1)} %copy.14.eig_ref, ...), custom_call_target="tpu_custom_call" | custom-call | flops 17179869184 | bytes 20971520 | tf_op jit(solution)/shard_map/pallas_call | solution.py:89
  169.8 100.8 %all_to_all.10.x_ref = bf16[8,2,16,128,128]{4,3,2,1,0:T(8,128)(2,1)} all-to-all(bf16[8,2,16,128,128]{4,3,2,1,0:T(8,128)(2,1)} %shard_map.74), channel_id=1, replica_groups=mesh['rad'=8,'mode'=16] {'rad'}, dimensions={0} | all-to-all | bytes 16777216 | tf_op jit(solution)/shard_map/all_to_all | solution.py:172
  270.7 7.9 %shard_map.75 = bf16[2,16,128,1024]{3,2,1,0:T(8,128)(2,1)} custom-call(bf16[8,2,16,128,128]{4,3,2,1,0:T(8,128)(2,1)} %all_to_all.10.x_ref), custom_call_target="tpu_custom_call" | custom-call | tf_op jit(solution)/shard_map/pallas_call | solution.py:122
  (9 shorter events, 0.1 us)
Async XLA Ops:
  0.0 22.8 %copy-start = (s32[256]{0:T(256)S(1)}, s32[256]{0:T(256)}, u32[]{:S(2)}) copy-start(s32[256]{0:T(256)} %param.18) | copy-start | bytes 3076
  9.6 12.0 %copy-start.3 = (s32[256]{0:T(256)S(1)}, s32[256]{0:T(256)}, u32[]{:S(2)}) copy-start(s32[256]{0:T(256)} %param.19) | copy-start | bytes 3076
  9.6 12.7 %copy-start.4 = (f32[1024]{0:T(1024)S(1)}, f32[1024]{0:T(1024)}, u32[]{:S(2)}) copy-start(f32[1024]{0:T(1024)} %param.14) | copy-start | bytes 12292
  9.6 12.9 %copy-start.5 = (f32[1024]{0:T(1024)S(1)}, f32[1024]{0:T(1024)}, u32[]{:S(2)}) copy-start(f32[1024]{0:T(1024)} %param.15) | copy-start | bytes 12292
  9.6 109.9 %all-to-all-start = ((bf16[128,2,1,128,128]{4,3,2,1,0:T(8,128)(2,1)}), bf16[128,2,1,128,128]{4,3,2,1,0:T(8,128)(2,1)}, u32[]{:S(2)}, u32[]{:S(2)}) async-start(bf16[128,2,1,128,128]{4,3,2,1,0:T(8,128)(2,1)} %shard_map.73), calls=%async_computation | async-start | bytes 16777216 | tf_op jit(solution)/shard_map/all_to_all | solution.py:151
  119.5 1.6 copy-start.1
  121.1 1.0 copy-start.2

commit v4 on v3

v4 whole, which is shorter than its diff:
```python
import functools

import jax
import jax.numpy as jnp
from jax import lax
from jax.experimental import pallas as pl
from jax.experimental.pallas import tpu as pltpu
from jax.sharding import PartitionSpec as P

PAD = 8


def pack_kernel(picks_ref, *refs):
    x_refs, o_ref = refs[:-1], refs[-1]
    nrad, window = o_ref.shape[0] // len(x_refs), o_ref.shape[-1]
    for i, x_ref in enumerate(x_refs):
        for w in range(nrad):
            o_ref[i * nrad + w] = x_ref[:, 0:1, :, w * window:(w + 1) * window]


def pack(spectra, picks, comp, groups, nrad, per_group, step=4):
    comps, rows_here, shells_here, slots_total = spectra.shape
    window = slots_total // nrad
    picks_total = groups * per_group

    def in_map(i):
        return lambda q, p: (comp, p[q * step + i], 0, 0)

    def out_map(q, p):
        return (q, 0, 0, 0, 0)

    assert per_group == 1 and picks_total % step == 0
    return pl.pallas_call(
        pack_kernel,
        out_shape=jax.ShapeDtypeStruct(
            (groups * nrad, 1, per_group, shells_here, window), spectra.dtype
        ),
        grid_spec=pltpu.PrefetchScalarGridSpec(
            num_scalar_prefetch=1,
            grid=(picks_total // step,),
            in_specs=[
                pl.BlockSpec((1, 1, shells_here, slots_total), in_map(i))
                for i in range(step)
            ],
            out_specs=pl.BlockSpec((step * nrad, 1, per_group, shells_here, window), out_map),
        ),
    )(picks, *([spectra] * step))


def solve_kernel(x_ref, info_ref, kappa_ref, invden_ref, eig_ref, d_ref, b_ref, o_ref, pad_ref):
    npos, nrad = x_ref.shape[0], x_ref.shape[1]
    sh, window = x_ref.shape[4], x_ref.shape[5]
    nr = nrad * sh
    cols = [x_ref[j, :, 0, 0].reshape(nr, window) for j in range(npos)]
    f = jnp.concatenate(cols, axis=1).astype(jnp.float32)
    width = f.shape[1]
    pad_ref[0:PAD, :] = jnp.zeros((PAD, width), jnp.float32)
    pad_ref[PAD + nr:PAD + nr + PAD, :] = jnp.zeros((PAD, width), jnp.float32)
    pad_ref[PAD:PAD + nr, :] = f
    m2 = pad_ref[PAD - 2:PAD - 2 + nr, :]
    m1 = pad_ref[PAD - 1:PAD - 1 + nr, :]
    p1 = pad_ref[PAD + 1:PAD + 1 + nr, :]
    p2 = pad_ref[PAD + 2:PAD + 2 + nr, :]
    second = (-m2 + 16.0 * m1 - 30.0 * f + 16.0 * p1 - p2) / 12.0
    deg = jnp.concatenate([info_ref[j, 0:1, :] for j in range(npos)], axis=1)
    live = jnp.concatenate([info_ref[j, 1:2, :] for j in range(npos)], axis=1) > 0.5
    lterm = deg * (deg + 1.0)
    damping = lterm * invden_ref[...]
    updated = f + 0.5 * kappa_ref[...] * (second - damping * f)
    updated = jnp.where(live, updated, 0.0).astype(jnp.bfloat16)
    projected = jnp.dot(d_ref[...], updated, preferred_element_type=jnp.float32)
    divisor = eig_ref[...] + 0.5 * lterm / float(nr * nr)
    scaled = (projected / divisor).astype(jnp.bfloat16)
    restored = jnp.dot(b_ref[...], scaled, preferred_element_type=jnp.float32)
    solved = jnp.where(live, restored, 0.0).astype(jnp.bfloat16)
    for j in range(npos):
        o_ref[:, 0, j] = solved[:, j * window:(j + 1) * window].reshape(nrad, sh, window)


def solve(recv, info, kappa, invden, eig, dual_full, basis_full, groups, nrad, per_group, npos=2):
    _, _, _, sh, window = recv.shape
    nr = nrad * sh
    rows_here = groups * per_group
    assert per_group == 1 and rows_here % npos == 0
    x = recv.reshape(groups, nrad, 1, per_group, sh, window)
    width = npos * window
    flops = 2 * 2 * nr * nr * window * rows_here
    return pl.pallas_call(
        solve_kernel,
        out_shape=jax.ShapeDtypeStruct((nrad, 1, rows_here, sh, window), jnp.bfloat16),
        grid=(rows_here // npos,),
        in_specs=[
            pl.BlockSpec((npos, nrad, 1, 1, sh, window), lambda q: (q, 0, 0, 0, 0, 0)),
            pl.BlockSpec((npos, 8, window), lambda q: (q, 0, 0)),
            pl.BlockSpec((nr, 1), lambda q: (0, 0)),
            pl.BlockSpec((nr, 1), lambda q: (0, 0)),
            pl.BlockSpec((nr, 1), lambda q: (0, 0)),
            pl.BlockSpec((nr, nr), lambda q: (0, 0)),
            pl.BlockSpec((nr, nr), lambda q: (0, 0)),
        ],
        out_specs=pl.BlockSpec((nrad, 1, npos, sh, window), lambda q: (0, 0, q, 0, 0)),
        scratch_shapes=[pltpu.VMEM((nr + 2 * PAD, width), jnp.float32)],
        compiler_params=pltpu.CompilerParams(vmem_limit_bytes=48 * 1024 * 1024),
        cost_estimate=pl.CostEstimate(
            flops=flops, transcendentals=0, bytes_accessed=4 * recv.size + 4 * nr * nr
        ),
    )(x, info, kappa, invden, eig, dual_full, basis_full)


def unpack_kernel(*refs):
    x_refs, o_ref = refs[:-1], refs[-1]
    nrad, window = x_refs[0].shape[0], x_refs[0].shape[-1]
    for c, x_ref in enumerate(x_refs):
        for w in range(nrad):
            o_ref[c, :, :, w * window:(w + 1) * window] = x_ref[w, 0]


def unpack(gots, step=4):
    nrad, _, rows_here, sh, window = gots[0].shape
    comps = len(gots)
    return pl.pallas_call(
        unpack_kernel,
        out_shape=jax.ShapeDtypeStruct((comps, rows_here, sh, nrad * window), gots[0].dtype),
        grid=(rows_here // step,),
        in_specs=[
            pl.BlockSpec((nrad, 1, step, sh, window), lambda r: (0, 0, r, 0, 0))
            for _ in gots
        ],
        out_specs=pl.BlockSpec((comps, step, sh, nrad * window), lambda r: (0, r, 0, 0)),
    )(*gots)


def on_device(
    spectra, diffusivity, eigenvalues, radial_basis, dual_basis, degree_count, order_slot
):
    comps, rows_here, shells_here, slots_total = spectra.shape
    shells_total = diffusivity.shape[0]
    orders_total = degree_count.shape[0]
    groups = lax.axis_size("mode")
    nrad = lax.axis_size("rad")
    per_group = rows_here // groups
    window = slots_total // nrad
    me_mode = lax.axis_index("mode")
    me_rad = lax.axis_index("rad")

    picks = (
        lax.dynamic_slice_in_dim(
            order_slot.reshape(groups, groups, per_group), me_mode, 1, 1
        ).reshape(groups * per_group)
        - me_mode * rows_here
    )
    recvs = []
    for comp in range(comps):
        send = pack(spectra, picks, comp, groups, nrad, per_group)
        recvs.append(lax.all_to_all(send, ("mode", "rad"), 0, 0, tiled=True))

    out_rows = me_mode * rows_here + jnp.arange(rows_here, dtype=jnp.int32)
    in_rows = jnp.take(order_slot, out_rows)
    orders = in_rows * slots_total // (2 * orders_total)
    slot_ids = me_rad * window + jnp.arange(window, dtype=jnp.int32)
    degree = (orders[:, None] + slot_ids[None, :]).astype(jnp.float32)
    live = (slot_ids[None, :] < jnp.take(degree_count, in_rows)[:, None]).astype(jnp.float32)
    info = jnp.zeros((rows_here, 8, window), jnp.float32)
    info = info.at[:, 0, :].set(degree)
    info = info.at[:, 1, :].set(live)

    radius = 1.2 + jnp.arange(shells_total, dtype=jnp.int32).astype(jnp.float32) / shells_total
    invden = (1.0 / ((shells_total * radius) ** 2)).reshape(shells_total, 1)
    kappa = diffusivity.reshape(shells_total, 1)
    eig = eigenvalues.reshape(shells_total, 1)

    identity = jnp.eye(shells_total, dtype=jnp.float32)
    basis_full = (identity + radial_basis.astype(jnp.float32)).astype(jnp.bfloat16)
    dual_full = (identity + dual_basis.astype(jnp.float32)).astype(jnp.bfloat16)
    gots = []
    for recv in recvs:
        back = solve(recv, info, kappa, invden, eig, dual_full, basis_full, groups, nrad, per_group)
        gots.append(lax.all_to_all(back, "rad", 0, 0, tiled=True))
    return unpack(gots)


def solution(mesh):
    placed = (P(None, "mode", "rad", None), P(), P(), P(), P(), P(), P())
    return jax.shard_map(
        on_device,
        mesh=mesh,
        in_specs=placed,
        out_specs=P(None, "mode", "rad", None),
        check_vma=False,
    )
```

time: 279 us -> 247 us (0.89)
  blocking collectives: 101 us -> 54.1 us
  starting transfers between devices: 12 us -> 22.8 us
  Pallas kernels: 63.7 us -> 68.5 us
    all_to_all x1, blocking collectives: 101 us -> 54.1 us  [on_device(): gots.append(lax.all_to_all(back, 'rad', 0, 0, tiled=True))]
    all_to_all x1 -> x3, starting transfers between devices: 12 us -> 22.8 us  [the longest x2 17.4 us: on_device(): recvs.append(lax.all_to_all(send, ('mode', 'rad'), 0, 0, tiled=True))]
    pallas_call x1 -> x2, Pallas kernels: 8.06 us -> 11.2 us  [pack(): pl.pallas_call(pack_kernel, out_shape=jax.ShapeDtypeStruct((groups * nrad...]
    pallas_call x1 -> x2, Pallas kernels: 47.7 us -> 49.6 us  [solve(): pl.pallas_call(solve_kernel, out_shape=jax.ShapeDtypeStruct((nrad, 1, row...]
    all_to_all x1 -> x3, waiting for transfers between devices: 90.5 us -> 89.8 us  [the longest x2 68.4 us: on_device(): recvs.append(lax.all_to_all(send, ('mode', 'rad'), 0, 0, tiled=True))]
  transfers between devices with their start and end apart: 1 -> 3, of which waited for: 1 -> 3; matrix products, arithmetic and copies ran while one was open for 3% -> 2% of each run, Pallas kernels for 0% -> 22%
where the time goes in v4:
time: 247 us; the launch traced here: 246 us
  waiting for transfers between devices  89.8 us (36%)
  Pallas kernels  68.5 us (28%)
  blocking collectives  54.1 us (22%)
  starting transfers between devices  22.8 us (9%)
  local copies, waits for them, and re-layouts  6.77 us (3%)
  other arithmetic  4.06 us (2%)
    all_to_all x2, waiting for transfers between devices, on_device(): recvs.append(lax.all_to_all(send, ('mode', 'rad'), 0, 0, tiled=True))  68.4 us
    all_to_all x1, blocking collectives, on_device(): gots.append(lax.all_to_all(back, 'rad', 0, 0, tiled=True))  54.1 us
    pallas_call x2, Pallas kernels, solve(): pl.pallas_call(solve_kernel, out_shape=jax.ShapeDtypeStruct((nrad, 1, row...  49.6 us
    all_to_all x1, waiting for transfers between devices, on_device(): gots.append(lax.all_to_all(back, 'rad', 0, 0, tiled=True))  21.4 us
    all_to_all x2, starting transfers between devices, on_device(): recvs.append(lax.all_to_all(send, ('mode', 'rad'), 0, 0, tiled=True))  17.4 us
    pallas_call x2, Pallas kernels, pack(): pl.pallas_call(pack_kernel, out_shape=jax.ShapeDtypeStruct((groups * nrad...  11.2 us
    pallas_call x1, Pallas kernels, unpack(): pl.pallas_call(unpack_kernel, out_shape=jax.ShapeDtypeStruct((comps, rows...  7.83 us
    all_to_all x1, starting transfers between devices, on_device(): gots.append(lax.all_to_all(back, 'rad', 0, 0, tiled=True))  5.36 us
  transfers between devices with their start and end apart: 3, of which 3 were waited for; matrix products, arithmetic and copies ran while one was open for 2% of the time, Pallas kernels for 22%

profile of v4, /device:TPU:1, one launch (start us, length us, event | category | flops | bytes accessed | tf_op | source)
XLA Modules:
  0.0 246.1 jit_solution(11893728655658184497)
XLA Ops:
  0.0 0.0 copy-start
  0.0 0.8 reshape.167
  0.8 0.7 subtract_reduce_fusion.picks_ref
  1.5 5.5 %shard_map.73 = bf16[128,1,1,128,128]{4,3,2,1,0:T(8,128)(2,1)} custom-call(s32[16]{0:T(128)} %subtract_reduce_fusion.picks_ref, bf16[2,16,128,1024]{3,2,1,0:T(8,128)(2,1)} %refs_3_.3, bf16[2,16,128,1024]{3,2,1,0:T(8,128)(2,1)} %refs_3_.3, bf16[2,16,128,1024]{3,2,1,0:T(8,128)(2,1)} %refs_3_.3, bf16[2,16,128,1024]{3,2,1,0:T(8,128)(2,1)} %refs_3_.3), custom_call_target="tpu_custom_call" | custom-call | tf_op jit(solution)/shard_map/pallas_call | solution.py:33
  7.1 11.9 %all-to-all-start = ((bf16[128,1,1,128,128]{4,3,2,1,0:T(8,128)(2,1)}), bf16[128,1,1,128,128]{4,3,2,1,0:T(8,128)(2,1)}, u32[]{:S(2)}, u32[]{:S(2)}) async-start(bf16[128,1,1,128,128]{4,3,2,1,0:T(8,128)(2,1)} %shard_map.73), calls=%async_computation | async-start | bytes 8388608 | tf_op jit(solution)/shard_map/all_to_all | solution.py:155
  19.0 5.6 %shard_map.75 = bf16[128,1,1,128,128]{4,3,2,1,0:T(8,128)(2,1)} custom-call(s32[16]{0:T(128)} %subtract_reduce_fusion.picks_ref, bf16[2,16,128,1024]{3,2,1,0:T(8,128)(2,1)} %refs_3_.3, bf16[2,16,128,1024]{3,2,1,0:T(8,128)(2,1)} %refs_3_.3, bf16[2,16,128,1024]{3,2,1,0:T(8,128)(2,1)} %refs_3_.3, bf16[2,16,128,1024]{3,2,1,0:T(8,128)(2,1)} %refs_3_.3), custom_call_target="tpu_custom_call" | custom-call | tf_op jit(solution)/shard_map/pallas_call | solution.py:33
  24.6 0.0 copy-start.5
  24.6 0.0 copy-start.6
  24.6 0.0 copy-start.7
  24.6 47.1 %all-to-all-done = bf16[128,1,1,128,128]{4,3,2,1,0:T(8,128)(2,1)} async-done(((bf16[128,1,1,128,128]{4,3,2,1,0:T(8,128)(2,1)}), bf16[128,1,1,128,128]{4,3,2,1,0:T(8,128)(2,1)}, u32[]{:S(2)}, u32[]{:S(2)}) %all-to-all-start) | async-done | bytes 4194336 | tf_op jit(solution)/shard_map/all_to_all | solution.py:155
  71.7 5.5 %all-to-all-start.2 = ((bf16[128,1,1,128,128]{4,3,2,1,0:T(8,128)(2,1)}), bf16[128,1,1,128,128]{4,3,2,1,0:T(8,128)(2,1)}, u32[]{:S(2)}, u32[]{:S(2)}) async-start(bf16[128,1,1,128,128]{4,3,2,1,0:T(8,128)(2,1)} %shard_map.75), calls=%async_computation.2 | async-start | bytes 8388608 | tf_op jit(solution)/shard_map/all_to_all | solution.py:155
  77.2 0.0 copy-done.5
  77.3 0.7 gather_fusion
  77.9 0.0 copy-done.6
  77.9 0.2 copy.19.kappa_ref
  78.2 0.0 copy-done.7
  78.2 0.2 copy.20.eig_ref
  78.4 0.0 copy-done
  78.4 0.7 gather_fusion.1
  79.1 0.1 add.68
  79.2 0.1 lt.23
  79.4 0.1 multiply_divide_fusion.invden_ref
  79.5 0.0 copy-start.3
  79.5 3.1 %fusion = (bf16[1024,1024]{1,0:T(8,128)(2,1)S(1)}, bf16[1024,1024]{1,0:T(8,128)(2,1)S(1)}) fusion(bf16[1024,1024]{1,0:T(8,128)(2,1)} %param.17, bf16[1024,1024]{1,0:T(8,128)(2,1)} %param.16), kind=kLoop, calls=%fused_computation.4 | loop fusion | flops 8388608 | bytes 8388608 | tf_op jit(solution)/shard_map/convert_element_type | solution.py:174
  82.6 0.0 copy-done.3
  82.7 24.8 %shard_map.74 = bf16[8,1,16,128,128]{4,3,2,1,0:T(8,128)(2,1)} custom-call(bf16[16,8,1,1,128,128]{5,4,3,2,1,0:T(8,128)(2,1)} %bitcast.x_ref, f32[16,8,128]{2,1,0:T(8,128)S(1)} %scatter.9.info_ref, f32[1024,1]{1,0:T(8,128)S(1)} %copy.19.kappa_ref, f32[1024,1]{1,0:T(8,128)S(1)} %multiply_divide_fusion.invden_ref, f32[1024,1]{1,0:T(8,128)S(1)} %copy.20.eig_ref, ...), custom_call_target="tpu_custom_call" | custom-call | flops 8589934592 | bytes 12582912 | tf_op jit(solution)/shard_map/pallas_call | solution.py:88
  107.4 0.0 copy-start.1
  107.4 1.4 copy-done.1
  108.8 21.3 %all-to-all-done.2 = bf16[128,1,1,128,128]{4,3,2,1,0:T(8,128)(2,1)} async-done(((bf16[128,1,1,128,128]{4,3,2,1,0:T(8,128)(2,1)}), bf16[128,1,1,128,128]{4,3,2,1,0:T(8,128)(2,1)}, u32[]{:S(2)}, u32[]{:S(2)}) %all-to-all-start.2) | async-done | bytes 4194336 | tf_op jit(solution)/shard_map/all_to_all | solution.py:155
  130.1 5.4 %all-to-all-start.1 = ((bf16[8,1,16,128,128]{4,3,2,1,0:T(8,128)(2,1)}), bf16[8,1,16,128,128]{4,3,2,1,0:T(8,128)(2,1)}, u32[]{:S(2)}, u32[]{:S(2)}) async-start(bf16[8,1,16,128,128]{4,3,2,1,0:T(8,128)(2,1)} %shard_map.74), calls=%async_computation.1 | async-start | bytes 8388608 | tf_op jit(solution)/shard_map/all_to_all | solution.py:178
  135.4 0.0 copy-start.2
  135.4 1.6 copy-done.2
  137.0 0.0 copy-start.4
  137.0 1.0 copy-done.4
  138.1 24.8 %shard_map.76 = bf16[8,1,16,128,128]{4,3,2,1,0:T(8,128)(2,1)} custom-call(bf16[16,8,1,1,128,128]{5,4,3,2,1,0:T(8,128)(2,1)} %bitcast.5.x_ref, f32[16,8,128]{2,1,0:T(8,128)S(1)} %scatter.9.info_ref, f32[1024,1]{1,0:T(8,128)S(1)} %copy.19.kappa_ref, f32[1024,1]{1,0:T(8,128)S(1)} %copy-done.4, f32[1024,1]{1,0:T(8,128)S(1)} %copy.20.eig_ref, ...), custom_call_target="tpu_custom_call" | custom-call | flops 8589934592 | bytes 12582912 | tf_op jit(solution)/shard_map/pallas_call | solution.py:88
  162.9 21.4 %all-to-all-done.1.refs_0_ = bf16[8,1,16,128,128]{4,3,2,1,0:T(8,128)(2,1)} async-done(((bf16[8,1,16,128,128]{4,3,2,1,0:T(8,128)(2,1)}), bf16[8,1,16,128,128]{4,3,2,1,0:T(8,128)(2,1)}, u32[]{:S(2)}, u32[]{:S(2)}) %all-to-all-start.1) | async-done | bytes 4194336 | tf_op jit(solution)/shard_map/all_to_all | solution.py:178
  184.2 54.1 %all_to_all.20.refs_1_ = bf16[8,1,16,128,128]{4,3,2,1,0:T(8,128)(2,1)} all-to-all(bf16[8,1,16,128,128]{4,3,2,1,0:T(8,128)(2,1)} %shard_map.76), channel_id=1, replica_groups=mesh['rad'=8,'mode'=16] {'rad'}, dimensions={0} | all-to-all | bytes 8388608 | tf_op jit(solution)/shard_map/all_to_all | solution.py:178
  238.3 7.8 %shard_map.77 = bf16[2,16,128,1024]{3,2,1,0:T(8,128)(2,1)} custom-call(bf16[8,1,16,128,128]{4,3,2,1,0:T(8,128)(2,1)} %all-to-all-done.1.refs_0_, bf16[8,1,16,128,128]{4,3,2,1,0:T(8,128)(2,1)} %all_to_all.20.refs_1_), custom_call_target="tpu_custom_call" | custom-call | tf_op jit(solution)/shard_map/pallas_call | solution.py:121
  (10 shorter events, 0.1 us)
Async XLA Ops:
  0.0 78.4 %copy-start = (s32[256]{0:T(256)S(1)}, s32[256]{0:T(256)}, u32[]{:S(2)}) copy-start(s32[256]{0:T(256)} %param.18) | copy-start | bytes 3076
  7.1 64.7 %all-to-all-start = ((bf16[128,1,1,128,128]{4,3,2,1,0:T(8,128)(2,1)}), bf16[128,1,1,128,128]{4,3,2,1,0:T(8,128)(2,1)}, u32[]{:S(2)}, u32[]{:S(2)}) async-start(bf16[128,1,1,128,128]{4,3,2,1,0:T(8,128)(2,1)} %shard_map.73), calls=%async_computation | async-start | bytes 8388608 | tf_op jit(solution)/shard_map/all_to_all | solution.py:155
  24.6 52.6 %copy-start.5 = (s32[256]{0:T(256)S(1)}, s32[256]{0:T(256)}, u32[]{:S(2)}) copy-start(s32[256]{0:T(256)} %param.19) | copy-start | bytes 3076
  24.6 53.3 %copy-start.6 = (f32[1024]{0:T(1024)S(1)}, f32[1024]{0:T(1024)}, u32[]{:S(2)}) copy-start(f32[1024]{0:T(1024)} %param.14) | copy-start | bytes 12292
  24.6 53.5 %copy-start.7 = (f32[1024]{0:T(1024)S(1)}, f32[1024]{0:T(1024)}, u32[]{:S(2)}) copy-start(f32[1024]{0:T(1024)} %param.15) | copy-start | bytes 12292
  71.7 58.3 %all-to-all-start.2 = ((bf16[128,1,1,128,128]{4,3,2,1,0:T(8,128)(2,1)}), bf16[128,1,1,128,128]{4,3,2,1,0:T(8,128)(2,1)}, u32[]{:S(2)}, u32[]{:S(2)}) async-start(bf16[128,1,1,128,128]{4,3,2,1,0:T(8,128)(2,1)} %shard_map.75), calls=%async_computation.2 | async-start | bytes 8388608 | tf_op jit(solution)/shard_map/all_to_all | solution.py:155
  79.5 3.2 %copy-start.3 = (f32[1024,1]{1,0:T(8,128)}, f32[1024,1]{1,0:T(8,128)S(1)}, u32[]{:S(2)}) copy-start(f32[1024,1]{1,0:T(8,128)S(1)} %multiply_divide_fusion.invden_ref) | copy-start | bytes 12292
  107.4 1.4 copy-start.1
  130.1 54.2 %all-to-all-start.1 = ((bf16[8,1,16,128,128]{4,3,2,1,0:T(8,128)(2,1)}), bf16[8,1,16,128,128]{4,3,2,1,0:T(8,128)(2,1)}, u32[]{:S(2)}, u32[]{:S(2)}) async-start(bf16[8,1,16,128,128]{4,3,2,1,0:T(8,128)(2,1)} %shard_map.74), calls=%async_computation.1 | async-start | bytes 8388608 | tf_op jit(solution)/shard_map/all_to_all | solution.py:178
  135.4 1.6 copy-start.2
  137.0 1.0 copy-start.4

commit v5 on v4

v5 whole, which is shorter than its diff:
```python
import functools

import jax
import jax.numpy as jnp
from jax import lax
from jax.experimental import pallas as pl
from jax.experimental.pallas import tpu as pltpu
from jax.sharding import PartitionSpec as P

PAD = 8


def layout_tables(groups, nrad, rows_here, slots_total, orders_total):
    window = slots_total // nrad
    nwin = []
    for s in range(groups):
        least = (s * rows_here) * slots_total // (2 * orders_total)
        nwin.append(max(1, min(nrad, -(-(slots_total - least) // window))))
    load = [0] * nrad
    shift = [0] * groups
    for s in sorted(range(groups), key=lambda s: nwin[s]):
        best = None
        for sh in range(nrad):
            trial = load[:]
            for w in range(nwin[s], nrad):
                trial[(w + sh) % nrad] += 1
            key = (max(trial), sum(x * x for x in trial))
            if best is None or key < best[0]:
                best = (key, sh, trial)
        shift[s], load = best[1], best[2]
    lists = []
    for r in range(nrad):
        lists.append([s for s in range(groups) if (r - shift[s]) % nrad < nwin[s]])
    count = max(len(x) for x in lists)
    pos_tab, win_tab, ok_tab = [], [], []
    for r in range(nrad):
        entries = lists[r] + [lists[r][0]] * (count - len(lists[r]))
        pos_tab.append(entries)
        win_tab.append([(r - shift[s]) % nrad for s in entries])
        ok_tab.append([1] * len(lists[r]) + [0] * (count - len(lists[r])))
    src_r, src_j, src_ok = [], [], []
    for s in range(groups):
        for w in range(nrad):
            r = (w + shift[s]) % nrad
            live = w < nwin[s]
            src_r.append(r)
            src_j.append(lists[r].index(s) if live else 0)
            src_ok.append(1 if live else 0)
    dest_tab = [[(w + shift[s]) % nrad for w in range(nrad)] for s in range(groups)]
    return dict(count=count, pos=pos_tab, win=win_tab, ok=ok_tab, src_r=src_r, src_j=src_j,
                src_ok=src_ok, dest=dest_tab)


def pack_kernel(picks_ref, dest_ref, *refs):
    x_refs, o_ref = refs[:-1], refs[-1]
    nrad, window = o_ref.shape[0] // len(x_refs), o_ref.shape[-1]
    for i, x_ref in enumerate(x_refs):
        for w in range(nrad):
            o_ref[i * nrad + dest_ref[w]] = x_ref[:, 0:1, :, w * window:(w + 1) * window]


def pack(spectra, picks, dests, comp, groups, nrad, per_group, step=4):
    comps, rows_here, shells_here, slots_total = spectra.shape
    window = slots_total // nrad
    picks_total = groups * per_group

    def in_map(i):
        return lambda q, p, d: (comp, p[q * step + i], 0, 0)

    def out_map(q, p, d):
        return (q, 0, 0, 0, 0)

    assert per_group == 1 and picks_total % step == 0
    return pl.pallas_call(
        pack_kernel,
        out_shape=jax.ShapeDtypeStruct(
            (groups * nrad, 1, per_group, shells_here, window), spectra.dtype
        ),
        grid_spec=pltpu.PrefetchScalarGridSpec(
            num_scalar_prefetch=2,
            grid=(picks_total // step,),
            in_specs=[
                pl.BlockSpec((1, 1, shells_here, slots_total), in_map(i))
                for i in range(step)
            ],
            out_specs=pl.BlockSpec((step * nrad, 1, per_group, shells_here, window), out_map),
        ),
    )(picks, dests, *([spectra] * step))


def solve_kernel(pos_ref, x_ref, info_ref, kappa_ref, invden_ref, eig_ref, d_ref, b_ref, o_ref,
                 pad_ref):
    nrad = x_ref.shape[1]
    sh, window = x_ref.shape[4], x_ref.shape[5]
    nr = nrad * sh
    f = x_ref[0, :, 0, 0].reshape(nr, window).astype(jnp.float32)
    width = f.shape[1]
    pad_ref[0:PAD, :] = jnp.zeros((PAD, width), jnp.float32)
    pad_ref[PAD + nr:PAD + nr + PAD, :] = jnp.zeros((PAD, width), jnp.float32)
    pad_ref[PAD:PAD + nr, :] = f
    m2 = pad_ref[PAD - 2:PAD - 2 + nr, :]
    m1 = pad_ref[PAD - 1:PAD - 1 + nr, :]
    p1 = pad_ref[PAD + 1:PAD + 1 + nr, :]
    p2 = pad_ref[PAD + 2:PAD + 2 + nr, :]
    second = (-m2 + 16.0 * m1 - 30.0 * f + 16.0 * p1 - p2) / 12.0
    deg = info_ref[0, 0:1, :]
    live = info_ref[0, 1:2, :] > 0.5
    lterm = deg * (deg + 1.0)
    damping = lterm * invden_ref[...]
    updated = f + 0.5 * kappa_ref[...] * (second - damping * f)
    updated = jnp.where(live, updated, 0.0).astype(jnp.bfloat16)
    projected = jnp.dot(d_ref[...], updated, preferred_element_type=jnp.float32)
    divisor = eig_ref[...] + 0.5 * lterm / float(nr * nr)
    scaled = (projected / divisor).astype(jnp.bfloat16)
    restored = jnp.dot(b_ref[...], scaled, preferred_element_type=jnp.float32)
    solved = jnp.where(live, restored, 0.0).astype(jnp.bfloat16)
    o_ref[:, 0, 0] = solved.reshape(nrad, sh, window)


def solve(recv, pos, info, kappa, invden, eig, dual_full, basis_full, groups, nrad, per_group):
    _, _, _, sh, window = recv.shape
    nr = nrad * sh
    count = pos.shape[0]
    assert per_group == 1
    x = recv.reshape(groups, nrad, 1, per_group, sh, window)
    flops = 2 * 2 * nr * nr * window * count
    return pl.pallas_call(
        solve_kernel,
        out_shape=jax.ShapeDtypeStruct((nrad, 1, count, sh, window), jnp.bfloat16),
        grid_spec=pltpu.PrefetchScalarGridSpec(
            num_scalar_prefetch=1,
            grid=(count,),
            in_specs=[
                pl.BlockSpec((1, nrad, 1, 1, sh, window), lambda q, p: (p[q], 0, 0, 0, 0, 0)),
                pl.BlockSpec((1, 8, window), lambda q, p: (q, 0, 0)),
                pl.BlockSpec((nr, 1), lambda q, p: (0, 0)),
                pl.BlockSpec((nr, 1), lambda q, p: (0, 0)),
                pl.BlockSpec((nr, 1), lambda q, p: (0, 0)),
                pl.BlockSpec((nr, nr), lambda q, p: (0, 0)),
                pl.BlockSpec((nr, nr), lambda q, p: (0, 0)),
            ],
            out_specs=pl.BlockSpec((nrad, 1, 1, sh, window), lambda q, p: (0, 0, q, 0, 0)),
            scratch_shapes=[pltpu.VMEM((nr + 2 * PAD, window), jnp.float32)],
        ),
        compiler_params=pltpu.CompilerParams(vmem_limit_bytes=48 * 1024 * 1024),
        cost_estimate=pl.CostEstimate(
            flops=flops, transcendentals=0, bytes_accessed=4 * count * nr * window + 4 * nr * nr
        ),
    )(pos, x, info, kappa, invden, eig, dual_full, basis_full)


def unpack_kernel(r_ref, j_ref, ok_ref, *refs):
    x_refs, o_ref = refs[:-1], refs[-1]
    nrad, window = x_refs[0].shape[0], x_refs[0].shape[-1]
    s = pl.program_id(0)
    for c, x_ref in enumerate(x_refs):
        for w in range(nrad):
            k = s * nrad + w
            blk = x_ref[r_ref[k], 0, j_ref[k]]
            o_ref[c, 0, :, w * window:(w + 1) * window] = jnp.where(
                ok_ref[k] > 0, blk, jnp.zeros_like(blk)
            )


def unpack(gots, src_r, src_j, src_ok, rows_here):
    nrad, _, count, sh, window = gots[0].shape
    comps = len(gots)
    return pl.pallas_call(
        unpack_kernel,
        out_shape=jax.ShapeDtypeStruct((comps, rows_here, sh, nrad * window), gots[0].dtype),
        grid_spec=pltpu.PrefetchScalarGridSpec(
            num_scalar_prefetch=3,
            grid=(rows_here,),
            in_specs=[
                pl.BlockSpec((nrad, 1, count, sh, window), lambda s, a, b, c: (0, 0, 0, 0, 0))
                for _ in gots
            ],
            out_specs=pl.BlockSpec(
                (comps, 1, sh, nrad * window), lambda s, a, b, c: (0, s, 0, 0)
            ),
        ),
        compiler_params=pltpu.CompilerParams(vmem_limit_bytes=48 * 1024 * 1024),
    )(src_r, src_j, src_ok, *gots)


def on_device(
    spectra, diffusivity, eigenvalues, radial_basis, dual_basis, degree_count, order_slot
):
    comps, rows_here, shells_here, slots_total = spectra.shape
    shells_total = diffusivity.shape[0]
    orders_total = degree_count.shape[0]
    groups = lax.axis_size("mode")
    nrad = lax.axis_size("rad")
    per_group = rows_here // groups
    window = slots_total // nrad
    me_mode = lax.axis_index("mode")
    me_rad = lax.axis_index("rad")
    tab = layout_tables(groups, nrad, rows_here, slots_total, orders_total)

    picks = (
        lax.dynamic_slice_in_dim(
            order_slot.reshape(groups, groups, per_group), me_mode, 1, 1
        ).reshape(groups * per_group)
        - me_mode * rows_here
    )
    dests = jnp.asarray(tab["dest"], jnp.int32)[me_mode]
    recvs = []
    for comp in range(comps):
        send = pack(spectra, picks, dests, comp, groups, nrad, per_group)
        recvs.append(lax.all_to_all(send, ("mode", "rad"), 0, 0, tiled=True))

    pos = jnp.asarray(tab["pos"], jnp.int32)[me_rad]
    win = jnp.asarray(tab["win"], jnp.int32)[me_rad]
    ok = jnp.asarray(tab["ok"], jnp.int32)[me_rad]
    in_rows = jnp.take(order_slot, me_mode * rows_here + pos)
    orders = in_rows * slots_total // (2 * orders_total)
    slot_ids = win[:, None] * window + jnp.arange(window, dtype=jnp.int32)[None, :]
    degree = (orders[:, None] + slot_ids).astype(jnp.float32)
    live = (slot_ids < jnp.take(degree_count, in_rows)[:, None]) & (ok[:, None] > 0)
    count = tab["count"]
    info = jnp.zeros((count, 8, window), jnp.float32)
    info = info.at[:, 0, :].set(degree)
    info = info.at[:, 1, :].set(live.astype(jnp.float32))

    radius = 1.2 + jnp.arange(shells_total, dtype=jnp.int32).astype(jnp.float32) / shells_total
    invden = (1.0 / ((shells_total * radius) ** 2)).reshape(shells_total, 1)
    kappa = diffusivity.reshape(shells_total, 1)
    eig = eigenvalues.reshape(shells_total, 1)

    identity = jnp.eye(shells_total, dtype=jnp.float32)
    basis_full = (identity + radial_basis.astype(jnp.float32)).astype(jnp.bfloat16)
    dual_full = (identity + dual_basis.astype(jnp.float32)).astype(jnp.bfloat16)
    gots = []
    for recv in recvs:
        back = solve(recv, pos, info, kappa, invden, eig, dual_full, basis_full, groups, nrad,
                     per_group)
        gots.append(lax.all_to_all(back, "rad", 0, 0, tiled=True))
    src_r = jnp.asarray(tab["src_r"], jnp.int32)
    src_j = jnp.asarray(tab["src_j"], jnp.int32)
    src_ok = jnp.asarray(tab["src_ok"], jnp.int32)
    return unpack(gots, src_r, src_j, src_ok, rows_here)


def solution(mesh):
    placed = (P(None, "mode", "rad", None), P(), P(), P(), P(), P(), P())
    return jax.shard_map(
        on_device,
        mesh=mesh,
        in_specs=placed,
        out_specs=P(None, "mode", "rad", None),
        check_vma=False,
    )
```

time: 247 us -> 233 us (0.943)
  waiting for transfers between devices: 89.8 us -> 56.1 us
  Pallas kernels: 68.5 us -> 89 us
  blocking collectives: 54.1 us -> 45.6 us
  local copies, waits for them, and re-layouts: 6.77 us -> 13.7 us
    all_to_all x1, waiting for transfers between devices: 21.4 us -> 0.3 us  [on_device(): gots.append(lax.all_to_all(back, 'rad', 0, 0, tiled=True))]
    pallas_call x2, Pallas kernels: 49.6 us -> 67.4 us  [solve(): pl.pallas_call(solve_kernel, out_shape=jax.ShapeDtypeStruct((nrad, 1, cou...]
    all_to_all x2, waiting for transfers between devices: 68.4 us -> 55.8 us  [on_device(): recvs.append(lax.all_to_all(send, ('mode', 'rad'), 0, 0, tiled=True))]
    all_to_all x1, blocking collectives: 54.1 us -> 45.6 us  [on_device(): gots.append(lax.all_to_all(back, 'rad', 0, 0, tiled=True))]
    unnamed x16 -> x36, local copies, waits for them, and re-layouts: 4.02 us -> 9.1 us
    pallas_call x1, Pallas kernels: 7.83 us -> 10.4 us  [unpack(): pl.pallas_call(unpack_kernel, out_shape=jax.ShapeDtypeStruct((comps, rows...]
  transfers between devices with their start and end apart: 3 -> 3, of which waited for: 3 -> 3; matrix products, arithmetic and copies ran while one was open for 2% -> 3% of each run, Pallas kernels for 22% -> 31%
where the time goes in v5:
time: 233 us; the launch traced here: 232 us
  Pallas kernels  89 us (38%)
  waiting for transfers between devices  56.1 us (24%)
  blocking collectives  45.6 us (20%)
  starting transfers between devices  21.9 us (9%)
  local copies, waits for them, and re-layouts  13.7 us (6%)
  other arithmetic  5.58 us (2%)
    pallas_call x2, Pallas kernels, solve(): pl.pallas_call(solve_kernel, out_shape=jax.ShapeDtypeStruct((nrad, 1, cou...  67.4 us
    all_to_all x2, waiting for transfers between devices, on_device(): recvs.append(lax.all_to_all(send, ('mode', 'rad'), 0, 0, tiled=True))  55.8 us
    all_to_all x1, blocking collectives, on_device(): gots.append(lax.all_to_all(back, 'rad', 0, 0, tiled=True))  45.6 us
    all_to_all x2, starting transfers between devices, on_device(): recvs.append(lax.all_to_all(send, ('mode', 'rad'), 0, 0, tiled=True))  17.4 us
    pallas_call x2, Pallas kernels, pack(): pl.pallas_call(pack_kernel, out_shape=jax.ShapeDtypeStruct((groups * nrad...  11.2 us
    pallas_call x1, Pallas kernels, unpack(): pl.pallas_call(unpack_kernel, out_shape=jax.ShapeDtypeStruct((comps, rows...  10.4 us
    unnamed x36, local copies, waits for them, and re-layouts  9.1 us
  transfers between devices with their start and end apart: 3, of which 3 were waited for; matrix products, arithmetic and copies ran while one was open for 3% of the time, Pallas kernels for 31%

profile of v5, /device:TPU:1, one launch (start us, length us, event | category | flops | bytes accessed | tf_op | source)
XLA Modules:
  0.0 232.1 jit_solution(1916668903176081944)
XLA Ops:
  0.0 0.0 copy-start
  0.0 0.8 reshape.201
  0.8 1.3 fusion.3.dest_ref
  2.1 0.7 subtract_reduce_fusion.picks_ref
  2.8 5.6 %shard_map.136 = bf16[128,1,1,128,128]{4,3,2,1,0:T(8,128)(2,1)} custom-call(s32[16]{0:T(128)} %subtract_reduce_fusion.picks_ref, s32[8]{0:T(128)} %fusion.3.dest_ref, bf16[2,16,128,1024]{3,2,1,0:T(8,128)(2,1)} %refs_3_.3, bf16[2,16,128,1024]{3,2,1,0:T(8,128)(2,1)} %refs_3_.3, bf16[2,16,128,1024]{3,2,1,0:T(8,128)(2,1)} %refs_3_.3, ...), custom_call_target="tpu_custom_call" | custom-call | tf_op jit(solution)/shard_map/pallas_call | solution.py:74
  8.3 11.9 %all-to-all-start = ((bf16[128,1,1,128,128]{4,3,2,1,0:T(8,128)(2,1)}), bf16[128,1,1,128,128]{4,3,2,1,0:T(8,128)(2,1)}, u32[]{:S(2)}, u32[]{:S(2)}) async-start(bf16[128,1,1,128,128]{4,3,2,1,0:T(8,128)(2,1)} %shard_map.136), calls=%async_computation | async-start | bytes 8388608 | tf_op jit(solution)/shard_map/all_to_all | solution.py:210
  20.3 5.7 %shard_map.138 = bf16[128,1,1,128,128]{4,3,2,1,0:T(8,128)(2,1)} custom-call(s32[16]{0:T(128)} %subtract_reduce_fusion.picks_ref, s32[8]{0:T(128)} %fusion.3.dest_ref, bf16[2,16,128,1024]{3,2,1,0:T(8,128)(2,1)} %refs_3_.3, bf16[2,16,128,1024]{3,2,1,0:T(8,128)(2,1)} %refs_3_.3, bf16[2,16,128,1024]{3,2,1,0:T(8,128)(2,1)} %refs_3_.3, ...), custom_call_target="tpu_custom_call" | custom-call | tf_op jit(solution)/shard_map/pallas_call | solution.py:74
  25.9 0.0 copy-start.14
  25.9 0.0 copy-start.16
  25.9 0.0 copy-start.17
  25.9 0.0 copy-start.15
  26.0 47.0 %all-to-all-done = bf16[128,1,1,128,128]{4,3,2,1,0:T(8,128)(2,1)} async-done(((bf16[128,1,1,128,128]{4,3,2,1,0:T(8,128)(2,1)}), bf16[128,1,1,128,128]{4,3,2,1,0:T(8,128)(2,1)}, u32[]{:S(2)}, u32[]{:S(2)}) %all-to-all-start) | async-done | bytes 4194336 | tf_op jit(solution)/shard_map/all_to_all | solution.py:210
  73.0 5.5 %all-to-all-start.2 = ((bf16[128,1,1,128,128]{4,3,2,1,0:T(8,128)(2,1)}), bf16[128,1,1,128,128]{4,3,2,1,0:T(8,128)(2,1)}, u32[]{:S(2)}, u32[]{:S(2)}) async-start(bf16[128,1,1,128,128]{4,3,2,1,0:T(8,128)(2,1)} %shard_map.138), calls=%async_computation.2 | async-start | bytes 8388608 | tf_op jit(solution)/shard_map/all_to_all | solution.py:210
  78.5 0.7 compare_select_fusion.1
  79.2 0.0 copy-done.14
  79.2 0.7 gather_fusion
  79.9 0.0 copy-done.16
  79.9 0.2 copy.24.kappa_ref
  80.1 0.0 copy-start.5
  80.1 0.0 copy-done.17
  80.1 0.2 copy.25.eig_ref
  80.4 0.0 copy-start.7
  80.4 0.7 compare_select_fusion
  81.1 0.0 copy-done
  81.1 0.7 gather_fusion.1
  81.8 0.7 fusion.5
  82.5 0.1 add_convert_fusion
  82.6 0.1 compare_convert_fusion
  82.8 0.7 fusion.2.pos_ref
  83.5 0.1 multiply_divide_fusion.invden_ref
  83.6 0.0 copy-done.15
  83.6 0.0 copy-start.9
  83.6 2.4 %fusion = (bf16[1024,1024]{1,0:T(8,128)(2,1)S(1)}, bf16[1024,1024]{1,0:T(8,128)(2,1)S(1)}) fusion(bf16[1024,1024]{1,0:T(8,128)(2,1)S(1)} %copy-done.15, bf16[1024,1024]{1,0:T(8,128)(2,1)} %param.23), kind=kLoop, calls=%fused_computation.4 | loop fusion | flops 8388608 | bytes 8388608 | tf_op jit(solution)/shard_map/convert_element_type | solution.py:232
  86.0 0.0 copy-done.5
  86.0 0.0 copy-done.7
  86.1 0.0 copy-done.9
  86.1 33.7 %shard_map.137 = bf16[8,1,13,128,128]{4,3,2,1,0:T(8,128)(2,1)} custom-call(s32[13]{0:T(128)S(1)} %fusion.2.pos_ref, bf16[16,8,1,1,128,128]{5,4,3,2,1,0:T(8,128)(2,1)} %bitcast.2.x_ref, f32[13,8,128]{2,1,0:T(8,128)S(1)} %scatter.9.info_ref, f32[1024,1]{1,0:T(8,128)S(1)} %copy.24.kappa_ref, f32[1024,1]{1,0:T(8,128)S(1)} %multiply_divide_fusion.invden_ref, ...), custom_call_target="tpu_custom_call" | custom-call | flops 6979321856 | bytes 11010048 | tf_op jit(solution)/shard_map/pallas_call | solution.py:127
  119.8 0.0 copy-start.1
  119.8 1.4 copy-done.1
  121.2 0.0 copy-start.3
  121.2 1.4 copy-done.3
  122.6 8.8 %all-to-all-done.2 = bf16[128,1,1,128,128]{4,3,2,1,0:T(8,128)(2,1)} async-done(((bf16[128,1,1,128,128]{4,3,2,1,0:T(8,128)(2,1)}), bf16[128,1,1,128,128]{4,3,2,1,0:T(8,128)(2,1)}, u32[]{:S(2)}, u32[]{:S(2)}) %all-to-all-start.2) | async-done | bytes 4194336 | tf_op jit(solution)/shard_map/all_to_all | solution.py:210
  131.4 4.5 %all-to-all-start.1 = ((bf16[8,1,13,128,128]{4,3,2,1,0:T(8,128)(2,1)}), bf16[8,1,13,128,128]{4,3,2,1,0:T(8,128)(2,1)S(1)}, u32[]{:S(2)}, u32[]{:S(2)}) async-start(bf16[8,1,13,128,128]{4,3,2,1,0:T(8,128)(2,1)} %shard_map.137), calls=%async_computation.1 | async-start | bytes 6815744 | tf_op jit(solution)/shard_map/all_to_all | solution.py:237
  135.8 0.0 copy-start.2
  135.8 1.6 copy-done.2
  137.4 0.0 copy-start.4
  137.4 1.6 copy-done.4
  139.0 0.0 copy-start.6
  139.0 1.0 copy-done.6
  140.1 0.0 copy-start.8
  140.1 1.0 copy-done.8
  141.1 0.0 copy-start.10
  141.1 1.0 copy-done.10
  142.2 33.7 %shard_map.139 = bf16[8,1,13,128,128]{4,3,2,1,0:T(8,128)(2,1)} custom-call(s32[13]{0:T(128)S(1)} %fusion.2.pos_ref, bf16[16,8,1,1,128,128]{5,4,3,2,1,0:T(8,128)(2,1)} %bitcast.6.x_ref, f32[13,8,128]{2,1,0:T(8,128)S(1)} %scatter.9.info_ref, f32[1024,1]{1,0:T(8,128)S(1)} %copy-done.6, f32[1024,1]{1,0:T(8,128)S(1)} %copy-done.10, f32[1024,1]{1,0:T(8,128)S(1)} %copy-done.8, ...), custom_call_target="tpu_custom_call" | custom-call | flops 6979321856 | bytes 11010048 | tf_op jit(solution)/shard_map/pallas_call | solution.py:127
  175.8 0.0 copy-start.11
  175.8 0.0 copy-start.12
  175.8 0.0 copy-start.13
  175.8 0.3 all-to-all-done.1.refs_0_
  176.1 45.6 %all_to_all.20.refs_1_ = bf16[8,1,13,128,128]{4,3,2,1,0:T(8,128)(2,1)} all-to-all(bf16[8,1,13,128,128]{4,3,2,1,0:T(8,128)(2,1)} %shard_map.139), channel_id=1, replica_groups=mesh['rad'=8,'mode'=16] {'rad'}, dimensions={0} | all-to-all | bytes 6815744 | tf_op jit(solution)/shard_map/all_to_all | solution.py:237
  221.7 0.0 copy-done.11
  221.7 0.0 copy-done.12
  221.7 0.0 copy-done.13
  221.8 10.4 %shard_map.140 = bf16[2,16,128,1024]{3,2,1,0:T(8,128)(2,1)} custom-call(s32[128]{0:T(128)S(1)} %copy-done.13, s32[128]{0:T(128)S(1)} %copy-done.12, s32[128]{0:T(128)S(1)} %copy-done.11, bf16[8,1,13,128,128]{4,3,2,1,0:T(8,128)(2,1)S(1)} %all-to-all-done.1.refs_0_, bf16[8,1,13,128,128]{4,3,2,1,0:T(8,128)(2,1)} %all_to_all.20.refs_1_), custom_call_target="tpu_custom_call" | custom-call | tf_op jit(solution)/shard_map/pallas_call | solution.py:168
  (5 shorter events, 0.1 us)
Async XLA Ops:
  0.0 81.1 %copy-start = (s32[256]{0:T(256)S(1)}, s32[256]{0:T(256)}, u32[]{:S(2)}) copy-start(s32[256]{0:T(256)} %param.25) | copy-start | bytes 3076
  8.3 64.7 %all-to-all-start = ((bf16[128,1,1,128,128]{4,3,2,1,0:T(8,128)(2,1)}), bf16[128,1,1,128,128]{4,3,2,1,0:T(8,128)(2,1)}, u32[]{:S(2)}, u32[]{:S(2)}) async-start(bf16[128,1,1,128,128]{4,3,2,1,0:T(8,128)(2,1)} %shard_map.136), calls=%async_computation | async-start | bytes 8388608 | tf_op jit(solution)/shard_map/all_to_all | solution.py:210
  25.9 53.3 %copy-start.14 = (s32[256]{0:T(256)S(1)}, s32[256]{0:T(256)}, u32[]{:S(2)}) copy-start(s32[256]{0:T(256)} %param.26) | copy-start | bytes 3076
  25.9 54.0 %copy-start.16 = (f32[1024]{0:T(1024)S(1)}, f32[1024]{0:T(1024)}, u32[]{:S(2)}) copy-start(f32[1024]{0:T(1024)} %param.21) | copy-start | bytes 12292
  25.9 54.2 %copy-start.17 = (f32[1024]{0:T(1024)S(1)}, f32[1024]{0:T(1024)}, u32[]{:S(2)}) copy-start(f32[1024]{0:T(1024)} %param.22) | copy-start | bytes 12292
  25.9 57.7 %copy-start.15 = (bf16[1024,1024]{1,0:T(8,128)(2,1)S(1)}, bf16[1024,1024]{1,0:T(8,128)(2,1)}, u32[]{:S(2)}) copy-start(bf16[1024,1024]{1,0:T(8,128)(2,1)} %param.24) | copy-start | bytes 6291460
  73.0 58.4 %all-to-all-start.2 = ((bf16[128,1,1,128,128]{4,3,2,1,0:T(8,128)(2,1)}), bf16[128,1,1,128,128]{4,3,2,1,0:T(8,128)(2,1)}, u32[]{:S(2)}, u32[]{:S(2)}) async-start(bf16[128,1,1,128,128]{4,3,2,1,0:T(8,128)(2,1)} %shard_map.138), calls=%async_computation.2 | async-start | bytes 8388608 | tf_op jit(solution)/shard_map/all_to_all | solution.py:210
  80.1 5.9 %copy-start.5 = (f32[1024,1]{1,0:T(8,128)}, f32[1024,1]{1,0:T(8,128)S(1)}, u32[]{:S(2)}) copy-start(f32[1024,1]{1,0:T(8,128)S(1)} %copy.24.kappa_ref) | copy-start | bytes 12292
  80.4 5.7 %copy-start.7 = (f32[1024,1]{1,0:T(8,128)}, f32[1024,1]{1,0:T(8,128)S(1)}, u32[]{:S(2)}) copy-start(f32[1024,1]{1,0:T(8,128)S(1)} %copy.25.eig_ref) | copy-start | bytes 12292
  83.6 2.5 %copy-start.9 = (f32[1024,1]{1,0:T(8,128)}, f32[1024,1]{1,0:T(8,128)S(1)}, u32[]{:S(2)}) copy-start(f32[1024,1]{1,0:T(8,128)S(1)} %multiply_divide_fusion.invden_ref) | copy-start | bytes 12292
  119.8 1.4 copy-start.1
  121.2 1.4 copy-start.3
  131.4 44.8 %all-to-all-start.1 = ((bf16[8,1,13,128,128]{4,3,2,1,0:T(8,128)(2,1)}), bf16[8,1,13,128,128]{4,3,2,1,0:T(8,128)(2,1)S(1)}, u32[]{:S(2)}, u32[]{:S(2)}) async-start(bf16[8,1,13,128,128]{4,3,2,1,0:T(8,128)(2,1)} %shard_map.137), calls=%async_computation.1 | async-start | bytes 6815744 | tf_op jit(solution)/shard_map/all_to_all | solution.py:237
  135.8 1.6 copy-start.2
  137.4 1.6 copy-start.4
  139.0 1.0 copy-start.6
  140.1 1.0 copy-start.8
  141.1 1.0 copy-start.10
  175.8 45.9 %copy-start.11 = (s32[128]{0:T(128)S(1)}, s32[128]{0:T(128)}, u32[]{:S(2)}) copy-start(s32[128]{0:T(128)} %constant.127.clone.ok_ref) | copy-start | bytes 1540
  175.8 45.9 %copy-start.12 = (s32[128]{0:T(128)S(1)}, s32[128]{0:T(128)}, u32[]{:S(2)}) copy-start(s32[128]{0:T(128)} %constant.126.clone.j_ref) | copy-start | bytes 1540
  175.8 45.9 %copy-start.13 = (s32[128]{0:T(128)S(1)}, s32[128]{0:T(128)}, u32[]{:S(2)}) copy-start(s32[128]{0:T(128)} %constant.125.clone.r_ref) | copy-start | bytes 1540

commit v6 on v5

--- a/solution.py
+++ b/solution.py
@@ -32,6 +32,7 @@
     for r in range(nrad):
         lists.append([s for s in range(groups) if (r - shift[s]) % nrad < nwin[s]])
     count = max(len(x) for x in lists)
+    count += count % 2
     pos_tab, win_tab, ok_tab = [], [], []
     for r in range(nrad):
         entries = lists[r] + [lists[r][0]] * (count - len(lists[r]))
@@ -88,12 +89,15 @@
     )(picks, dests, *([spectra] * step))
 
 
-def solve_kernel(pos_ref, x_ref, info_ref, kappa_ref, invden_ref, eig_ref, d_ref, b_ref, o_ref,
-                 pad_ref):
-    nrad = x_ref.shape[1]
-    sh, window = x_ref.shape[4], x_ref.shape[5]
+def solve_kernel(pos_ref, *refs):
+    npos = len(refs) - 8
+    x_refs = refs[:npos]
+    info_ref, kappa_ref, invden_ref, eig_ref, d_ref, b_ref, o_ref, pad_ref = refs[npos:]
+    nrad = x_refs[0].shape[1]
+    sh, window = x_refs[0].shape[4], x_refs[0].shape[5]
     nr = nrad * sh
-    f = x_ref[0, :, 0, 0].reshape(nr, window).astype(jnp.float32)
+    cols = [x_ref[0, :, 0, 0].reshape(nr, window) for x_ref in x_refs]
+    f = jnp.concatenate(cols, axis=1).astype(jnp.float32)
     width = f.shape[1]
     pad_ref[0:PAD, :] = jnp.zeros((PAD, width), jnp.float32)
     pad_ref[PAD + nr:PAD + nr + PAD, :] = jnp.zeros((PAD, width), jnp.float32)
@@ -103,8 +107,8 @@
     p1 = pad_ref[PAD + 1:PAD + 1 + nr, :]
     p2 = pad_ref[PAD + 2:PAD + 2 + nr, :]
     second = (-m2 + 16.0 * m1 - 30.0 * f + 16.0 * p1 - p2) / 12.0
-    deg = info_ref[0, 0:1, :]
-    live = info_ref[0, 1:2, :] > 0.5
+    deg = jnp.concatenate([info_ref[j, 0:1, :] for j in range(npos)], axis=1)
+    live = jnp.concatenate([info_ref[j, 1:2, :] for j in range(npos)], axis=1) > 0.5
     lterm = deg * (deg + 1.0)
     damping = lterm * invden_ref[...]
     updated = f + 0.5 * kappa_ref[...] * (second - damping * f)
@@ -114,73 +118,84 @@
     scaled = (projected / divisor).astype(jnp.bfloat16)
     restored = jnp.dot(b_ref[...], scaled, preferred_element_type=jnp.float32)
     solved = jnp.where(live, restored, 0.0).astype(jnp.bfloat16)
-    o_ref[:, 0, 0] = solved.reshape(nrad, sh, window)
-
-
-def solve(recv, pos, info, kappa, invden, eig, dual_full, basis_full, groups, nrad, per_group):
+    for j in range(npos):
+        o_ref[:, 0, j] = solved[:, j * window:(j + 1) * window].reshape(nrad, sh, window)
+
+
+def solve(recv, pos, info, kappa, invden, eig, dual_full, basis_full, groups, nrad, per_group,
+          npos=2):
     _, _, _, sh, window = recv.shape
     nr = nrad * sh
     count = pos.shape[0]
-    assert per_group == 1
+    assert per_group == 1 and count % npos == 0
     x = recv.reshape(groups, nrad, 1, per_group, sh, window)
     flops = 2 * 2 * nr * nr * window * count
+
+    def x_map(j):
+        return lambda q, p: (p[q * npos + j], 0, 0, 0, 0, 0)
+
     return pl.pallas_call(
         solve_kernel,
         out_shape=jax.ShapeDtypeStruct((nrad, 1, count, sh, window), jnp.bfloat16),
         grid_spec=pltpu.PrefetchScalarGridSpec(
             num_scalar_prefetch=1,
-            grid=(count,),
+            grid=(count // npos,),
             in_specs=[
-                pl.BlockSpec((1, nrad, 1, 1, sh, window), lambda q, p: (p[q], 0, 0, 0, 0, 0)),
-                pl.BlockSpec((1, 8, window), lambda q, p: (q, 0, 0)),
+                pl.BlockSpec((1, nrad, 1, 1, sh, window), x_map(j)) for j in range(npos)
+            ] + [
+                pl.BlockSpec((npos, 8, window), lambda q, p: (q, 0, 0)),
                 pl.BlockSpec((nr, 1), lambda q, p: (0, 0)),
                 pl.BlockSpec((nr, 1), lambda q, p: (0, 0)),
                 pl.BlockSpec((nr, 1), lambda q, p: (0, 0)),
                 pl.BlockSpec((nr, nr), lambda q, p: (0, 0)),
                 pl.BlockSpec((nr, nr), lambda q, p: (0, 0)),
             ],
-            out_specs=pl.BlockSpec((nrad, 1, 1, sh, window), lambda q, p: (0, 0, q, 0, 0)),
-            scratch_shapes=[pltpu.VMEM((nr + 2 * PAD, window), jnp.float32)],
+            out_specs=pl.BlockSpec((nrad, 1, npos, sh, window), lambda q, p: (0, 0, q, 0, 0)),
+            scratch_shapes=[pltpu.VMEM((nr + 2 * PAD, npos * window), jnp.float32)],
         ),
         compiler_params=pltpu.CompilerParams(vmem_limit_bytes=48 * 1024 * 1024),
         cost_estimate=pl.CostEstimate(
             flops=flops, transcendentals=0, bytes_accessed=4 * count * nr * window + 4 * nr * nr
         ),
-    )(pos, x, info, kappa, invden, eig, dual_full, basis_full)
-
-
-def unpack_kernel(r_ref, j_ref, ok_ref, *refs):
-    x_refs, o_ref = refs[:-1], refs[-1]
-    nrad, window = x_refs[0].shape[0], x_refs[0].shape[-1]
+    )(pos, *([x] * npos), info, kappa, invden, eig, dual_full, basis_full)
+
+
+def unpack_kernel(r_ref, j_ref, ok_ref, x_ref, *refs):
+    o_ref = refs[-1]
+    nrad, window = x_ref.shape[0], x_ref.shape[-1]
     s = pl.program_id(0)
-    for c, x_ref in enumerate(x_refs):
-        for w in range(nrad):
-            k = s * nrad + w
-            blk = x_ref[r_ref[k], 0, j_ref[k]]
-            o_ref[c, 0, :, w * window:(w + 1) * window] = jnp.where(
-                ok_ref[k] > 0, blk, jnp.zeros_like(blk)
-            )
-
-
-def unpack(gots, src_r, src_j, src_ok, rows_here):
-    nrad, _, count, sh, window = gots[0].shape
-    comps = len(gots)
+    for w in range(nrad):
+        k = s * nrad + w
+        blk = x_ref[r_ref[k], 0, j_ref[k]]
+        o_ref[0, 0, :, w * window:(w + 1) * window] = jnp.where(
+            ok_ref[k] > 0, blk, jnp.zeros_like(blk)
+        )
+
+
+def unpack(got, comp, comps, prev, src_r, src_j, src_ok, rows_here):
+    nrad, _, count, sh, window = got.shape
+    shape = (comps, rows_here, sh, nrad * window)
+    in_specs = [pl.BlockSpec((nrad, 1, count, sh, window), lambda s, a, b, c: (0, 0, 0, 0, 0))]
+    args = [got]
+    aliases = {}
+    if prev is not None:
+        in_specs.append(pl.BlockSpec(memory_space=pl.ANY))
+        args.append(prev)
+        aliases = {4: 0}
     return pl.pallas_call(
         unpack_kernel,
-        out_shape=jax.ShapeDtypeStruct((comps, rows_here, sh, nrad * window), gots[0].dtype),
+        out_shape=jax.ShapeDtypeStruct(shape, got.dtype),
         grid_spec=pltpu.PrefetchScalarGridSpec(
             num_scalar_prefetch=3,
             grid=(rows_here,),
-            in_specs=[
-                pl.BlockSpec((nrad, 1, count, sh, window), lambda s, a, b, c: (0, 0, 0, 0, 0))
-                for _ in gots
-            ],
+            in_specs=in_specs,
             out_specs=pl.BlockSpec(
-                (comps, 1, sh, nrad * window), lambda s, a, b, c: (0, s, 0, 0)
+                (1, 1, sh, nrad * window), lambda s, a, b, c: (comp, s, 0, 0)
             ),
         ),
+        input_output_aliases=aliases,
         compiler_params=pltpu.CompilerParams(vmem_limit_bytes=48 * 1024 * 1024),
-    )(src_r, src_j, src_ok, *gots)
+    )(src_r, src_j, src_ok, *args)
 
 
 def on_device(
@@ -238,7 +253,10 @@
     src_r = jnp.asarray(tab["src_r"], jnp.int32)
     src_j = jnp.asarray(tab["src_j"], jnp.int32)
     src_ok = jnp.asarray(tab["src_ok"], jnp.int32)
-    return unpack(gots, src_r, src_j, src_ok, rows_here)
+    out = None
+    for comp, got in enumerate(gots):
+        out = unpack(got, comp, comps, out, src_r, src_j, src_ok, rows_here)
+    return out
 
 
 def solution(mesh):

time: 233 us -> 238 us (1.021)
  waiting for transfers between devices: 56.1 us -> 120 us
  blocking collectives: 45.6 us -> 0 us
  Pallas kernels: 89 us -> 73.9 us
  starting transfers between devices: 21.9 us -> 28.1 us
  local copies, waits for them, and re-layouts: 13.7 us -> 8.58 us
    all_to_all x1 -> x2, waiting for transfers between devices: 0.3 us -> 52.3 us  [on_device(): gots.append(lax.all_to_all(back, 'rad', 0, 0, tiled=True))]
    all_to_all x1 -> x0, blocking collectives: 45.6 us -> none  [on_device(): gots.append(lax.all_to_all(back, 'rad', 0, 0, tiled=True))]
    pallas_call x2, Pallas kernels: 67.4 us -> 44.8 us  [solve(): pl.pallas_call(solve_kernel, out_shape=jax.ShapeDtypeStruct((nrad, 1, cou...]
    all_to_all x2, waiting for transfers between devices: 55.8 us -> 67.4 us  [on_device(): recvs.append(lax.all_to_all(send, ('mode', 'rad'), 0, 0, tiled=True))]
    pallas_call x1 -> x2, Pallas kernels: 10.4 us -> 18 us  [unpack(): pl.pallas_call(unpack_kernel, out_shape=jax.ShapeDtypeStruct(shape, got.d...]
    all_to_all x1 -> x2, starting transfers between devices: 4.49 us -> 10.7 us  [on_device(): gots.append(lax.all_to_all(back, 'rad', 0, 0, tiled=True))]
    unnamed x36 -> x22, local copies, waits for them, and re-layouts: 9.1 us -> 4.02 us
  transfers between devices with their start and end apart: 3 -> 4, of which waited for: 3 -> 4; matrix products, arithmetic and copies ran while one was open for 3% -> 4% of each run, Pallas kernels for 31% -> 25%
where the time goes in v6:
time: 238 us; the launch traced here: 237 us
  waiting for transfers between devices  120 us (50%)
  Pallas kernels  73.9 us (31%)
  starting transfers between devices  28.1 us (12%)
  local copies, waits for them, and re-layouts  8.58 us (4%)
  other arithmetic  6.88 us (3%)
    all_to_all x2, waiting for transfers between devices, on_device(): recvs.append(lax.all_to_all(send, ('mode', 'rad'), 0, 0, tiled=True))  67.4 us
    all_to_all x2, waiting for transfers between devices, on_device(): gots.append(lax.all_to_all(back, 'rad', 0, 0, tiled=True))  52.3 us
    pallas_call x2, Pallas kernels, solve(): pl.pallas_call(solve_kernel, out_shape=jax.ShapeDtypeStruct((nrad, 1, cou...  44.8 us
    pallas_call x2, Pallas kernels, unpack(): pl.pallas_call(unpack_kernel, out_shape=jax.ShapeDtypeStruct(shape, got.d...  18 us
    all_to_all x2, starting transfers between devices, on_device(): recvs.append(lax.all_to_all(send, ('mode', 'rad'), 0, 0, tiled=True))  17.4 us
    pallas_call x2, Pallas kernels, pack(): pl.pallas_call(pack_kernel, out_shape=jax.ShapeDtypeStruct((groups * nrad...  11.2 us
    all_to_all x2, starting transfers between devices, on_device(): gots.append(lax.all_to_all(back, 'rad', 0, 0, tiled=True))  10.7 us
  transfers between devices with their start and end apart: 4, of which 4 were waited for; matrix products, arithmetic and copies ran while one was open for 4% of the time, Pallas kernels for 25%

profile of v6, /device:TPU:1, one launch (start us, length us, event | category | flops | bytes accessed | tf_op | source)
XLA Modules:
  0.0 237.4 jit_solution(18281384986337617634)
XLA Ops:
  0.0 0.0 copy-start
  0.0 0.8 reshape.201
  0.8 1.3 fusion.3.dest_ref
  2.0 0.7 subtract_reduce_fusion.picks_ref
  2.8 5.6 %shard_map.138 = bf16[128,1,1,128,128]{4,3,2,1,0:T(8,128)(2,1)} custom-call(s32[16]{0:T(128)} %subtract_reduce_fusion.picks_ref, s32[8]{0:T(128)} %fusion.3.dest_ref, bf16[2,16,128,1024]{3,2,1,0:T(8,128)(2,1)} %refs_3_.3, bf16[2,16,128,1024]{3,2,1,0:T(8,128)(2,1)} %refs_3_.3, bf16[2,16,128,1024]{3,2,1,0:T(8,128)(2,1)} %refs_3_.3, ...), custom_call_target="tpu_custom_call" | custom-call | tf_op jit(solution)/shard_map/pallas_call | solution.py:75
  8.3 11.9 %all-to-all-start.2 = ((bf16[128,1,1,128,128]{4,3,2,1,0:T(8,128)(2,1)}), bf16[128,1,1,128,128]{4,3,2,1,0:T(8,128)(2,1)}, u32[]{:S(2)}, u32[]{:S(2)}) async-start(bf16[128,1,1,128,128]{4,3,2,1,0:T(8,128)(2,1)} %shard_map.138), calls=%async_computation.2 | async-start | bytes 8388608 | tf_op jit(solution)/shard_map/all_to_all | solution.py:225
  20.3 5.6 %shard_map.136 = bf16[128,1,1,128,128]{4,3,2,1,0:T(8,128)(2,1)} custom-call(s32[16]{0:T(128)} %subtract_reduce_fusion.picks_ref, s32[8]{0:T(128)} %fusion.3.dest_ref, bf16[2,16,128,1024]{3,2,1,0:T(8,128)(2,1)} %refs_3_.3, bf16[2,16,128,1024]{3,2,1,0:T(8,128)(2,1)} %refs_3_.3, bf16[2,16,128,1024]{3,2,1,0:T(8,128)(2,1)} %refs_3_.3, ...), custom_call_target="tpu_custom_call" | custom-call | tf_op jit(solution)/shard_map/pallas_call | solution.py:75
  25.9 0.0 copy-start.8
  25.9 0.0 copy-start.9
  25.9 0.0 copy-start.10
  25.9 47.1 %all-to-all-done.2 = bf16[128,1,1,128,128]{4,3,2,1,0:T(8,128)(2,1)} async-done(((bf16[128,1,1,128,128]{4,3,2,1,0:T(8,128)(2,1)}), bf16[128,1,1,128,128]{4,3,2,1,0:T(8,128)(2,1)}, u32[]{:S(2)}, u32[]{:S(2)}) %all-to-all-start.2) | async-done | bytes 4194336 | tf_op jit(solution)/shard_map/all_to_all | solution.py:225
  73.0 5.5 %all-to-all-start = ((bf16[128,1,1,128,128]{4,3,2,1,0:T(8,128)(2,1)}), bf16[128,1,1,128,128]{4,3,2,1,0:T(8,128)(2,1)}, u32[]{:S(2)}, u32[]{:S(2)}) async-start(bf16[128,1,1,128,128]{4,3,2,1,0:T(8,128)(2,1)} %shard_map.136), calls=%async_computation | async-start | bytes 8388608 | tf_op jit(solution)/shard_map/all_to_all | solution.py:225
  78.5 0.7 compare_select_fusion.1
  79.2 0.0 copy-done.8
  79.2 0.7 gather_fusion
  79.9 0.0 copy-done.9
  79.9 0.2 copy.25.refs_3_
  80.1 0.0 copy-done.10
  80.1 0.2 copy.26.refs_5_
  80.4 0.7 compare_select_fusion
  81.1 0.0 copy-done
  81.1 0.7 gather_fusion.1
  81.8 0.7 fusion.5
  82.5 0.1 add_convert_fusion
  82.6 0.7 compare_bitcast_fusion
  83.3 0.1 and_convert_fusion
  83.5 0.7 fusion.2.pos_ref
  84.2 0.1 multiply_divide_fusion.refs_4_
  84.3 0.0 copy-start.3
  84.3 3.0 %fusion = (bf16[1024,1024]{1,0:T(8,128)(2,1)S(1)}, bf16[1024,1024]{1,0:T(8,128)(2,1)S(1)}) fusion(bf16[1024,1024]{1,0:T(8,128)(2,1)} %param.24, bf16[1024,1024]{1,0:T(8,128)(2,1)} %param.23), kind=kLoop, calls=%fused_computation.4 | loop fusion | flops 8388608 | bytes 8388608 | tf_op jit(solution)/shard_map/convert_element_type | solution.py:247
  87.3 0.0 copy-done.3
  87.3 22.4 %shard_map.139 = bf16[8,1,14,128,128]{4,3,2,1,0:T(8,128)(2,1)} custom-call(s32[14]{0:T(128)S(1)} %fusion.2.pos_ref, bf16[16,8,1,1,128,128]{5,4,3,2,1,0:T(8,128)(2,1)} %bitcast.7.refs_0_.refs_1_, bf16[16,8,1,1,128,128]{5,4,3,2,1,0:T(8,128)(2,1)} %bitcast.7.refs_0_.refs_1_, f32[14,8,128]{2,1,0:T(8,128)S(1)} %scatter.9.refs_2_, f32[1024,1]{1,0:T(8,128)S(1)} %copy.25.refs_3_, ...), custom_call_target="tpu_custom_call" | custom-call | flops 7516192768 | bytes 11534336 | tf_op jit(solution)/shard_map/pallas_call | solution.py:137
  109.7 0.0 copy-start.1
  109.7 1.4 copy-done.1
  111.1 20.3 %all-to-all-done = bf16[128,1,1,128,128]{4,3,2,1,0:T(8,128)(2,1)} async-done(((bf16[128,1,1,128,128]{4,3,2,1,0:T(8,128)(2,1)}), bf16[128,1,1,128,128]{4,3,2,1,0:T(8,128)(2,1)}, u32[]{:S(2)}, u32[]{:S(2)}) %all-to-all-start) | async-done | bytes 4194336 | tf_op jit(solution)/shard_map/all_to_all | solution.py:225
  131.4 5.3 %all-to-all-start.3 = ((bf16[8,1,14,128,128]{4,3,2,1,0:T(8,128)(2,1)}), bf16[8,1,14,128,128]{4,3,2,1,0:T(8,128)(2,1)}, u32[]{:S(2)}, u32[]{:S(2)}) async-start(bf16[8,1,14,128,128]{4,3,2,1,0:T(8,128)(2,1)} %shard_map.139), calls=%async_computation.3 | async-start | bytes 7340032 | tf_op jit(solution)/shard_map/all_to_all | solution.py:252
  136.7 0.0 copy-start.2
  136.7 1.6 copy-done.2
  138.3 0.0 copy-start.4
  138.3 1.0 copy-done.4
  139.3 22.4 %shard_map.137 = bf16[8,1,14,128,128]{4,3,2,1,0:T(8,128)(2,1)} custom-call(s32[14]{0:T(128)S(1)} %fusion.2.pos_ref, bf16[16,8,1,1,128,128]{5,4,3,2,1,0:T(8,128)(2,1)} %bitcast.2.refs_0_.refs_1_, bf16[16,8,1,1,128,128]{5,4,3,2,1,0:T(8,128)(2,1)} %bitcast.2.refs_0_.refs_1_, f32[14,8,128]{2,1,0:T(8,128)S(1)} %scatter.9.refs_2_, f32[1024,1]{1,0:T(8,128)S(1)} %copy.25.refs_3_, ...), custom_call_target="tpu_custom_call" | custom-call | flops 7516192768 | bytes 11534336 | tf_op jit(solution)/shard_map/pallas_call | solution.py:137
  161.8 0.0 copy-start.5
  161.8 0.0 copy-start.6
  161.8 0.0 copy-start.7
  161.8 18.1 %all-to-all-done.3.x_ref = bf16[8,1,14,128,128]{4,3,2,1,0:T(8,128)(2,1)} async-done(((bf16[8,1,14,128,128]{4,3,2,1,0:T(8,128)(2,1)}), bf16[8,1,14,128,128]{4,3,2,1,0:T(8,128)(2,1)}, u32[]{:S(2)}, u32[]{:S(2)}) %all-to-all-start.3) | async-done | bytes 3670048 | tf_op jit(solution)/shard_map/all_to_all | solution.py:252
  179.9 5.3 %all-to-all-start.1 = ((bf16[8,1,14,128,128]{4,3,2,1,0:T(8,128)(2,1)}), bf16[8,1,14,128,128]{4,3,2,1,0:T(8,128)(2,1)}, u32[]{:S(2)}, u32[]{:S(2)}) async-start(bf16[8,1,14,128,128]{4,3,2,1,0:T(8,128)(2,1)} %shard_map.137), calls=%async_computation.1 | async-start | bytes 7340032 | tf_op jit(solution)/shard_map/all_to_all | solution.py:252
  185.2 0.0 copy-done.5
  185.2 0.0 copy-done.6
  185.2 0.0 copy-done.7
  185.3 9.0 %shard_map.140.refs_0_ = bf16[2,16,128,1024]{3,2,1,0:T(8,128)(2,1)} custom-call(s32[128]{0:T(128)S(1)} %copy-done.7, s32[128]{0:T(128)S(1)} %copy-done.6, s32[128]{0:T(128)S(1)} %copy-done.5, bf16[8,1,14,128,128]{4,3,2,1,0:T(8,128)(2,1)} %all-to-all-done.3.x_ref), custom_call_target="tpu_custom_call" | custom-call | tf_op jit(solution)/shard_map/pallas_call | solution.py:185
  194.2 34.2 %all-to-all-done.1.x_ref = bf16[8,1,14,128,128]{4,3,2,1,0:T(8,128)(2,1)} async-done(((bf16[8,1,14,128,128]{4,3,2,1,0:T(8,128)(2,1)}), bf16[8,1,14,128,128]{4,3,2,1,0:T(8,128)(2,1)}, u32[]{:S(2)}, u32[]{:S(2)}) %all-to-all-start.1) | async-done | bytes 3670048 | tf_op jit(solution)/shard_map/all_to_all | solution.py:252
  228.4 9.0 %shard_map.141 = bf16[2,16,128,1024]{3,2,1,0:T(8,128)(2,1)} custom-call(s32[128]{0:T(128)S(1)} %copy-done.7, s32[128]{0:T(128)S(1)} %copy-done.6, s32[128]{0:T(128)S(1)} %copy-done.5, bf16[8,1,14,128,128]{4,3,2,1,0:T(8,128)(2,1)} %all-to-all-done.1.x_ref, bf16[2,16,128,1024]{3,2,1,0:T(8,128)(2,1)} %shard_map.140.refs_0_), custom_call_target="tpu_custom_call", output_to_operand_aliasing={{}: (4, {})} | custom-call | tf_op jit(solution)/shard_map/pallas_call | solution.py:185
  (5 shorter events, 0.1 us)
Async XLA Ops:
  0.0 81.1 %copy-start = (s32[256]{0:T(256)S(1)}, s32[256]{0:T(256)}, u32[]{:S(2)}) copy-start(s32[256]{0:T(256)} %param.25) | copy-start | bytes 3076
  8.3 64.7 %all-to-all-start.2 = ((bf16[128,1,1,128,128]{4,3,2,1,0:T(8,128)(2,1)}), bf16[128,1,1,128,128]{4,3,2,1,0:T(8,128)(2,1)}, u32[]{:S(2)}, u32[]{:S(2)}) async-start(bf16[128,1,1,128,128]{4,3,2,1,0:T(8,128)(2,1)} %shard_map.138), calls=%async_computation.2 | async-start | bytes 8388608 | tf_op jit(solution)/shard_map/all_to_all | solution.py:225
  25.9 53.4 %copy-start.8 = (s32[256]{0:T(256)S(1)}, s32[256]{0:T(256)}, u32[]{:S(2)}) copy-start(s32[256]{0:T(256)} %param.26) | copy-start | bytes 3076
  25.9 54.0 %copy-start.9 = (f32[1024]{0:T(1024)S(1)}, f32[1024]{0:T(1024)}, u32[]{:S(2)}) copy-start(f32[1024]{0:T(1024)} %param.21) | copy-start | bytes 12292
  25.9 54.3 %copy-start.10 = (f32[1024]{0:T(1024)S(1)}, f32[1024]{0:T(1024)}, u32[]{:S(2)}) copy-start(f32[1024]{0:T(1024)} %param.22) | copy-start | bytes 12292
  73.0 58.3 %all-to-all-start = ((bf16[128,1,1,128,128]{4,3,2,1,0:T(8,128)(2,1)}), bf16[128,1,1,128,128]{4,3,2,1,0:T(8,128)(2,1)}, u32[]{:S(2)}, u32[]{:S(2)}) async-start(bf16[128,1,1,128,128]{4,3,2,1,0:T(8,128)(2,1)} %shard_map.136), calls=%async_computation | async-start | bytes 8388608 | tf_op jit(solution)/shard_map/all_to_all | solution.py:225
  84.3 3.0 %copy-start.3 = (f32[1024,1]{1,0:T(8,128)}, f32[1024,1]{1,0:T(8,128)S(1)}, u32[]{:S(2)}) copy-start(f32[1024,1]{1,0:T(8,128)S(1)} %multiply_divide_fusion.refs_4_) | copy-start | bytes 12292
  109.7 1.4 copy-start.1
  131.4 48.5 %all-to-all-start.3 = ((bf16[8,1,14,128,128]{4,3,2,1,0:T(8,128)(2,1)}), bf16[8,1,14,128,128]{4,3,2,1,0:T(8,128)(2,1)}, u32[]{:S(2)}, u32[]{:S(2)}) async-start(bf16[8,1,14,128,128]{4,3,2,1,0:T(8,128)(2,1)} %shard_map.139), calls=%async_computation.3 | async-start | bytes 7340032 | tf_op jit(solution)/shard_map/all_to_all | solution.py:252
  136.7 1.6 copy-start.2
  138.3 1.0 copy-start.4
  161.8 23.5 %copy-start.5 = (s32[128]{0:T(128)S(1)}, s32[128]{0:T(128)}, u32[]{:S(2)}) copy-start(s32[128]{0:T(128)} %constant.127.clone.ok_ref) | copy-start | bytes 1540
  161.8 23.5 %copy-start.6 = (s32[128]{0:T(128)S(1)}, s32[128]{0:T(128)}, u32[]{:S(2)}) copy-start(s32[128]{0:T(128)} %constant.126.clone.j_ref) | copy-start | bytes 1540
  161.8 23.5 %copy-start.7 = (s32[128]{0:T(128)S(1)}, s32[128]{0:T(128)}, u32[]{:S(2)}) copy-start(s32[128]{0:T(128)} %constant.125.clone.r_ref) | copy-start | bytes 1540
  179.9 48.5 %all-to-all-start.1 = ((bf16[8,1,14,128,128]{4,3,2,1,0:T(8,128)(2,1)}), bf16[8,1,14,128,128]{4,3,2,1,0:T(8,128)(2,1)}, u32[]{:S(2)}, u32[]{:S(2)}) async-start(bf16[8,1,14,128,128]{4,3,2,1,0:T(8,128)(2,1)} %shard_map.137), calls=%async_computation.1 | async-start | bytes 7340032 | tf_op jit(solution)/shard_map/all_to_all | solution.py:252

commit v7 on v6

--- a/solution.py
+++ b/solution.py
@@ -32,7 +32,6 @@
     for r in range(nrad):
         lists.append([s for s in range(groups) if (r - shift[s]) % nrad < nwin[s]])
     count = max(len(x) for x in lists)
-    count += count % 2
     pos_tab, win_tab, ok_tab = [], [], []
     for r in range(nrad):
         entries = lists[r] + [lists[r][0]] * (count - len(lists[r]))
@@ -123,7 +122,7 @@
 
 
 def solve(recv, pos, info, kappa, invden, eig, dual_full, basis_full, groups, nrad, per_group,
-          npos=2):
+          npos=1):
     _, _, _, sh, window = recv.shape
     nr = nrad * sh
     count = pos.shape[0]
@@ -163,16 +162,18 @@
 def unpack_kernel(r_ref, j_ref, ok_ref, x_ref, *refs):
     o_ref = refs[-1]
     nrad, window = x_ref.shape[0], x_ref.shape[-1]
+    step = o_ref.shape[1]
     s = pl.program_id(0)
-    for w in range(nrad):
-        k = s * nrad + w
-        blk = x_ref[r_ref[k], 0, j_ref[k]]
-        o_ref[0, 0, :, w * window:(w + 1) * window] = jnp.where(
-            ok_ref[k] > 0, blk, jnp.zeros_like(blk)
-        )
-
-
-def unpack(got, comp, comps, prev, src_r, src_j, src_ok, rows_here):
+    for i in range(step):
+        for w in range(nrad):
+            k = (s * step + i) * nrad + w
+            blk = x_ref[r_ref[k], 0, j_ref[k]]
+            o_ref[0, i, :, w * window:(w + 1) * window] = jnp.where(
+                ok_ref[k] > 0, blk, jnp.zeros_like(blk)
+            )
+
+
+def unpack(got, comp, comps, prev, src_r, src_j, src_ok, rows_here, step=4):
     nrad, _, count, sh, window = got.shape
     shape = (comps, rows_here, sh, nrad * window)
     in_specs = [pl.BlockSpec((nrad, 1, count, sh, window), lambda s, a, b, c: (0, 0, 0, 0, 0))]
@@ -187,10 +188,10 @@
         out_shape=jax.ShapeDtypeStruct(shape, got.dtype),
         grid_spec=pltpu.PrefetchScalarGridSpec(
             num_scalar_prefetch=3,
-            grid=(rows_here,),
+            grid=(rows_here // step,),
             in_specs=in_specs,
             out_specs=pl.BlockSpec(
-                (1, 1, sh, nrad * window), lambda s, a, b, c: (comp, s, 0, 0)
+                (1, step, sh, nrad * window), lambda s, a, b, c: (comp, s, 0, 0)
             ),
         ),
         input_output_aliases=aliases,

time: 238 us -> 228 us (0.958)
  waiting for transfers between devices: 120 us -> 93 us
  Pallas kernels: 73.9 us -> 87.6 us
  local copies, waits for them, and re-layouts: 8.58 us -> 13.7 us
    pallas_call x2, Pallas kernels: 44.8 us -> 67.4 us  [solve(): pl.pallas_call(solve_kernel, out_shape=jax.ShapeDtypeStruct((nrad, 1, cou...]
    all_to_all x2, waiting for transfers between devices: 52.3 us -> 37.1 us  [on_device(): gots.append(lax.all_to_all(back, 'rad', 0, 0, tiled=True))]
    all_to_all x2, waiting for transfers between devices: 67.4 us -> 55.9 us  [on_device(): recvs.append(lax.all_to_all(send, ('mode', 'rad'), 0, 0, tiled=True))]
    pallas_call x2, Pallas kernels: 18 us -> 9.03 us  [unpack(): pl.pallas_call(unpack_kernel, out_shape=jax.ShapeDtypeStruct(shape, got.d...]
    unnamed x22 -> x36, local copies, waits for them, and re-layouts: 4.02 us -> 9.11 us
  transfers between devices with their start and end apart: 4 -> 4, of which waited for: 4 -> 4; matrix products, arithmetic and copies ran while one was open for 4% -> 3% of each run, Pallas kernels for 25% -> 34%
where the time goes in v7:
time: 228 us; the launch traced here: 227 us
  waiting for transfers between devices  93 us (41%)
  Pallas kernels  87.6 us (38%)
  starting transfers between devices  27.2 us (12%)
  local copies, waits for them, and re-layouts  13.7 us (6%)
  other arithmetic  5.66 us (2%)
    pallas_call x2, Pallas kernels, solve(): pl.pallas_call(solve_kernel, out_shape=jax.ShapeDtypeStruct((nrad, 1, cou...  67.4 us
    all_to_all x2, waiting for transfers between devices, on_device(): recvs.append(lax.all_to_all(send, ('mode', 'rad'), 0, 0, tiled=True))  55.9 us
    all_to_all x2, waiting for transfers between devices, on_device(): gots.append(lax.all_to_all(back, 'rad', 0, 0, tiled=True))  37.1 us
    all_to_all x2, starting transfers between devices, on_device(): recvs.append(lax.all_to_all(send, ('mode', 'rad'), 0, 0, tiled=True))  17.4 us
    pallas_call x2, Pallas kernels, pack(): pl.pallas_call(pack_kernel, out_shape=jax.ShapeDtypeStruct((groups * nrad...  11.1 us
    all_to_all x2, starting transfers between devices, on_device(): gots.append(lax.all_to_all(back, 'rad', 0, 0, tiled=True))  9.8 us
    unnamed x36, local copies, waits for them, and re-layouts  9.11 us
    pallas_call x2, Pallas kernels, unpack(): pl.pallas_call(unpack_kernel, out_shape=jax.ShapeDtypeStruct(shape, got.d...  9.03 us
  transfers between devices with their start and end apart: 4, of which 4 were waited for; matrix products, arithmetic and copies ran while one was open for 3% of the time, Pallas kernels for 34%

profile of v7, /device:TPU:1, one launch (start us, length us, event | category | flops | bytes accessed | tf_op | source)
XLA Modules:
  0.0 227.4 jit_solution(16944265693635185592)
XLA Ops:
  0.0 0.0 copy-start
  0.0 0.8 reshape.201
  0.8 1.3 fusion.3.dest_ref
  2.0 0.8 subtract_reduce_fusion.picks_ref
  2.8 5.5 %shard_map.138 = bf16[128,1,1,128,128]{4,3,2,1,0:T(8,128)(2,1)} custom-call(s32[16]{0:T(128)} %subtract_reduce_fusion.picks_ref, s32[8]{0:T(128)} %fusion.3.dest_ref, bf16[2,16,128,1024]{3,2,1,0:T(8,128)(2,1)} %refs_3_.3, bf16[2,16,128,1024]{3,2,1,0:T(8,128)(2,1)} %refs_3_.3, bf16[2,16,128,1024]{3,2,1,0:T(8,128)(2,1)} %refs_3_.3, ...), custom_call_target="tpu_custom_call" | custom-call | tf_op jit(solution)/shard_map/pallas_call | solution.py:74
  8.4 11.9 %all-to-all-start.2 = ((bf16[128,1,1,128,128]{4,3,2,1,0:T(8,128)(2,1)}), bf16[128,1,1,128,128]{4,3,2,1,0:T(8,128)(2,1)}, u32[]{:S(2)}, u32[]{:S(2)}) async-start(bf16[128,1,1,128,128]{4,3,2,1,0:T(8,128)(2,1)} %shard_map.138), calls=%async_computation.2 | async-start | bytes 8388608 | tf_op jit(solution)/shard_map/all_to_all | solution.py:226
  20.3 5.6 %shard_map.136 = bf16[128,1,1,128,128]{4,3,2,1,0:T(8,128)(2,1)} custom-call(s32[16]{0:T(128)} %subtract_reduce_fusion.picks_ref, s32[8]{0:T(128)} %fusion.3.dest_ref, bf16[2,16,128,1024]{3,2,1,0:T(8,128)(2,1)} %refs_3_.3, bf16[2,16,128,1024]{3,2,1,0:T(8,128)(2,1)} %refs_3_.3, bf16[2,16,128,1024]{3,2,1,0:T(8,128)(2,1)} %refs_3_.3, ...), custom_call_target="tpu_custom_call" | custom-call | tf_op jit(solution)/shard_map/pallas_call | solution.py:74
  25.9 0.0 copy-start.14
  25.9 0.0 copy-start.16
  25.9 0.0 copy-start.17
  25.9 0.0 copy-start.15
  25.9 47.1 %all-to-all-done.2 = bf16[128,1,1,128,128]{4,3,2,1,0:T(8,128)(2,1)} async-done(((bf16[128,1,1,128,128]{4,3,2,1,0:T(8,128)(2,1)}), bf16[128,1,1,128,128]{4,3,2,1,0:T(8,128)(2,1)}, u32[]{:S(2)}, u32[]{:S(2)}) %all-to-all-start.2) | async-done | bytes 4194336 | tf_op jit(solution)/shard_map/all_to_all | solution.py:226
  73.0 5.5 %all-to-all-start = ((bf16[128,1,1,128,128]{4,3,2,1,0:T(8,128)(2,1)}), bf16[128,1,1,128,128]{4,3,2,1,0:T(8,128)(2,1)}, u32[]{:S(2)}, u32[]{:S(2)}) async-start(bf16[128,1,1,128,128]{4,3,2,1,0:T(8,128)(2,1)} %shard_map.136), calls=%async_computation | async-start | bytes 8388608 | tf_op jit(solution)/shard_map/all_to_all | solution.py:226
  78.5 0.7 compare_select_fusion.1
  79.3 0.0 copy-done.14
  79.3 0.7 gather_fusion
  79.9 0.0 copy-done.16
  79.9 0.2 copy.25.refs_2_
  80.2 0.0 copy-start.5
  80.2 0.0 copy-done.17
  80.2 0.2 copy.26.refs_4_
  80.4 0.0 copy-start.7
  80.4 0.7 compare_select_fusion
  81.2 0.0 copy-done
  81.2 0.7 gather_fusion.1
  81.8 0.7 fusion.5
  82.5 0.1 add_convert_fusion
  82.7 0.1 compare_convert_fusion
  82.8 0.7 fusion.2.pos_ref
  83.5 0.1 multiply_divide_fusion.refs_3_
  83.6 0.0 copy-done.15
  83.6 0.0 copy-start.9
  83.7 2.4 %fusion = (bf16[1024,1024]{1,0:T(8,128)(2,1)S(1)}, bf16[1024,1024]{1,0:T(8,128)(2,1)S(1)}) fusion(bf16[1024,1024]{1,0:T(8,128)(2,1)S(1)} %copy-done.15, bf16[1024,1024]{1,0:T(8,128)(2,1)} %param.23), kind=kLoop, calls=%fused_computation.4 | loop fusion | flops 8388608 | bytes 8388608 | tf_op jit(solution)/shard_map/convert_element_type | solution.py:248
  86.1 0.0 copy-done.5
  86.1 0.0 copy-done.7
  86.1 0.0 copy-done.9
  86.1 33.8 %shard_map.139 = bf16[8,1,13,128,128]{4,3,2,1,0:T(8,128)(2,1)} custom-call(s32[13]{0:T(128)S(1)} %fusion.2.pos_ref, bf16[16,8,1,1,128,128]{5,4,3,2,1,0:T(8,128)(2,1)} %bitcast.6.refs_0_, f32[13,8,128]{2,1,0:T(8,128)S(1)} %scatter.9.refs_1_, f32[1024,1]{1,0:T(8,128)S(1)} %copy.25.refs_2_, f32[1024,1]{1,0:T(8,128)S(1)} %multiply_divide_fusion.refs_3_, ...), custom_call_target="tpu_custom_call" | custom-call | flops 6979321856 | bytes 11010048 | tf_op jit(solution)/shard_map/pallas_call | solution.py:136
  119.9 0.0 copy-start.1
  119.9 1.4 copy-done.1
  121.2 0.0 copy-start.3
  121.2 1.4 copy-done.3
  122.6 8.8 %all-to-all-done = bf16[128,1,1,128,128]{4,3,2,1,0:T(8,128)(2,1)} async-done(((bf16[128,1,1,128,128]{4,3,2,1,0:T(8,128)(2,1)}), bf16[128,1,1,128,128]{4,3,2,1,0:T(8,128)(2,1)}, u32[]{:S(2)}, u32[]{:S(2)}) %all-to-all-start) | async-done | bytes 4194336 | tf_op jit(solution)/shard_map/all_to_all | solution.py:226
  131.4 4.5 %all-to-all-start.3 = ((bf16[8,1,13,128,128]{4,3,2,1,0:T(8,128)(2,1)}), bf16[8,1,13,128,128]{4,3,2,1,0:T(8,128)(2,1)S(1)}, u32[]{:S(2)}, u32[]{:S(2)}) async-start(bf16[8,1,13,128,128]{4,3,2,1,0:T(8,128)(2,1)} %shard_map.139), calls=%async_computation.3 | async-start | bytes 6815744 | tf_op jit(solution)/shard_map/all_to_all | solution.py:253
  135.9 1.6 copy-done.2
  137.5 0.0 copy-start.4
  137.5 1.6 copy-done.4
  139.1 0.0 copy-start.6
  139.1 1.0 copy-done.6
  140.1 0.0 copy-start.8
  140.1 1.0 copy-done.8
  141.1 0.0 copy-start.10
  141.1 1.0 copy-done.10
  142.2 33.7 %shard_map.137 = bf16[8,1,13,128,128]{4,3,2,1,0:T(8,128)(2,1)} custom-call(s32[13]{0:T(128)S(1)} %fusion.2.pos_ref, bf16[16,8,1,1,128,128]{5,4,3,2,1,0:T(8,128)(2,1)} %bitcast.2.refs_0_, f32[13,8,128]{2,1,0:T(8,128)S(1)} %scatter.9.refs_1_, f32[1024,1]{1,0:T(8,128)S(1)} %copy-done.6, f32[1024,1]{1,0:T(8,128)S(1)} %copy-done.10, f32[1024,1]{1,0:T(8,128)S(1)} %copy-done.8, ...), custom_call_target="tpu_custom_call" | custom-call | flops 6979321856 | bytes 11010048 | tf_op jit(solution)/shard_map/pallas_call | solution.py:136
  175.9 0.0 copy-start.11
  175.9 0.0 copy-start.12
  175.9 0.0 copy-start.13
  175.9 0.3 all-to-all-done.3.x_ref
  176.2 5.3 %all-to-all-start.1 = ((bf16[8,1,13,128,128]{4,3,2,1,0:T(8,128)(2,1)}), bf16[8,1,13,128,128]{4,3,2,1,0:T(8,128)(2,1)}, u32[]{:S(2)}, u32[]{:S(2)}) async-start(bf16[8,1,13,128,128]{4,3,2,1,0:T(8,128)(2,1)} %shard_map.137), calls=%async_computation.1 | async-start | bytes 6815744 | tf_op jit(solution)/shard_map/all_to_all | solution.py:253
  181.5 0.0 copy-done.11
  181.5 0.0 copy-done.12
  181.5 0.0 copy-done.13
  181.5 3.5 %shard_map.140.refs_0_ = bf16[2,16,128,1024]{3,2,1,0:T(8,128)(2,1)} custom-call(s32[128]{0:T(128)S(1)} %copy-done.13, s32[128]{0:T(128)S(1)} %copy-done.12, s32[128]{0:T(128)S(1)} %copy-done.11, bf16[8,1,13,128,128]{4,3,2,1,0:T(8,128)(2,1)S(1)} %all-to-all-done.3.x_ref), custom_call_target="tpu_custom_call" | custom-call | tf_op jit(solution)/shard_map/pallas_call | solution.py:186
  185.0 36.8 %all-to-all-done.1.x_ref = bf16[8,1,13,128,128]{4,3,2,1,0:T(8,128)(2,1)} async-done(((bf16[8,1,13,128,128]{4,3,2,1,0:T(8,128)(2,1)}), bf16[8,1,13,128,128]{4,3,2,1,0:T(8,128)(2,1)}, u32[]{:S(2)}, u32[]{:S(2)}) %all-to-all-start.1) | async-done | bytes 3407904 | tf_op jit(solution)/shard_map/all_to_all | solution.py:253
  221.9 5.5 %shard_map.141 = bf16[2,16,128,1024]{3,2,1,0:T(8,128)(2,1)} custom-call(s32[128]{0:T(128)S(1)} %copy-done.13, s32[128]{0:T(128)S(1)} %copy-done.12, s32[128]{0:T(128)S(1)} %copy-done.11, bf16[8,1,13,128,128]{4,3,2,1,0:T(8,128)(2,1)} %all-to-all-done.1.x_ref, bf16[2,16,128,1024]{3,2,1,0:T(8,128)(2,1)} %shard_map.140.refs_0_), custom_call_target="tpu_custom_call", output_to_operand_aliasing={{}: (4, {})} | custom-call | tf_op jit(solution)/shard_map/pallas_call | solution.py:186
  (6 shorter events, 0.1 us)
Async XLA Ops:
  0.0 81.2 %copy-start = (s32[256]{0:T(256)S(1)}, s32[256]{0:T(256)}, u32[]{:S(2)}) copy-start(s32[256]{0:T(256)} %param.25) | copy-start | bytes 3076
  8.4 64.7 %all-to-all-start.2 = ((bf16[128,1,1,128,128]{4,3,2,1,0:T(8,128)(2,1)}), bf16[128,1,1,128,128]{4,3,2,1,0:T(8,128)(2,1)}, u32[]{:S(2)}, u32[]{:S(2)}) async-start(bf16[128,1,1,128,128]{4,3,2,1,0:T(8,128)(2,1)} %shard_map.138), calls=%async_computation.2 | async-start | bytes 8388608 | tf_op jit(solution)/shard_map/all_to_all | solution.py:226
  25.9 53.4 %copy-start.14 = (s32[256]{0:T(256)S(1)}, s32[256]{0:T(256)}, u32[]{:S(2)}) copy-start(s32[256]{0:T(256)} %param.26) | copy-start | bytes 3076
  25.9 54.0 %copy-start.16 = (f32[1024]{0:T(1024)S(1)}, f32[1024]{0:T(1024)}, u32[]{:S(2)}) copy-start(f32[1024]{0:T(1024)} %param.21) | copy-start | bytes 12292
  25.9 54.3 %copy-start.17 = (f32[1024]{0:T(1024)S(1)}, f32[1024]{0:T(1024)}, u32[]{:S(2)}) copy-start(f32[1024]{0:T(1024)} %param.22) | copy-start | bytes 12292
  25.9 57.7 %copy-start.15 = (bf16[1024,1024]{1,0:T(8,128)(2,1)S(1)}, bf16[1024,1024]{1,0:T(8,128)(2,1)}, u32[]{:S(2)}) copy-start(bf16[1024,1024]{1,0:T(8,128)(2,1)} %param.24) | copy-start | bytes 6291460
  73.0 58.3 %all-to-all-start = ((bf16[128,1,1,128,128]{4,3,2,1,0:T(8,128)(2,1)}), bf16[128,1,1,128,128]{4,3,2,1,0:T(8,128)(2,1)}, u32[]{:S(2)}, u32[]{:S(2)}) async-start(bf16[128,1,1,128,128]{4,3,2,1,0:T(8,128)(2,1)} %shard_map.136), calls=%async_computation | async-start | bytes 8388608 | tf_op jit(solution)/shard_map/all_to_all | solution.py:226
  80.2 5.9 %copy-start.5 = (f32[1024,1]{1,0:T(8,128)}, f32[1024,1]{1,0:T(8,128)S(1)}, u32[]{:S(2)}) copy-start(f32[1024,1]{1,0:T(8,128)S(1)} %copy.25.refs_2_) | copy-start | bytes 12292
  80.4 5.7 %copy-start.7 = (f32[1024,1]{1,0:T(8,128)}, f32[1024,1]{1,0:T(8,128)S(1)}, u32[]{:S(2)}) copy-start(f32[1024,1]{1,0:T(8,128)S(1)} %copy.26.refs_4_) | copy-start | bytes 12292
  83.6 2.5 %copy-start.9 = (f32[1024,1]{1,0:T(8,128)}, f32[1024,1]{1,0:T(8,128)S(1)}, u32[]{:S(2)}) copy-start(f32[1024,1]{1,0:T(8,128)S(1)} %multiply_divide_fusion.refs_3_) | copy-start | bytes 12292
  119.9 1.4 copy-start.1
  121.2 1.4 copy-start.3
  131.4 44.8 %all-to-all-start.3 = ((bf16[8,1,13,128,128]{4,3,2,1,0:T(8,128)(2,1)}), bf16[8,1,13,128,128]{4,3,2,1,0:T(8,128)(2,1)S(1)}, u32[]{:S(2)}, u32[]{:S(2)}) async-start(bf16[8,1,13,128,128]{4,3,2,1,0:T(8,128)(2,1)} %shard_map.139), calls=%async_computation.3 | async-start | bytes 6815744 | tf_op jit(solution)/shard_map/all_to_all | solution.py:253
  135.9 1.6 copy-start.2
  137.5 1.6 copy-start.4
  139.1 1.0 copy-start.6
  140.1 1.0 copy-start.8
  141.1 1.0 copy-start.10
  175.9 5.6 %copy-start.11 = (s32[128]{0:T(128)S(1)}, s32[128]{0:T(128)}, u32[]{:S(2)}) copy-start(s32[128]{0:T(128)} %constant.127.clone.ok_ref) | copy-start | bytes 1540
  175.9 5.6 %copy-start.12 = (s32[128]{0:T(128)S(1)}, s32[128]{0:T(128)}, u32[]{:S(2)}) copy-start(s32[128]{0:T(128)} %constant.126.clone.j_ref) | copy-start | bytes 1540
  175.9 5.6 %copy-start.13 = (s32[128]{0:T(128)S(1)}, s32[128]{0:T(128)}, u32[]{:S(2)}) copy-start(s32[128]{0:T(128)} %constant.125.clone.r_ref) | copy-start | bytes 1540
  176.2 45.7 %all-to-all-start.1 = ((bf16[8,1,13,128,128]{4,3,2,1,0:T(8,128)(2,1)}), bf16[8,1,13,128,128]{4,3,2,1,0:T(8,128)(2,1)}, u32[]{:S(2)}, u32[]{:S(2)}) async-start(bf16[8,1,13,128,128]{4,3,2,1,0:T(8,128)(2,1)} %shard_map.137), calls=%async_computation.1 | async-start | bytes 6815744 | tf_op jit(solution)/shard_map/all_to_all | solution.py:253

commit v8 on v5

--- a/solution.py
+++ b/solution.py
@@ -8,6 +8,7 @@
 from jax.sharding import PartitionSpec as P
 
 PAD = 8
+SPLIT = 4
 
 
 def layout_tables(groups, nrad, rows_here, slots_total, orders_total):
@@ -59,13 +60,13 @@
             o_ref[i * nrad + dest_ref[w]] = x_ref[:, 0:1, :, w * window:(w + 1) * window]
 
 
-def pack(spectra, picks, dests, comp, groups, nrad, per_group, step=4):
+def pack(spectra, picks, dests, groups, nrad, per_group, step=4):
     comps, rows_here, shells_here, slots_total = spectra.shape
     window = slots_total // nrad
     picks_total = groups * per_group
 
     def in_map(i):
-        return lambda q, p, d: (comp, p[q * step + i], 0, 0)
+        return lambda q, p, d: (0, p[q * step + i], 0, 0)
 
     def out_map(q, p, d):
         return (q, 0, 0, 0, 0)
@@ -74,26 +75,27 @@
     return pl.pallas_call(
         pack_kernel,
         out_shape=jax.ShapeDtypeStruct(
-            (groups * nrad, 1, per_group, shells_here, window), spectra.dtype
+            (groups * nrad, comps, per_group, shells_here, window), spectra.dtype
         ),
         grid_spec=pltpu.PrefetchScalarGridSpec(
             num_scalar_prefetch=2,
             grid=(picks_total // step,),
             in_specs=[
-                pl.BlockSpec((1, 1, shells_here, slots_total), in_map(i))
+                pl.BlockSpec((comps, 1, shells_here, slots_total), in_map(i))
                 for i in range(step)
             ],
-            out_specs=pl.BlockSpec((step * nrad, 1, per_group, shells_here, window), out_map),
+            out_specs=pl.BlockSpec((step * nrad, comps, per_group, shells_here, window), out_map),
         ),
     )(picks, dests, *([spectra] * step))
 
 
 def solve_kernel(pos_ref, x_ref, info_ref, kappa_ref, invden_ref, eig_ref, d_ref, b_ref, o_ref,
                  pad_ref):
-    nrad = x_ref.shape[1]
+    nrad, comps = x_ref.shape[1], x_ref.shape[2]
     sh, window = x_ref.shape[4], x_ref.shape[5]
     nr = nrad * sh
-    f = x_ref[0, :, 0, 0].reshape(nr, window).astype(jnp.float32)
+    cols = [x_ref[0, :, c, 0].reshape(nr, window) for c in range(comps)]
+    f = jnp.concatenate(cols, axis=1).astype(jnp.float32)
     width = f.shape[1]
     pad_ref[0:PAD, :] = jnp.zeros((PAD, width), jnp.float32)
     pad_ref[PAD + nr:PAD + nr + PAD, :] = jnp.zeros((PAD, width), jnp.float32)
@@ -103,8 +105,8 @@
     p1 = pad_ref[PAD + 1:PAD + 1 + nr, :]
     p2 = pad_ref[PAD + 2:PAD + 2 + nr, :]
     second = (-m2 + 16.0 * m1 - 30.0 * f + 16.0 * p1 - p2) / 12.0
-    deg = info_ref[0, 0:1, :]
-    live = info_ref[0, 1:2, :] > 0.5
+    deg = jnp.concatenate([info_ref[0, 0:1, :]] * comps, axis=1)
+    live = jnp.concatenate([info_ref[0, 1:2, :]] * comps, axis=1) > 0.5
     lterm = deg * (deg + 1.0)
     damping = lterm * invden_ref[...]
     updated = f + 0.5 * kappa_ref[...] * (second - damping * f)
@@ -114,24 +116,25 @@
     scaled = (projected / divisor).astype(jnp.bfloat16)
     restored = jnp.dot(b_ref[...], scaled, preferred_element_type=jnp.float32)
     solved = jnp.where(live, restored, 0.0).astype(jnp.bfloat16)
-    o_ref[:, 0, 0] = solved.reshape(nrad, sh, window)
+    for c in range(comps):
+        o_ref[:, c, 0] = solved[:, c * window:(c + 1) * window].reshape(nrad, sh, window)
 
 
 def solve(recv, pos, info, kappa, invden, eig, dual_full, basis_full, groups, nrad, per_group):
-    _, _, _, sh, window = recv.shape
+    _, comps, _, sh, window = recv.shape
     nr = nrad * sh
     count = pos.shape[0]
     assert per_group == 1
-    x = recv.reshape(groups, nrad, 1, per_group, sh, window)
-    flops = 2 * 2 * nr * nr * window * count
+    x = recv.reshape(groups, nrad, comps, per_group, sh, window)
+    flops = 2 * 2 * nr * nr * window * comps * count
     return pl.pallas_call(
         solve_kernel,
-        out_shape=jax.ShapeDtypeStruct((nrad, 1, count, sh, window), jnp.bfloat16),
+        out_shape=jax.ShapeDtypeStruct((nrad, comps, count, sh, window), jnp.bfloat16),
         grid_spec=pltpu.PrefetchScalarGridSpec(
             num_scalar_prefetch=1,
             grid=(count,),
             in_specs=[
-                pl.BlockSpec((1, nrad, 1, 1, sh, window), lambda q, p: (p[q], 0, 0, 0, 0, 0)),
+                pl.BlockSpec((1, nrad, comps, 1, sh, window), lambda q, p: (p[q], 0, 0, 0, 0, 0)),
                 pl.BlockSpec((1, 8, window), lambda q, p: (q, 0, 0)),
                 pl.BlockSpec((nr, 1), lambda q, p: (0, 0)),
                 pl.BlockSpec((nr, 1), lambda q, p: (0, 0)),
@@ -139,48 +142,72 @@
                 pl.BlockSpec((nr, nr), lambda q, p: (0, 0)),
                 pl.BlockSpec((nr, nr), lambda q, p: (0, 0)),
             ],
-            out_specs=pl.BlockSpec((nrad, 1, 1, sh, window), lambda q, p: (0, 0, q, 0, 0)),
-            scratch_shapes=[pltpu.VMEM((nr + 2 * PAD, window), jnp.float32)],
+            out_specs=pl.BlockSpec((nrad, comps, 1, sh, window), lambda q, p: (0, 0, q, 0, 0)),
+            scratch_shapes=[pltpu.VMEM((nr + 2 * PAD, comps * window), jnp.float32)],
         ),
         compiler_params=pltpu.CompilerParams(vmem_limit_bytes=48 * 1024 * 1024),
         cost_estimate=pl.CostEstimate(
-            flops=flops, transcendentals=0, bytes_accessed=4 * count * nr * window + 4 * nr * nr
+            flops=flops, transcendentals=0,
+            bytes_accessed=4 * count * comps * nr * window + 4 * nr * nr,
         ),
     )(pos, x, info, kappa, invden, eig, dual_full, basis_full)
 
 
-def unpack_kernel(r_ref, j_ref, ok_ref, *refs):
-    x_refs, o_ref = refs[:-1], refs[-1]
-    nrad, window = x_refs[0].shape[0], x_refs[0].shape[-1]
+def unpack_kernel(first, r_ref, j_ref, ok_ref, *refs):
+    o_ref = refs[-1]
+    x_refs = [r for r in refs[:-1] if len(r.shape) == 5]
+    nrad, comps, window = x_refs[0].shape[0], x_refs[0].shape[1], x_refs[0].shape[-1]
+    split = x_refs[0].shape[2]
+    step = o_ref.shape[1]
     s = pl.program_id(0)
-    for c, x_ref in enumerate(x_refs):
+    for i in range(step):
         for w in range(nrad):
-            k = s * nrad + w
-            blk = x_ref[r_ref[k], 0, j_ref[k]]
-            o_ref[c, 0, :, w * window:(w + 1) * window] = jnp.where(
-                ok_ref[k] > 0, blk, jnp.zeros_like(blk)
-            )
-
-
-def unpack(gots, src_r, src_j, src_ok, rows_here):
-    nrad, _, count, sh, window = gots[0].shape
-    comps = len(gots)
+            k = (first + s * step + i) * nrad + w
+            r, j, ok = r_ref[k], j_ref[k], ok_ref[k]
+            for c in range(comps):
+                if len(x_refs) == 1:
+                    blk = x_ref_pick(x_refs[0], r, c, jnp.minimum(j, split - 1))
+                else:
+                    low = x_ref_pick(x_refs[0], r, c, jnp.minimum(j, split - 1))
+                    high = x_ref_pick(x_refs[1], r, c, jnp.maximum(j - split, 0))
+                    blk = jnp.where(j < split, low, high)
+                o_ref[c, i, :, w * window:(w + 1) * window] = jnp.where(
+                    ok > 0, blk, jnp.zeros_like(blk)
+                )
+
+
+def x_ref_pick(x_ref, r, c, j):
+    return x_ref[r, c, j]
+
+
+def unpack(gots, first, last, prev, src_r, src_j, src_ok, rows_here, step=4):
+    nrad, comps, _, sh, window = gots[0].shape
+    shape = (comps, rows_here, sh, nrad * window)
+    assert first % step == 0 and last % step == 0
+    in_specs = [
+        pl.BlockSpec(g.shape, lambda s, a, b, c: (0, 0, 0, 0, 0)) for g in gots
+    ]
+    args = list(gots)
+    aliases = {}
+    if prev is not None:
+        in_specs.append(pl.BlockSpec(memory_space=pl.ANY))
+        args.append(prev)
+        aliases = {3 + len(gots): 0}
+    base = first // step
     return pl.pallas_call(
-        unpack_kernel,
-        out_shape=jax.ShapeDtypeStruct((comps, rows_here, sh, nrad * window), gots[0].dtype),
+        functools.partial(unpack_kernel, first),
+        out_shape=jax.ShapeDtypeStruct(shape, gots[0].dtype),
         grid_spec=pltpu.PrefetchScalarGridSpec(
             num_scalar_prefetch=3,
-            grid=(rows_here,),
-            in_specs=[
-                pl.BlockSpec((nrad, 1, count, sh, window), lambda s, a, b, c: (0, 0, 0, 0, 0))
-                for _ in gots
-            ],
+            grid=((last - first) // step,),
+            in_specs=in_specs,
             out_specs=pl.BlockSpec(
-                (comps, 1, sh, nrad * window), lambda s, a, b, c: (0, s, 0, 0)
+                (comps, step, sh, nrad * window), lambda s, a, b, c: (0, base + s, 0, 0)
             ),
         ),
+        input_output_aliases=aliases,
         compiler_params=pltpu.CompilerParams(vmem_limit_bytes=48 * 1024 * 1024),
-    )(src_r, src_j, src_ok, *gots)
+    )(src_r, src_j, src_ok, *args)
 
 
 def on_device(
@@ -204,10 +231,8 @@
         - me_mode * rows_here
     )
     dests = jnp.asarray(tab["dest"], jnp.int32)[me_mode]
-    recvs = []
-    for comp in range(comps):
-        send = pack(spectra, picks, dests, comp, groups, nrad, per_group)
-        recvs.append(lax.all_to_all(send, ("mode", "rad"), 0, 0, tiled=True))
+    send = pack(spectra, picks, dests, groups, nrad, per_group)
+    recv = lax.all_to_all(send, ("mode", "rad"), 0, 0, tiled=True)
 
     pos = jnp.asarray(tab["pos"], jnp.int32)[me_rad]
     win = jnp.asarray(tab["win"], jnp.int32)[me_rad]
@@ -230,15 +255,17 @@
     identity = jnp.eye(shells_total, dtype=jnp.float32)
     basis_full = (identity + radial_basis.astype(jnp.float32)).astype(jnp.bfloat16)
     dual_full = (identity + dual_basis.astype(jnp.float32)).astype(jnp.bfloat16)
+    split = SPLIT
     gots = []
-    for recv in recvs:
-        back = solve(recv, pos, info, kappa, invden, eig, dual_full, basis_full, groups, nrad,
-                     per_group)
+    for lo, hi in ((0, split), (split, count)):
+        back = solve(recv, pos[lo:hi], info[lo:hi], kappa, invden, eig, dual_full, basis_full,
+                     groups, nrad, per_group)
         gots.append(lax.all_to_all(back, "rad", 0, 0, tiled=True))
     src_r = jnp.asarray(tab["src_r"], jnp.int32)
     src_j = jnp.asarray(tab["src_j"], jnp.int32)
     src_ok = jnp.asarray(tab["src_ok"], jnp.int32)
-    return unpack(gots, src_r, src_j, src_ok, rows_here)
+    out = unpack(gots[:1], 0, split, None, src_r, src_j, src_ok, rows_here)
+    return unpack(gots, split, rows_here, out, src_r, src_j, src_ok, rows_here)
 
 
 def solution(mesh):

time: 233 us -> 242 us (1.039)
  waiting for transfers between devices: 56.1 us -> 140 us
  blocking collectives: 45.6 us -> 0 us
  Pallas kernels: 89 us -> 59.6 us
  other arithmetic: 5.58 us -> 8.39 us
  local copies, waits for them, and re-layouts: 13.7 us -> 11.2 us
    all_to_all x1 -> x2, waiting for transfers between devices: 0.3 us -> 51.9 us  [on_device(): gots.append(lax.all_to_all(back, 'rad', 0, 0, tiled=True))]
    all_to_all x1 -> x0, blocking collectives: 45.6 us -> none  [on_device(): gots.append(lax.all_to_all(back, 'rad', 0, 0, tiled=True))]
    all_to_all x2 -> x1, waiting for transfers between devices: 55.8 us -> 87.7 us  [on_device(): recv = lax.all_to_all(send, ('mode', 'rad'), 0, 0, tiled=True)]
    pallas_call x3 -> x4, Pallas kernels: 77.8 us -> 51.5 us  [the longest x2 42 us: solve(): pl.pallas_call(solve_kernel, out_shape=jax.ShapeDtypeStruct((nrad, comps,...]
    all_to_all x1 -> x2, starting transfers between devices: 4.49 us -> 9.99 us  [on_device(): gots.append(lax.all_to_all(back, 'rad', 0, 0, tiled=True))]
    all_to_all x2 -> x1, starting transfers between devices: 17.4 us -> 12 us  [on_device(): recv = lax.all_to_all(send, ('mode', 'rad'), 0, 0, tiled=True)]
    pallas_call x2 -> x1, Pallas kernels: 11.2 us -> 8.08 us  [pack(): pl.pallas_call(pack_kernel, out_shape=jax.ShapeDtypeStruct((groups * nrad...]
    unnamed x36 -> x26, local copies, waits for them, and re-layouts: 9.1 us -> 6.61 us
  transfers between devices with their start and end apart: 3 -> 3, of which waited for: 3 -> 2; matrix products, arithmetic and copies ran while one was open for 3% -> 4% of each run, Pallas kernels for 31% -> 13%
where the time goes in v8:
time: 242 us; the launch traced here: 241 us
  waiting for transfers between devices  140 us (58%)
  Pallas kernels  59.6 us (25%)
  starting transfers between devices  21.9 us (9%)
  local copies, waits for them, and re-layouts  11.2 us (5%)
  other arithmetic  8.39 us (3%)
    all_to_all x1, waiting for transfers between devices, on_device(): recv = lax.all_to_all(send, ('mode', 'rad'), 0, 0, tiled=True)  87.7 us
    all_to_all x2, waiting for transfers between devices, on_device(): gots.append(lax.all_to_all(back, 'rad', 0, 0, tiled=True))  51.9 us
    pallas_call x2, Pallas kernels, solve(): pl.pallas_call(solve_kernel, out_shape=jax.ShapeDtypeStruct((nrad, comps,...  42 us
    all_to_all x1, starting transfers between devices, on_device(): recv = lax.all_to_all(send, ('mode', 'rad'), 0, 0, tiled=True)  12 us
    all_to_all x2, starting transfers between devices, on_device(): gots.append(lax.all_to_all(back, 'rad', 0, 0, tiled=True))  9.99 us
    pallas_call x2, Pallas kernels, unpack(): pl.pallas_call(functools.partial(unpack_kernel, first), out_shape=jax.Sha...  9.53 us
    pallas_call x1, Pallas kernels, pack(): pl.pallas_call(pack_kernel, out_shape=jax.ShapeDtypeStruct((groups * nrad...  8.08 us
    unnamed x26, local copies, waits for them, and re-layouts  6.61 us
  transfers between devices with their start and end apart: 3, of which 2 were waited for; matrix products, arithmetic and copies ran while one was open for 4% of the time, Pallas kernels for 13%

profile of v8, /device:TPU:1, one launch (start us, length us, event | category | flops | bytes accessed | tf_op | source)
XLA Modules:
  0.0 240.9 jit_solution(17500250404771990615)
XLA Ops:
  0.0 0.0 copy-start
  0.0 0.8 reshape.203
  0.8 1.2 fusion.2.dest_ref
  2.0 0.8 subtract_reduce_fusion.picks_ref
  2.8 8.1 %shard_map.136 = bf16[128,2,1,128,128]{4,3,2,1,0:T(8,128)(2,1)} custom-call(s32[16]{0:T(128)} %subtract_reduce_fusion.picks_ref, s32[8]{0:T(128)} %fusion.2.dest_ref, bf16[2,16,128,1024]{3,2,1,0:T(8,128)(2,1)} %refs_3_.1, bf16[2,16,128,1024]{3,2,1,0:T(8,128)(2,1)} %refs_3_.1, bf16[2,16,128,1024]{3,2,1,0:T(8,128)(2,1)} %refs_3_.1, ...), custom_call_target="tpu_custom_call" | custom-call | tf_op jit(solution)/shard_map/pallas_call | solution.py:75
  10.8 0.0 copy-start.10
  10.8 0.0 copy-start.11
  10.8 0.0 copy-start.12
  10.8 12.0 %all-to-all-start = ((bf16[128,2,1,128,128]{4,3,2,1,0:T(8,128)(2,1)}), bf16[128,2,1,128,128]{4,3,2,1,0:T(8,128)(2,1)}, u32[]{:S(2)}, u32[]{:S(2)}) async-start(bf16[128,2,1,128,128]{4,3,2,1,0:T(8,128)(2,1)} %shard_map.136), calls=%async_computation | async-start | bytes 16777216 | tf_op jit(solution)/shard_map/all_to_all | solution.py:235
  22.8 0.7 compare_select_fusion.1
  23.5 0.0 copy-done.10
  23.5 0.7 gather_fusion
  24.2 0.7 compare_select_fusion
  24.9 0.0 copy-done
  24.9 0.7 gather_fusion.1
  25.6 0.7 fusion.4
  26.3 0.1 add_convert_fusion
  26.4 0.1 compare_convert_fusion
  26.6 0.0 copy-done.11
  26.6 0.2 copy.25.kappa_ref
  26.8 0.0 copy-done.12
  26.8 0.2 copy.26.eig_ref
  27.0 0.7 constant_dynamic-slice_fusion.2
  27.7 1.0 multiply_divide_fusion.invden_ref
  28.7 4.3 %fusion = (bf16[1024,1024]{1,0:T(8,128)(2,1)S(1)}, bf16[1024,1024]{1,0:T(8,128)(2,1)}) fusion(bf16[1024,1024]{1,0:T(8,128)(2,1)} %param.24, bf16[1024,1024]{1,0:T(8,128)(2,1)} %param.23), kind=kLoop, calls=%fused_computation.4 | loop fusion | flops 8388608 | bytes 8388608 | tf_op jit(solution)/shard_map/convert_element_type | solution.py:257
  33.1 0.0 copy-start.2
  33.1 87.7 %all-to-all-done = bf16[128,2,1,128,128]{4,3,2,1,0:T(8,128)(2,1)} async-done(((bf16[128,2,1,128,128]{4,3,2,1,0:T(8,128)(2,1)}), bf16[128,2,1,128,128]{4,3,2,1,0:T(8,128)(2,1)}, u32[]{:S(2)}, u32[]{:S(2)}) %all-to-all-start) | async-done | bytes 8388640 | tf_op jit(solution)/shard_map/all_to_all | solution.py:235
  120.8 0.0 copy-start.5
  120.8 1.0 copy-done.5
  121.8 13.8 %shard_map.137 = bf16[8,2,4,128,128]{4,3,2,1,0:T(8,128)(2,1)S(1)} custom-call(s32[4]{0:T(128)S(1)} %slice_bitcast_fusion.1.pos_ref, bf16[16,8,2,1,128,128]{5,4,3,2,1,0:T(8,128)(2,1)} %bitcast.2.x_ref, f32[4,8,128]{2,1,0:T(8,128)S(1)} %slice.67.info_ref, f32[1024,1]{1,0:T(8,128)S(1)} %copy.25.kappa_ref, f32[1024,1]{1,0:T(8,128)S(1)} %copy-done.5, ...), custom_call_target="tpu_custom_call" | custom-call | flops 4294967296 | bytes 8388608 | tf_op jit(solution)/shard_map/pallas_call | solution.py:130
  135.6 0.0 copy-done.2
  135.7 0.0 copy-start.1
  135.7 1.3 copy-done.1
  137.0 5.0 %all-to-all-start.1 = ((bf16[8,2,4,128,128]{4,3,2,1,0:T(8,128)(2,1)}), bf16[8,2,4,128,128]{4,3,2,1,0:T(8,128)(2,1)S(1)}, u32[]{:S(2)}, u32[]{:S(2)}) async-start(bf16[8,2,4,128,128]{4,3,2,1,0:T(8,128)(2,1)} %copy-done.1), calls=%async_computation.1 | async-start | bytes 4194304 | tf_op jit(solution)/shard_map/all_to_all | solution.py:263
  142.0 0.1 slice_bitcast_fusion.pos_ref
  142.1 0.0 copy-start.3
  142.1 1.6 copy-done.3
  143.7 0.0 copy-start.4
  143.7 1.6 copy-done.4
  145.3 0.0 copy-start.6
  145.3 1.0 copy-done.6
  146.3 28.2 %shard_map.138 = bf16[8,2,9,128,128]{4,3,2,1,0:T(8,128)(2,1)} custom-call(s32[9]{0:T(128)S(1)} %slice_bitcast_fusion.pos_ref, bf16[16,8,2,1,128,128]{5,4,3,2,1,0:T(8,128)(2,1)} %bitcast.2.x_ref, f32[9,8,128]{2,1,0:T(8,128)S(1)} %slice.68.info_ref, f32[1024,1]{1,0:T(8,128)S(1)} %copy.25.kappa_ref, f32[1024,1]{1,0:T(8,128)S(1)} %copy-done.6, ...), custom_call_target="tpu_custom_call" | custom-call | flops 9663676416 | bytes 13631488 | tf_op jit(solution)/shard_map/pallas_call | solution.py:130
  174.5 0.0 copy-start.7
  174.5 0.0 copy-start.8
  174.5 0.0 copy-start.9
  174.5 0.0 all-to-all-done.1.refs_0_
  174.5 5.0 %all-to-all-start.2 = ((bf16[8,2,9,128,128]{4,3,2,1,0:T(8,128)(2,1)}), bf16[8,2,9,128,128]{4,3,2,1,0:T(8,128)(2,1)}, u32[]{:S(2)}, u32[]{:S(2)}) async-start(bf16[8,2,9,128,128]{4,3,2,1,0:T(8,128)(2,1)} %shard_map.138), calls=%async_computation.2 | async-start | bytes 9437184 | tf_op jit(solution)/shard_map/all_to_all | solution.py:263
  179.4 0.0 copy-done.7
  179.5 0.0 copy-done.8
  179.5 0.0 copy-done.9
  179.5 2.5 %shard_map.139.refs_2_ = bf16[2,16,128,1024]{3,2,1,0:T(8,128)(2,1)} custom-call(s32[128]{0:T(128)S(1)} %copy-done.9, s32[128]{0:T(128)S(1)} %copy-done.8, s32[128]{0:T(128)S(1)} %copy-done.7, bf16[8,2,4,128,128]{4,3,2,1,0:T(8,128)(2,1)S(1)} %all-to-all-done.1.refs_0_), custom_call_target="tpu_custom_call" | custom-call | tf_op jit(solution)/shard_map/pallas_call | solution.py:197
  182.0 51.9 %all-to-all-done.2.refs_1_ = bf16[8,2,9,128,128]{4,3,2,1,0:T(8,128)(2,1)} async-done(((bf16[8,2,9,128,128]{4,3,2,1,0:T(8,128)(2,1)}), bf16[8,2,9,128,128]{4,3,2,1,0:T(8,128)(2,1)}, u32[]{:S(2)}, u32[]{:S(2)}) %all-to-all-start.2) | async-done | bytes 4718624 | tf_op jit(solution)/shard_map/all_to_all | solution.py:263
  233.8 7.0 %shard_map.140 = bf16[2,16,128,1024]{3,2,1,0:T(8,128)(2,1)} custom-call(s32[128]{0:T(128)S(1)} %copy-done.9, s32[128]{0:T(128)S(1)} %copy-done.8, s32[128]{0:T(128)S(1)} %copy-done.7, bf16[8,2,4,128,128]{4,3,2,1,0:T(8,128)(2,1)S(1)} %all-to-all-done.1.refs_0_, bf16[8,2,9,128,128]{4,3,2,1,0:T(8,128)(2,1)} %all-to-all-done.2.refs_1_, ...), custom_call_target="tpu_custom_call", output_to_operand_aliasing={{}: (5, {})} | custom-call | tf_op jit(solution)/shard_map/pallas_call | solution.py:197
  (8 shorter events, 0.1 us)
Async XLA Ops:
  0.0 24.9 %copy-start = (s32[256]{0:T(256)S(1)}, s32[256]{0:T(256)}, u32[]{:S(2)}) copy-start(s32[256]{0:T(256)} %param.25) | copy-start | bytes 3076
  10.8 12.7 %copy-start.10 = (s32[256]{0:T(256)S(1)}, s32[256]{0:T(256)}, u32[]{:S(2)}) copy-start(s32[256]{0:T(256)} %param.26) | copy-start | bytes 3076
  10.8 15.7 %copy-start.11 = (f32[1024]{0:T(1024)S(1)}, f32[1024]{0:T(1024)}, u32[]{:S(2)}) copy-start(f32[1024]{0:T(1024)} %param.21) | copy-start | bytes 12292
  10.8 16.0 %copy-start.12 = (f32[1024]{0:T(1024)S(1)}, f32[1024]{0:T(1024)}, u32[]{:S(2)}) copy-start(f32[1024]{0:T(1024)} %param.22) | copy-start | bytes 12292
  10.8 109.9 %all-to-all-start = ((bf16[128,2,1,128,128]{4,3,2,1,0:T(8,128)(2,1)}), bf16[128,2,1,128,128]{4,3,2,1,0:T(8,128)(2,1)}, u32[]{:S(2)}, u32[]{:S(2)}) async-start(bf16[128,2,1,128,128]{4,3,2,1,0:T(8,128)(2,1)} %shard_map.136), calls=%async_computation | async-start | bytes 16777216 | tf_op jit(solution)/shard_map/all_to_all | solution.py:235
  33.1 102.6 %copy-start.2 = (bf16[1024,1024]{1,0:T(8,128)(2,1)}, bf16[1024,1024]{1,0:T(8,128)(2,1)S(1)}, u32[]{:S(2)}) copy-start(bf16[1024,1024]{1,0:T(8,128)(2,1)S(1)} %get-tuple-element.34.d_ref) | copy-start | bytes 6291460
  120.8 1.0 copy-start.5
  135.7 1.3 copy-start.1
  137.0 37.5 %all-to-all-start.1 = ((bf16[8,2,4,128,128]{4,3,2,1,0:T(8,128)(2,1)}), bf16[8,2,4,128,128]{4,3,2,1,0:T(8,128)(2,1)S(1)}, u32[]{:S(2)}, u32[]{:S(2)}) async-start(bf16[8,2,4,128,128]{4,3,2,1,0:T(8,128)(2,1)} %copy-done.1), calls=%async_computation.1 | async-start | bytes 4194304 | tf_op jit(solution)/shard_map/all_to_all | solution.py:263
  142.1 1.6 copy-start.3
  143.7 1.6 copy-start.4
  145.3 1.0 copy-start.6
  174.5 5.0 %copy-start.7 = (s32[128]{0:T(128)S(1)}, s32[128]{0:T(128)}, u32[]{:S(2)}) copy-start(s32[128]{0:T(128)} %constant.127.clone.ok_ref) | copy-start | bytes 1540
  174.5 5.0 %copy-start.8 = (s32[128]{0:T(128)S(1)}, s32[128]{0:T(128)}, u32[]{:S(2)}) copy-start(s32[128]{0:T(128)} %constant.126.clone.j_ref) | copy-start | bytes 1540
  174.5 5.0 %copy-start.9 = (s32[128]{0:T(128)S(1)}, s32[128]{0:T(128)}, u32[]{:S(2)}) copy-start(s32[128]{0:T(128)} %constant.125.clone.r_ref) | copy-start | bytes 1540
  174.5 59.4 %all-to-all-start.2 = ((bf16[8,2,9,128,128]{4,3,2,1,0:T(8,128)(2,1)}), bf16[8,2,9,128,128]{4,3,2,1,0:T(8,128)(2,1)}, u32[]{:S(2)}, u32[]{:S(2)}) async-start(bf16[8,2,9,128,128]{4,3,2,1,0:T(8,128)(2,1)} %shard_map.138), calls=%async_computation.2 | async-start | bytes 9437184 | tf_op jit(solution)/shard_map/all_to_all | solution.py:263

commit v9 on v7

--- a/solution.py
+++ b/solution.py
@@ -1,6 +1,7 @@
 import functools
 
 import jax
+import numpy as np
 import jax.numpy as jnp
 from jax import lax
 from jax.experimental import pallas as pl
@@ -51,33 +52,34 @@
                 src_ok=src_ok, dest=dest_tab)
 
 
-def pack_kernel(picks_ref, dest_ref, *refs):
+def pack_kernel(picks_total, prefetch_ref, *refs):
     x_refs, o_ref = refs[:-1], refs[-1]
     nrad, window = o_ref.shape[0] // len(x_refs), o_ref.shape[-1]
     for i, x_ref in enumerate(x_refs):
         for w in range(nrad):
-            o_ref[i * nrad + dest_ref[w]] = x_ref[:, 0:1, :, w * window:(w + 1) * window]
-
-
-def pack(spectra, picks, dests, comp, groups, nrad, per_group, step=4):
+            dest = prefetch_ref[picks_total + w]
+            o_ref[i * nrad + dest] = x_ref[:, 0:1, :, w * window:(w + 1) * window]
+
+
+def pack(spectra, prefetch, comp, groups, nrad, per_group, step=4):
     comps, rows_here, shells_here, slots_total = spectra.shape
     window = slots_total // nrad
     picks_total = groups * per_group
 
     def in_map(i):
-        return lambda q, p, d: (comp, p[q * step + i], 0, 0)
-
-    def out_map(q, p, d):
+        return lambda q, p: (comp, p[q * step + i], 0, 0)
+
+    def out_map(q, p):
         return (q, 0, 0, 0, 0)
 
     assert per_group == 1 and picks_total % step == 0
     return pl.pallas_call(
-        pack_kernel,
+        functools.partial(pack_kernel, picks_total),
         out_shape=jax.ShapeDtypeStruct(
             (groups * nrad, 1, per_group, shells_here, window), spectra.dtype
         ),
         grid_spec=pltpu.PrefetchScalarGridSpec(
-            num_scalar_prefetch=2,
+            num_scalar_prefetch=1,
             grid=(picks_total // step,),
             in_specs=[
                 pl.BlockSpec((1, 1, shells_here, slots_total), in_map(i))
@@ -85,7 +87,7 @@
             ],
             out_specs=pl.BlockSpec((step * nrad, 1, per_group, shells_here, window), out_map),
         ),
-    )(picks, dests, *([spectra] * step))
+    )(prefetch, *([spectra] * step))
 
 
 def solve_kernel(pos_ref, *refs):
@@ -213,16 +215,23 @@
     me_rad = lax.axis_index("rad")
     tab = layout_tables(groups, nrad, rows_here, slots_total, orders_total)
 
-    picks = (
-        lax.dynamic_slice_in_dim(
-            order_slot.reshape(groups, groups, per_group), me_mode, 1, 1
-        ).reshape(groups * per_group)
-        - me_mode * rows_here
+    slots = np.arange(groups * per_group)
+    where = (slots // per_group) * rows_here + slots % per_group
+    table = np.concatenate(
+        [np.zeros((groups, groups * per_group), np.int64), np.asarray(tab["dest"])], axis=1
     )
-    dests = jnp.asarray(tab["dest"], jnp.int32)[me_mode]
+    index = np.concatenate([where, np.zeros(nrad, np.int64)]).astype(np.int32)
+    is_pick = np.concatenate([np.ones(groups * per_group), np.zeros(nrad)]).astype(np.int32)
+    looked = jnp.take(order_slot, jnp.asarray(index) + me_mode * per_group)
+    prefetch = jnp.where(
+        jnp.asarray(is_pick) > 0,
+        looked - me_mode * rows_here,
+        jnp.take(jnp.asarray(table.reshape(-1), jnp.int32),
+                 me_mode * table.shape[1] + jnp.arange(table.shape[1], dtype=jnp.int32)),
+    )
     recvs = []
     for comp in range(comps):
-        send = pack(spectra, picks, dests, comp, groups, nrad, per_group)
+        send = pack(spectra, prefetch, comp, groups, nrad, per_group)
         recvs.append(lax.all_to_all(send, ("mode", "rad"), 0, 0, tiled=True))
 
     pos = jnp.asarray(tab["pos"], jnp.int32)[me_rad]

time: 228 us -> 230 us (level)
  transfers between devices with their start and end apart: 4 -> 4, of which waited for: 4 -> 4; matrix products, arithmetic and copies ran while one was open for 3% -> 3% of each run, Pallas kernels for 34% -> 33%
where the time goes in v9:
time: 230 us; the launch traced here: 229 us
  waiting for transfers between devices  93 us (40%)
  Pallas kernels  87.6 us (38%)
  starting transfers between devices  27.2 us (12%)
  local copies, waits for them, and re-layouts  13.7 us (6%)
  other arithmetic  6.8 us (3%)
    pallas_call x2, Pallas kernels, solve(): pl.pallas_call(solve_kernel, out_shape=jax.ShapeDtypeStruct((nrad, 1, cou...  67.4 us
    all_to_all x2, waiting for transfers between devices, on_device(): recvs.append(lax.all_to_all(send, ('mode', 'rad'), 0, 0, tiled=True))  55.9 us
    all_to_all x2, waiting for transfers between devices, on_device(): gots.append(lax.all_to_all(back, 'rad', 0, 0, tiled=True))  37.1 us
    all_to_all x2, starting transfers between devices, on_device(): recvs.append(lax.all_to_all(send, ('mode', 'rad'), 0, 0, tiled=True))  17.4 us
    pallas_call x2, Pallas kernels, pack(): pl.pallas_call(functools.partial(pack_kernel, picks_total), out_shape=jax...  11.1 us
    all_to_all x2, starting transfers between devices, on_device(): gots.append(lax.all_to_all(back, 'rad', 0, 0, tiled=True))  9.82 us
    unnamed x36, local copies, waits for them, and re-layouts  9.1 us
    pallas_call x2, Pallas kernels, unpack(): pl.pallas_call(unpack_kernel, out_shape=jax.ShapeDtypeStruct(shape, got.d...  9.03 us
  transfers between devices with their start and end apart: 4, of which 4 were waited for; matrix products, arithmetic and copies ran while one was open for 3% of the time, Pallas kernels for 33%

profile of v9, /device:TPU:1, one launch (start us, length us, event | category | flops | bytes accessed | tf_op | source)
XLA Modules:
  0.0 228.6 jit_solution(10464707930624364289)
XLA Ops:
  0.0 0.0 copy-start
  0.0 0.7 compare_select_fusion.4
  0.7 1.4 gather_fusion.1
  2.1 0.0 copy-done
  2.1 0.7 gather_fusion
  2.8 1.2 fusion.2.prefetch_ref
  4.0 5.5 %shard_map.156 = bf16[128,1,1,128,128]{4,3,2,1,0:T(8,128)(2,1)} custom-call(s32[24]{0:T(128)} %fusion.2.prefetch_ref, bf16[2,16,128,1024]{3,2,1,0:T(8,128)(2,1)} %refs_3_.3, bf16[2,16,128,1024]{3,2,1,0:T(8,128)(2,1)} %refs_3_.3, bf16[2,16,128,1024]{3,2,1,0:T(8,128)(2,1)} %refs_3_.3, bf16[2,16,128,1024]{3,2,1,0:T(8,128)(2,1)} %refs_3_.3), custom_call_target="tpu_custom_call" | custom-call | tf_op jit(solution)/shard_map/pallas_call | solution.py:76
  9.6 11.9 %all-to-all-start.2 = ((bf16[128,1,1,128,128]{4,3,2,1,0:T(8,128)(2,1)}), bf16[128,1,1,128,128]{4,3,2,1,0:T(8,128)(2,1)}, u32[]{:S(2)}, u32[]{:S(2)}) async-start(bf16[128,1,1,128,128]{4,3,2,1,0:T(8,128)(2,1)} %shard_map.156), calls=%async_computation.2 | async-start | bytes 8388608 | tf_op jit(solution)/shard_map/all_to_all | solution.py:235
  21.5 5.6 %shard_map.154 = bf16[128,1,1,128,128]{4,3,2,1,0:T(8,128)(2,1)} custom-call(s32[24]{0:T(128)} %fusion.2.prefetch_ref, bf16[2,16,128,1024]{3,2,1,0:T(8,128)(2,1)} %refs_3_.3, bf16[2,16,128,1024]{3,2,1,0:T(8,128)(2,1)} %refs_3_.3, bf16[2,16,128,1024]{3,2,1,0:T(8,128)(2,1)} %refs_3_.3, bf16[2,16,128,1024]{3,2,1,0:T(8,128)(2,1)} %refs_3_.3), custom_call_target="tpu_custom_call" | custom-call | tf_op jit(solution)/shard_map/pallas_call | solution.py:76
  27.1 0.0 copy-start.16
  27.1 0.0 copy-start.17
  27.1 0.0 copy-start.14
  27.1 0.0 copy-start.15
  27.1 47.1 %all-to-all-done.2 = bf16[128,1,1,128,128]{4,3,2,1,0:T(8,128)(2,1)} async-done(((bf16[128,1,1,128,128]{4,3,2,1,0:T(8,128)(2,1)}), bf16[128,1,1,128,128]{4,3,2,1,0:T(8,128)(2,1)}, u32[]{:S(2)}, u32[]{:S(2)}) %all-to-all-start.2) | async-done | bytes 4194336 | tf_op jit(solution)/shard_map/all_to_all | solution.py:235
  74.2 5.5 %all-to-all-start = ((bf16[128,1,1,128,128]{4,3,2,1,0:T(8,128)(2,1)}), bf16[128,1,1,128,128]{4,3,2,1,0:T(8,128)(2,1)}, u32[]{:S(2)}, u32[]{:S(2)}) async-start(bf16[128,1,1,128,128]{4,3,2,1,0:T(8,128)(2,1)} %shard_map.154), calls=%async_computation | async-start | bytes 8388608 | tf_op jit(solution)/shard_map/all_to_all | solution.py:235
  79.7 0.7 compare_select_fusion.1
  80.4 0.7 gather_fusion.2
  81.1 0.0 copy-done.16
  81.1 0.2 copy.23.refs_2_
  81.3 0.0 copy-start.5
  81.4 0.0 copy-done.17
  81.4 0.2 copy.24.refs_4_
  81.6 0.0 copy-start.7
  81.6 0.7 compare_select_fusion
  82.3 0.0 copy-done.14
  82.4 0.7 gather_fusion.3
  83.0 0.7 multiply_bitcast_fusion
  83.7 0.1 add_convert_fusion
  83.8 0.1 compare_convert_fusion
  84.0 0.7 dynamic-slice_bitcast_fusion.pos_ref
  84.7 0.1 multiply_divide_fusion.refs_3_
  84.8 0.0 copy-done.15
  84.8 0.0 copy-start.9
  84.8 2.4 %fusion = (bf16[1024,1024]{1,0:T(8,128)(2,1)S(1)}, bf16[1024,1024]{1,0:T(8,128)(2,1)S(1)}) fusion(bf16[1024,1024]{1,0:T(8,128)(2,1)S(1)} %copy-done.15, bf16[1024,1024]{1,0:T(8,128)(2,1)} %param.25), kind=kLoop, calls=%fused_computation.6 | loop fusion | flops 8388608 | bytes 8388608 | tf_op jit(solution)/shard_map/convert_element_type | solution.py:257
  87.3 0.0 copy-done.5
  87.3 0.0 copy-done.7
  87.3 0.0 copy-done.9
  87.3 33.8 %shard_map.157 = bf16[8,1,13,128,128]{4,3,2,1,0:T(8,128)(2,1)} custom-call(s32[13]{0:T(128)S(1)} %dynamic-slice_bitcast_fusion.pos_ref, bf16[16,8,1,1,128,128]{5,4,3,2,1,0:T(8,128)(2,1)} %bitcast.6.refs_0_, f32[13,8,128]{2,1,0:T(8,128)S(1)} %scatter.9.refs_1_, f32[1024,1]{1,0:T(8,128)S(1)} %copy.23.refs_2_, f32[1024,1]{1,0:T(8,128)S(1)} %multiply_divide_fusion.refs_3_, ...), custom_call_target="tpu_custom_call" | custom-call | flops 6979321856 | bytes 11010048 | tf_op jit(solution)/shard_map/pallas_call | solution.py:138
  121.0 0.0 copy-start.1
  121.1 1.3 copy-done.1
  122.4 0.0 copy-start.3
  122.4 1.4 copy-done.3
  123.8 8.8 %all-to-all-done = bf16[128,1,1,128,128]{4,3,2,1,0:T(8,128)(2,1)} async-done(((bf16[128,1,1,128,128]{4,3,2,1,0:T(8,128)(2,1)}), bf16[128,1,1,128,128]{4,3,2,1,0:T(8,128)(2,1)}, u32[]{:S(2)}, u32[]{:S(2)}) %all-to-all-start) | async-done | bytes 4194336 | tf_op jit(solution)/shard_map/all_to_all | solution.py:235
  132.6 4.5 %all-to-all-start.3 = ((bf16[8,1,13,128,128]{4,3,2,1,0:T(8,128)(2,1)}), bf16[8,1,13,128,128]{4,3,2,1,0:T(8,128)(2,1)S(1)}, u32[]{:S(2)}, u32[]{:S(2)}) async-start(bf16[8,1,13,128,128]{4,3,2,1,0:T(8,128)(2,1)} %shard_map.157), calls=%async_computation.3 | async-start | bytes 6815744 | tf_op jit(solution)/shard_map/all_to_all | solution.py:262
  137.1 0.0 copy-start.2
  137.1 1.6 copy-done.2
  138.7 0.0 copy-start.4
  138.7 1.6 copy-done.4
  140.3 0.0 copy-start.6
  140.3 1.0 copy-done.6
  141.3 0.0 copy-start.8
  141.3 1.0 copy-done.8
  142.3 0.0 copy-start.10
  142.3 1.0 copy-done.10
  143.4 33.7 %shard_map.155 = bf16[8,1,13,128,128]{4,3,2,1,0:T(8,128)(2,1)} custom-call(s32[13]{0:T(128)S(1)} %dynamic-slice_bitcast_fusion.pos_ref, bf16[16,8,1,1,128,128]{5,4,3,2,1,0:T(8,128)(2,1)} %bitcast.2.refs_0_, f32[13,8,128]{2,1,0:T(8,128)S(1)} %scatter.9.refs_1_, f32[1024,1]{1,0:T(8,128)S(1)} %copy-done.6, f32[1024,1]{1,0:T(8,128)S(1)} %copy-done.10, ...), custom_call_target="tpu_custom_call" | custom-call | flops 6979321856 | bytes 11010048 | tf_op jit(solution)/shard_map/pallas_call | solution.py:138
  177.1 0.0 copy-start.11
  177.1 0.3 all-to-all-done.3.x_ref
  177.4 5.3 %all-to-all-start.1 = ((bf16[8,1,13,128,128]{4,3,2,1,0:T(8,128)(2,1)}), bf16[8,1,13,128,128]{4,3,2,1,0:T(8,128)(2,1)}, u32[]{:S(2)}, u32[]{:S(2)}) async-start(bf16[8,1,13,128,128]{4,3,2,1,0:T(8,128)(2,1)} %shard_map.155), calls=%async_computation.1 | async-start | bytes 6815744 | tf_op jit(solution)/shard_map/all_to_all | solution.py:262
  182.7 0.0 copy-done.11
  182.7 0.0 copy-done.12
  182.7 0.0 copy-done.13
  182.7 3.5 %shard_map.158.refs_0_ = bf16[2,16,128,1024]{3,2,1,0:T(8,128)(2,1)} custom-call(s32[128]{0:T(128)S(1)} %copy-done.13, s32[128]{0:T(128)S(1)} %copy-done.12, s32[128]{0:T(128)S(1)} %copy-done.11, bf16[8,1,13,128,128]{4,3,2,1,0:T(8,128)(2,1)S(1)} %all-to-all-done.3.x_ref), custom_call_target="tpu_custom_call" | custom-call | tf_op jit(solution)/shard_map/pallas_call | solution.py:188
  186.2 36.8 %all-to-all-done.1.x_ref = bf16[8,1,13,128,128]{4,3,2,1,0:T(8,128)(2,1)} async-done(((bf16[8,1,13,128,128]{4,3,2,1,0:T(8,128)(2,1)}), bf16[8,1,13,128,128]{4,3,2,1,0:T(8,128)(2,1)}, u32[]{:S(2)}, u32[]{:S(2)}) %all-to-all-start.1) | async-done | bytes 3407904 | tf_op jit(solution)/shard_map/all_to_all | solution.py:262
  223.1 5.5 %shard_map.159 = bf16[2,16,128,1024]{3,2,1,0:T(8,128)(2,1)} custom-call(s32[128]{0:T(128)S(1)} %copy-done.13, s32[128]{0:T(128)S(1)} %copy-done.12, s32[128]{0:T(128)S(1)} %copy-done.11, bf16[8,1,13,128,128]{4,3,2,1,0:T(8,128)(2,1)} %all-to-all-done.1.x_ref, bf16[2,16,128,1024]{3,2,1,0:T(8,128)(2,1)} %shard_map.158.refs_0_), custom_call_target="tpu_custom_call", output_to_operand_aliasing={{}: (4, {})} | custom-call | tf_op jit(solution)/shard_map/pallas_call | solution.py:188
  (10 shorter events, 0.1 us)
Async XLA Ops:
  0.0 2.1 copy-start
  9.6 64.7 %all-to-all-start.2 = ((bf16[128,1,1,128,128]{4,3,2,1,0:T(8,128)(2,1)}), bf16[128,1,1,128,128]{4,3,2,1,0:T(8,128)(2,1)}, u32[]{:S(2)}, u32[]{:S(2)}) async-start(bf16[128,1,1,128,128]{4,3,2,1,0:T(8,128)(2,1)} %shard_map.156), calls=%async_computation.2 | async-start | bytes 8388608 | tf_op jit(solution)/shard_map/all_to_all | solution.py:235
  27.1 54.0 %copy-start.16 = (f32[1024]{0:T(1024)S(1)}, f32[1024]{0:T(1024)}, u32[]{:S(2)}) copy-start(f32[1024]{0:T(1024)} %param.23) | copy-start | bytes 12292
  27.1 54.3 %copy-start.17 = (f32[1024]{0:T(1024)S(1)}, f32[1024]{0:T(1024)}, u32[]{:S(2)}) copy-start(f32[1024]{0:T(1024)} %param.24) | copy-start | bytes 12292
  27.1 55.2 %copy-start.14 = (s32[256]{0:T(256)S(1)}, s32[256]{0:T(256)}, u32[]{:S(2)}) copy-start(s32[256]{0:T(256)} %param.27) | copy-start | bytes 3076
  27.1 57.7 %copy-start.15 = (bf16[1024,1024]{1,0:T(8,128)(2,1)S(1)}, bf16[1024,1024]{1,0:T(8,128)(2,1)}, u32[]{:S(2)}) copy-start(bf16[1024,1024]{1,0:T(8,128)(2,1)} %param.26) | copy-start | bytes 6291460
  74.2 58.3 %all-to-all-start = ((bf16[128,1,1,128,128]{4,3,2,1,0:T(8,128)(2,1)}), bf16[128,1,1,128,128]{4,3,2,1,0:T(8,128)(2,1)}, u32[]{:S(2)}, u32[]{:S(2)}) async-start(bf16[128,1,1,128,128]{4,3,2,1,0:T(8,128)(2,1)} %shard_map.154), calls=%async_computation | async-start | bytes 8388608 | tf_op jit(solution)/shard_map/all_to_all | solution.py:235
  81.3 5.9 %copy-start.5 = (f32[1024,1]{1,0:T(8,128)}, f32[1024,1]{1,0:T(8,128)S(1)}, u32[]{:S(2)}) copy-start(f32[1024,1]{1,0:T(8,128)S(1)} %copy.23.refs_2_) | copy-start | bytes 12292
  81.6 5.7 %copy-start.7 = (f32[1024,1]{1,0:T(8,128)}, f32[1024,1]{1,0:T(8,128)S(1)}, u32[]{:S(2)}) copy-start(f32[1024,1]{1,0:T(8,128)S(1)} %copy.24.refs_4_) | copy-start | bytes 12292
  84.8 2.5 %copy-start.9 = (f32[1024,1]{1,0:T(8,128)}, f32[1024,1]{1,0:T(8,128)S(1)}, u32[]{:S(2)}) copy-start(f32[1024,1]{1,0:T(8,128)S(1)} %multiply_divide_fusion.refs_3_) | copy-start | bytes 12292
  121.0 1.4 copy-start.1
  122.4 1.4 copy-start.3
  132.6 44.8 %all-to-all-start.3 = ((bf16[8,1,13,128,128]{4,3,2,1,0:T(8,128)(2,1)}), bf16[8,1,13,128,128]{4,3,2,1,0:T(8,128)(2,1)S(1)}, u32[]{:S(2)}, u32[]{:S(2)}) async-start(bf16[8,1,13,128,128]{4,3,2,1,0:T(8,128)(2,1)} %shard_map.157), calls=%async_computation.3 | async-start | bytes 6815744 | tf_op jit(solution)/shard_map/all_to_all | solution.py:262
  137.1 1.6 copy-start.2
  138.7 1.6 copy-start.4
  140.3 1.0 copy-start.6
  141.3 1.0 copy-start.8
  142.3 1.0 copy-start.10
  177.1 5.6 %copy-start.11 = (s32[128]{0:T(128)S(1)}, s32[128]{0:T(128)}, u32[]{:S(2)}) copy-start(s32[128]{0:T(128)} %constant.165.clone.ok_ref) | copy-start | bytes 1540
  177.1 5.6 %copy-start.12 = (s32[128]{0:T(128)S(1)}, s32[128]{0:T(128)}, u32[]{:S(2)}) copy-start(s32[128]{0:T(128)} %constant.164.clone.j_ref) | copy-start | bytes 1540
  177.1 5.6 %copy-start.13 = (s32[128]{0:T(128)S(1)}, s32[128]{0:T(128)}, u32[]{:S(2)}) copy-start(s32[128]{0:T(128)} %constant.163.clone.r_ref) | copy-start | bytes 1540
  177.4 45.7 %all-to-all-start.1 = ((bf16[8,1,13,128,128]{4,3,2,1,0:T(8,128)(2,1)}), bf16[8,1,13,128,128]{4,3,2,1,0:T(8,128)(2,1)}, u32[]{:S(2)}, u32[]{:S(2)}) async-start(bf16[8,1,13,128,128]{4,3,2,1,0:T(8,128)(2,1)} %shard_map.155), calls=%async_computation.1 | async-start | bytes 6815744 | tf_op jit(solution)/shard_map/all_to_all | solution.py:262

commit v10 on v7

--- a/solution.py
+++ b/solution.py
@@ -51,21 +51,26 @@
                 src_ok=src_ok, dest=dest_tab)
 
 
-def pack_kernel(picks_ref, dest_ref, *refs):
+def pack_kernel(order_ref, shift_ref, *refs):
     x_refs, o_ref = refs[:-1], refs[-1]
     nrad, window = o_ref.shape[0] // len(x_refs), o_ref.shape[-1]
+    turn = shift_ref[lax.axis_index("mode")]
     for i, x_ref in enumerate(x_refs):
         for w in range(nrad):
-            o_ref[i * nrad + dest_ref[w]] = x_ref[:, 0:1, :, w * window:(w + 1) * window]
-
-
-def pack(spectra, picks, dests, comp, groups, nrad, per_group, step=4):
+            o_ref[i * nrad + (w + turn) % nrad] = x_ref[:, 0:1, :, w * window:(w + 1) * window]
+
+
+def pack(spectra, order_slot, shifts, comp, groups, nrad, per_group, step=4):
     comps, rows_here, shells_here, slots_total = spectra.shape
     window = slots_total // nrad
     picks_total = groups * per_group
 
     def in_map(i):
-        return lambda q, p, d: (comp, p[q * step + i], 0, 0)
+        def index(q, p, d):
+            me = lax.axis_index("mode")
+            return (comp, p[(q * step + i) * rows_here + me * per_group] - me * rows_here, 0, 0)
+
+        return index
 
     def out_map(q, p, d):
         return (q, 0, 0, 0, 0)
@@ -85,7 +90,7 @@
             ],
             out_specs=pl.BlockSpec((step * nrad, 1, per_group, shells_here, window), out_map),
         ),
-    )(picks, dests, *([spectra] * step))
+    )(order_slot, shifts, *([spectra] * step))
 
 
 def solve_kernel(pos_ref, *refs):
@@ -213,16 +218,10 @@
     me_rad = lax.axis_index("rad")
     tab = layout_tables(groups, nrad, rows_here, slots_total, orders_total)
 
-    picks = (
-        lax.dynamic_slice_in_dim(
-            order_slot.reshape(groups, groups, per_group), me_mode, 1, 1
-        ).reshape(groups * per_group)
-        - me_mode * rows_here
-    )
-    dests = jnp.asarray(tab["dest"], jnp.int32)[me_mode]
+    shifts = jnp.asarray([row[0] for row in tab["dest"]], jnp.int32)
     recvs = []
     for comp in range(comps):
-        send = pack(spectra, picks, dests, comp, groups, nrad, per_group)
+        send = pack(spectra, order_slot, shifts, comp, groups, nrad, per_group)
         recvs.append(lax.all_to_all(send, ("mode", "rad"), 0, 0, tiled=True))
 
     pos = jnp.asarray(tab["pos"], jnp.int32)[me_rad]

time: 228 us -> 226 us (level)
  no operation moved by 1% of the time
where the time goes in v10:
time: 226 us; the launch traced here: 225 us
  waiting for transfers between devices  93 us (41%)
  Pallas kernels  87.8 us (39%)
  starting transfers between devices  27.2 us (12%)
  local copies, waits for them, and re-layouts  11.6 us (5%)
  other arithmetic  4.88 us (2%)
    pallas_call x2, Pallas kernels, solve(): pl.pallas_call(solve_kernel, out_shape=jax.ShapeDtypeStruct((nrad, 1, cou...  67.4 us
    all_to_all x2, waiting for transfers between devices, on_device(): recvs.append(lax.all_to_all(send, ('mode', 'rad'), 0, 0, tiled=True))  55.8 us
    all_to_all x2, waiting for transfers between devices, on_device(): gots.append(lax.all_to_all(back, 'rad', 0, 0, tiled=True))  37.1 us
    all_to_all x2, starting transfers between devices, on_device(): recvs.append(lax.all_to_all(send, ('mode', 'rad'), 0, 0, tiled=True))  17.4 us
    pallas_call x2, Pallas kernels, pack(): pl.pallas_call(pack_kernel, out_shape=jax.ShapeDtypeStruct((groups * nrad...  11.4 us
    all_to_all x2, starting transfers between devices, on_device(): gots.append(lax.all_to_all(back, 'rad', 0, 0, tiled=True))  9.82 us
    unnamed x36, local copies, waits for them, and re-layouts  9.1 us
    pallas_call x2, Pallas kernels, unpack(): pl.pallas_call(unpack_kernel, out_shape=jax.ShapeDtypeStruct(shape, got.d...  9.03 us
  transfers between devices with their start and end apart: 4, of which 4 were waited for; matrix products, arithmetic and copies ran while one was open for 3% of the time, Pallas kernels for 34%

profile of v10, /device:TPU:1, one launch (start us, length us, event | category | flops | bytes accessed | tf_op | source)
XLA Modules:
  0.0 224.8 jit_solution(12173205309620840020)
XLA Ops:
  0.0 0.0 copy-start
  0.0 5.8 %shard_map.138 = bf16[128,1,1,128,128]{4,3,2,1,0:T(8,128)(2,1)} custom-call(s32[256]{0:T(256)} %order_ref.3, s32[16]{0:T(128)} %constant.121.clone.shift_ref, bf16[2,16,128,1024]{3,2,1,0:T(8,128)(2,1)} %refs_3_.3, bf16[2,16,128,1024]{3,2,1,0:T(8,128)(2,1)} %refs_3_.3, bf16[2,16,128,1024]{3,2,1,0:T(8,128)(2,1)} %refs_3_.3, bf16[2,16,128,1024]{3,2,1,0:T(8,128)(2,1)} %refs_3_.3), custom_call_target="tpu_custom_call" | custom-call | tf_op jit(solution)/shard_map/pallas_call | solution.py:79
  5.8 11.9 %all-to-all-start.2 = ((bf16[128,1,1,128,128]{4,3,2,1,0:T(8,128)(2,1)}), bf16[128,1,1,128,128]{4,3,2,1,0:T(8,128)(2,1)}, u32[]{:S(2)}, u32[]{:S(2)}) async-start(bf16[128,1,1,128,128]{4,3,2,1,0:T(8,128)(2,1)} %shard_map.138), calls=%async_computation.2 | async-start | bytes 8388608 | tf_op jit(solution)/shard_map/all_to_all | solution.py:225
  17.7 5.6 %shard_map.136 = bf16[128,1,1,128,128]{4,3,2,1,0:T(8,128)(2,1)} custom-call(s32[256]{0:T(256)} %order_ref.3, s32[16]{0:T(128)} %constant.121.clone.shift_ref, bf16[2,16,128,1024]{3,2,1,0:T(8,128)(2,1)} %refs_3_.3, bf16[2,16,128,1024]{3,2,1,0:T(8,128)(2,1)} %refs_3_.3, bf16[2,16,128,1024]{3,2,1,0:T(8,128)(2,1)} %refs_3_.3, bf16[2,16,128,1024]{3,2,1,0:T(8,128)(2,1)} %refs_3_.3), custom_call_target="tpu_custom_call" | custom-call | tf_op jit(solution)/shard_map/pallas_call | solution.py:79
  23.3 0.0 copy-start.14
  23.4 0.0 copy-start.16
  23.4 0.0 copy-start.17
  23.4 0.0 copy-start.15
  23.4 47.1 %all-to-all-done.2 = bf16[128,1,1,128,128]{4,3,2,1,0:T(8,128)(2,1)} async-done(((bf16[128,1,1,128,128]{4,3,2,1,0:T(8,128)(2,1)}), bf16[128,1,1,128,128]{4,3,2,1,0:T(8,128)(2,1)}, u32[]{:S(2)}, u32[]{:S(2)}) %all-to-all-start.2) | async-done | bytes 4194336 | tf_op jit(solution)/shard_map/all_to_all | solution.py:225
  70.4 5.5 %all-to-all-start = ((bf16[128,1,1,128,128]{4,3,2,1,0:T(8,128)(2,1)}), bf16[128,1,1,128,128]{4,3,2,1,0:T(8,128)(2,1)}, u32[]{:S(2)}, u32[]{:S(2)}) async-start(bf16[128,1,1,128,128]{4,3,2,1,0:T(8,128)(2,1)} %shard_map.136), calls=%async_computation | async-start | bytes 8388608 | tf_op jit(solution)/shard_map/all_to_all | solution.py:225
  75.9 0.7 compare_select_fusion.1
  76.6 0.0 copy-done.14
  76.6 0.7 gather_fusion
  77.3 0.0 copy-done.16
  77.3 0.2 copy.21.refs_2_
  77.5 0.0 copy-start.5
  77.5 0.0 copy-done.17
  77.6 0.2 copy.22.refs_4_
  77.8 0.0 copy-start.7
  77.8 0.7 compare_select_fusion
  78.5 0.0 copy-done
  78.5 0.7 gather_fusion.1
  79.2 0.7 multiply_bitcast_fusion
  79.9 0.1 add_convert_fusion
  80.0 0.1 compare_convert_fusion
  80.2 0.7 dynamic-slice_bitcast_fusion.pos_ref
  80.9 0.1 multiply_divide_fusion.refs_3_
  81.0 0.0 copy-done.15
  81.0 0.0 copy-start.9
  81.0 2.4 %fusion = (bf16[1024,1024]{1,0:T(8,128)(2,1)S(1)}, bf16[1024,1024]{1,0:T(8,128)(2,1)S(1)}) fusion(bf16[1024,1024]{1,0:T(8,128)(2,1)S(1)} %copy-done.15, bf16[1024,1024]{1,0:T(8,128)(2,1)} %param.23), kind=kLoop, calls=%fused_computation.4 | loop fusion | flops 8388608 | bytes 8388608 | tf_op jit(solution)/shard_map/convert_element_type | solution.py:247
  83.5 0.0 copy-done.5
  83.5 0.0 copy-done.7
  83.5 0.0 copy-done.9
  83.5 33.8 %shard_map.139 = bf16[8,1,13,128,128]{4,3,2,1,0:T(8,128)(2,1)} custom-call(s32[13]{0:T(128)S(1)} %dynamic-slice_bitcast_fusion.pos_ref, bf16[16,8,1,1,128,128]{5,4,3,2,1,0:T(8,128)(2,1)} %bitcast.5.refs_0_, f32[13,8,128]{2,1,0:T(8,128)S(1)} %scatter.9.refs_1_, f32[1024,1]{1,0:T(8,128)S(1)} %copy.21.refs_2_, f32[1024,1]{1,0:T(8,128)S(1)} %multiply_divide_fusion.refs_3_, ...), custom_call_target="tpu_custom_call" | custom-call | flops 6979321856 | bytes 11010048 | tf_op jit(solution)/shard_map/pallas_call | solution.py:141
  117.2 0.0 copy-start.1
  117.2 1.3 copy-done.1
  118.6 0.0 copy-start.3
  118.6 1.4 copy-done.3
  120.0 8.8 %all-to-all-done = bf16[128,1,1,128,128]{4,3,2,1,0:T(8,128)(2,1)} async-done(((bf16[128,1,1,128,128]{4,3,2,1,0:T(8,128)(2,1)}), bf16[128,1,1,128,128]{4,3,2,1,0:T(8,128)(2,1)}, u32[]{:S(2)}, u32[]{:S(2)}) %all-to-all-start) | async-done | bytes 4194336 | tf_op jit(solution)/shard_map/all_to_all | solution.py:225
  128.8 4.5 %all-to-all-start.3 = ((bf16[8,1,13,128,128]{4,3,2,1,0:T(8,128)(2,1)}), bf16[8,1,13,128,128]{4,3,2,1,0:T(8,128)(2,1)S(1)}, u32[]{:S(2)}, u32[]{:S(2)}) async-start(bf16[8,1,13,128,128]{4,3,2,1,0:T(8,128)(2,1)} %shard_map.139), calls=%async_computation.3 | async-start | bytes 6815744 | tf_op jit(solution)/shard_map/all_to_all | solution.py:252
  133.3 0.0 copy-start.2
  133.3 1.6 copy-done.2
  134.8 0.0 copy-start.4
  134.9 1.6 copy-done.4
  136.4 0.0 copy-start.6
  136.4 1.0 copy-done.6
  137.5 0.0 copy-start.8
  137.5 1.0 copy-done.8
  138.5 0.0 copy-start.10
  138.5 1.0 copy-done.10
  139.6 33.7 %shard_map.137 = bf16[8,1,13,128,128]{4,3,2,1,0:T(8,128)(2,1)} custom-call(s32[13]{0:T(128)S(1)} %dynamic-slice_bitcast_fusion.pos_ref, bf16[16,8,1,1,128,128]{5,4,3,2,1,0:T(8,128)(2,1)} %bitcast.1.refs_0_, f32[13,8,128]{2,1,0:T(8,128)S(1)} %scatter.9.refs_1_, f32[1024,1]{1,0:T(8,128)S(1)} %copy-done.6, f32[1024,1]{1,0:T(8,128)S(1)} %copy-done.10, ...), custom_call_target="tpu_custom_call" | custom-call | flops 6979321856 | bytes 11010048 | tf_op jit(solution)/shard_map/pallas_call | solution.py:141
  173.2 0.0 copy-start.11
  173.2 0.0 copy-start.12
  173.2 0.0 copy-start.13
  173.2 0.3 all-to-all-done.3.x_ref
  173.5 5.3 %all-to-all-start.1 = ((bf16[8,1,13,128,128]{4,3,2,1,0:T(8,128)(2,1)}), bf16[8,1,13,128,128]{4,3,2,1,0:T(8,128)(2,1)}, u32[]{:S(2)}, u32[]{:S(2)}) async-start(bf16[8,1,13,128,128]{4,3,2,1,0:T(8,128)(2,1)} %shard_map.137), calls=%async_computation.1 | async-start | bytes 6815744 | tf_op jit(solution)/shard_map/all_to_all | solution.py:252
  178.9 0.0 copy-done.11
  178.9 0.0 copy-done.12
  178.9 0.0 copy-done.13
  178.9 3.5 %shard_map.140.refs_0_ = bf16[2,16,128,1024]{3,2,1,0:T(8,128)(2,1)} custom-call(s32[128]{0:T(128)S(1)} %copy-done.13, s32[128]{0:T(128)S(1)} %copy-done.12, s32[128]{0:T(128)S(1)} %copy-done.11, bf16[8,1,13,128,128]{4,3,2,1,0:T(8,128)(2,1)S(1)} %all-to-all-done.3.x_ref), custom_call_target="tpu_custom_call" | custom-call | tf_op jit(solution)/shard_map/pallas_call | solution.py:191
  182.4 36.8 %all-to-all-done.1.x_ref = bf16[8,1,13,128,128]{4,3,2,1,0:T(8,128)(2,1)} async-done(((bf16[8,1,13,128,128]{4,3,2,1,0:T(8,128)(2,1)}), bf16[8,1,13,128,128]{4,3,2,1,0:T(8,128)(2,1)}, u32[]{:S(2)}, u32[]{:S(2)}) %all-to-all-start.1) | async-done | bytes 3407904 | tf_op jit(solution)/shard_map/all_to_all | solution.py:252
  219.3 5.5 %shard_map.141 = bf16[2,16,128,1024]{3,2,1,0:T(8,128)(2,1)} custom-call(s32[128]{0:T(128)S(1)} %copy-done.13, s32[128]{0:T(128)S(1)} %copy-done.12, s32[128]{0:T(128)S(1)} %copy-done.11, bf16[8,1,13,128,128]{4,3,2,1,0:T(8,128)(2,1)} %all-to-all-done.1.x_ref, bf16[2,16,128,1024]{3,2,1,0:T(8,128)(2,1)} %shard_map.140.refs_0_), custom_call_target="tpu_custom_call", output_to_operand_aliasing={{}: (4, {})} | custom-call | tf_op jit(solution)/shard_map/pallas_call | solution.py:191
  (5 shorter events, 0.1 us)
Async XLA Ops:
  0.0 78.5 %copy-start = (s32[256]{0:T(256)S(1)}, s32[256]{0:T(256)}, u32[]{:S(2)}) copy-start(s32[256]{0:T(256)} %param.25) | copy-start | bytes 3076
  5.8 64.7 %all-to-all-start.2 = ((bf16[128,1,1,128,128]{4,3,2,1,0:T(8,128)(2,1)}), bf16[128,1,1,128,128]{4,3,2,1,0:T(8,128)(2,1)}, u32[]{:S(2)}, u32[]{:S(2)}) async-start(bf16[128,1,1,128,128]{4,3,2,1,0:T(8,128)(2,1)} %shard_map.138), calls=%async_computation.2 | async-start | bytes 8388608 | tf_op jit(solution)/shard_map/all_to_all | solution.py:225
  23.3 53.3 %copy-start.14 = (s32[256]{0:T(256)S(1)}, s32[256]{0:T(256)}, u32[]{:S(2)}) copy-start(s32[256]{0:T(256)} %order_ref.3) | copy-start | bytes 3076
  23.4 54.0 %copy-start.16 = (f32[1024]{0:T(1024)S(1)}, f32[1024]{0:T(1024)}, u32[]{:S(2)}) copy-start(f32[1024]{0:T(1024)} %param.21) | copy-start | bytes 12292
  23.4 54.2 %copy-start.17 = (f32[1024]{0:T(1024)S(1)}, f32[1024]{0:T(1024)}, u32[]{:S(2)}) copy-start(f32[1024]{0:T(1024)} %param.22) | copy-start | bytes 12292
  23.4 57.7 %copy-start.15 = (bf16[1024,1024]{1,0:T(8,128)(2,1)S(1)}, bf16[1024,1024]{1,0:T(8,128)(2,1)}, u32[]{:S(2)}) copy-start(bf16[1024,1024]{1,0:T(8,128)(2,1)} %param.24) | copy-start | bytes 6291460
  70.4 58.3 %all-to-all-start = ((bf16[128,1,1,128,128]{4,3,2,1,0:T(8,128)(2,1)}), bf16[128,1,1,128,128]{4,3,2,1,0:T(8,128)(2,1)}, u32[]{:S(2)}, u32[]{:S(2)}) async-start(bf16[128,1,1,128,128]{4,3,2,1,0:T(8,128)(2,1)} %shard_map.136), calls=%async_computation | async-start | bytes 8388608 | tf_op jit(solution)/shard_map/all_to_all | solution.py:225
  77.5 5.9 %copy-start.5 = (f32[1024,1]{1,0:T(8,128)}, f32[1024,1]{1,0:T(8,128)S(1)}, u32[]{:S(2)}) copy-start(f32[1024,1]{1,0:T(8,128)S(1)} %copy.21.refs_2_) | copy-start | bytes 12292
  77.8 5.7 %copy-start.7 = (f32[1024,1]{1,0:T(8,128)}, f32[1024,1]{1,0:T(8,128)S(1)}, u32[]{:S(2)}) copy-start(f32[1024,1]{1,0:T(8,128)S(1)} %copy.22.refs_4_) | copy-start | bytes 12292
  81.0 2.5 %copy-start.9 = (f32[1024,1]{1,0:T(8,128)}, f32[1024,1]{1,0:T(8,128)S(1)}, u32[]{:S(2)}) copy-start(f32[1024,1]{1,0:T(8,128)S(1)} %multiply_divide_fusion.refs_3_) | copy-start | bytes 12292
  117.2 1.4 copy-start.1
  118.6 1.4 copy-start.3
  128.8 44.8 %all-to-all-start.3 = ((bf16[8,1,13,128,128]{4,3,2,1,0:T(8,128)(2,1)}), bf16[8,1,13,128,128]{4,3,2,1,0:T(8,128)(2,1)S(1)}, u32[]{:S(2)}, u32[]{:S(2)}) async-start(bf16[8,1,13,128,128]{4,3,2,1,0:T(8,128)(2,1)} %shard_map.139), calls=%async_computation.3 | async-start | bytes 6815744 | tf_op jit(solution)/shard_map/all_to_all | solution.py:252
  133.3 1.6 copy-start.2
  134.8 1.6 copy-start.4
  136.4 1.0 copy-start.6
  137.5 1.0 copy-start.8
  138.5 1.0 copy-start.10
  173.2 5.6 %copy-start.11 = (s32[128]{0:T(128)S(1)}, s32[128]{0:T(128)}, u32[]{:S(2)}) copy-start(s32[128]{0:T(128)} %constant.127.clone.ok_ref) | copy-start | bytes 1540
  173.2 5.6 %copy-start.12 = (s32[128]{0:T(128)S(1)}, s32[128]{0:T(128)}, u32[]{:S(2)}) copy-start(s32[128]{0:T(128)} %constant.126.clone.j_ref) | copy-start | bytes 1540
  173.2 5.6 %copy-start.13 = (s32[128]{0:T(128)S(1)}, s32[128]{0:T(128)}, u32[]{:S(2)}) copy-start(s32[128]{0:T(128)} %constant.125.clone.r_ref) | copy-start | bytes 1540
  173.5 45.7 %all-to-all-start.1 = ((bf16[8,1,13,128,128]{4,3,2,1,0:T(8,128)(2,1)}), bf16[8,1,13,128,128]{4,3,2,1,0:T(8,128)(2,1)}, u32[]{:S(2)}, u32[]{:S(2)}) async-start(bf16[8,1,13,128,128]{4,3,2,1,0:T(8,128)(2,1)} %shard_map.137), calls=%async_computation.1 | async-start | bytes 6815744 | tf_op jit(solution)/shard_map/all_to_all | solution.py:252

commit v11 on v10

--- a/solution.py
+++ b/solution.py
@@ -60,7 +60,7 @@
             o_ref[i * nrad + (w + turn) % nrad] = x_ref[:, 0:1, :, w * window:(w + 1) * window]
 
 
-def pack(spectra, order_slot, shifts, comp, groups, nrad, per_group, step=4):
+def pack(spectra, order_slot, shifts, comp, groups, nrad, per_group, step=8):
     comps, rows_here, shells_here, slots_total = spectra.shape
     window = slots_total // nrad
     picks_total = groups * per_group
@@ -178,7 +178,7 @@
             )
 
 
-def unpack(got, comp, comps, prev, src_r, src_j, src_ok, rows_here, step=4):
+def unpack(got, comp, comps, prev, src_r, src_j, src_ok, rows_here, step=8):
     nrad, _, count, sh, window = got.shape
     shape = (comps, rows_here, sh, nrad * window)
     in_specs = [pl.BlockSpec((nrad, 1, count, sh, window), lambda s, a, b, c: (0, 0, 0, 0, 0))]

time: 226 us -> 224 us (level)
  Pallas kernels: 87.8 us -> 85.4 us
where the time goes in v11:
time: 224 us; the launch traced here: 223 us
  waiting for transfers between devices  94.2 us (42%)
  Pallas kernels  85.4 us (38%)
  starting transfers between devices  27.2 us (12%)
  local copies, waits for them, and re-layouts  11.6 us (5%)
  other arithmetic  4.88 us (2%)
    pallas_call x2, Pallas kernels, solve(): pl.pallas_call(solve_kernel, out_shape=jax.ShapeDtypeStruct((nrad, 1, cou...  67.4 us
    all_to_all x2, waiting for transfers between devices, on_device(): recvs.append(lax.all_to_all(send, ('mode', 'rad'), 0, 0, tiled=True))  56.8 us
    all_to_all x2, waiting for transfers between devices, on_device(): gots.append(lax.all_to_all(back, 'rad', 0, 0, tiled=True))  37.4 us
    all_to_all x2, starting transfers between devices, on_device(): recvs.append(lax.all_to_all(send, ('mode', 'rad'), 0, 0, tiled=True))  17.4 us
    all_to_all x2, starting transfers between devices, on_device(): gots.append(lax.all_to_all(back, 'rad', 0, 0, tiled=True))  9.82 us
    pallas_call x2, Pallas kernels, pack(): pl.pallas_call(pack_kernel, out_shape=jax.ShapeDtypeStruct((groups * nrad...  9.47 us
    unnamed x36, local copies, waits for them, and re-layouts  9.11 us
    pallas_call x2, Pallas kernels, unpack(): pl.pallas_call(unpack_kernel, out_shape=jax.ShapeDtypeStruct(shape, got.d...  8.48 us
  transfers between devices with their start and end apart: 4, of which 4 were waited for; matrix products, arithmetic and copies ran while one was open for 3% of the time, Pallas kernels for 34%

profile of v11, /device:TPU:1, one launch (start us, length us, event | category | flops | bytes accessed | tf_op | source)
XLA Modules:
  0.0 223.5 jit_solution(5992421416788025743)
XLA Ops:
  0.0 0.0 copy-start
  0.0 4.8 %shard_map.138 = bf16[128,1,1,128,128]{4,3,2,1,0:T(8,128)(2,1)} custom-call(s32[256]{0:T(256)} %order_ref.3, s32[16]{0:T(128)} %constant.121.clone.shift_ref, bf16[2,16,128,1024]{3,2,1,0:T(8,128)(2,1)} %refs_7_.3, bf16[2,16,128,1024]{3,2,1,0:T(8,128)(2,1)} %refs_7_.3, bf16[2,16,128,1024]{3,2,1,0:T(8,128)(2,1)} %refs_7_.3, ...), custom_call_target="tpu_custom_call" | custom-call | tf_op jit(solution)/shard_map/pallas_call | solution.py:79
  4.8 11.9 %all-to-all-start.2 = ((bf16[128,1,1,128,128]{4,3,2,1,0:T(8,128)(2,1)}), bf16[128,1,1,128,128]{4,3,2,1,0:T(8,128)(2,1)}, u32[]{:S(2)}, u32[]{:S(2)}) async-start(bf16[128,1,1,128,128]{4,3,2,1,0:T(8,128)(2,1)} %shard_map.138), calls=%async_computation.2 | async-start | bytes 8388608 | tf_op jit(solution)/shard_map/all_to_all | solution.py:225
  16.7 4.7 %shard_map.136 = bf16[128,1,1,128,128]{4,3,2,1,0:T(8,128)(2,1)} custom-call(s32[256]{0:T(256)} %order_ref.3, s32[16]{0:T(128)} %constant.121.clone.shift_ref, bf16[2,16,128,1024]{3,2,1,0:T(8,128)(2,1)} %refs_7_.3, bf16[2,16,128,1024]{3,2,1,0:T(8,128)(2,1)} %refs_7_.3, bf16[2,16,128,1024]{3,2,1,0:T(8,128)(2,1)} %refs_7_.3, ...), custom_call_target="tpu_custom_call" | custom-call | tf_op jit(solution)/shard_map/pallas_call | solution.py:79
  21.4 0.0 copy-start.14
  21.4 0.0 copy-start.16
  21.4 0.0 copy-start.17
  21.4 0.0 copy-start.15
  21.5 48.0 %all-to-all-done.2 = bf16[128,1,1,128,128]{4,3,2,1,0:T(8,128)(2,1)} async-done(((bf16[128,1,1,128,128]{4,3,2,1,0:T(8,128)(2,1)}), bf16[128,1,1,128,128]{4,3,2,1,0:T(8,128)(2,1)}, u32[]{:S(2)}, u32[]{:S(2)}) %all-to-all-start.2) | async-done | bytes 4194336 | tf_op jit(solution)/shard_map/all_to_all | solution.py:225
  69.5 5.5 %all-to-all-start = ((bf16[128,1,1,128,128]{4,3,2,1,0:T(8,128)(2,1)}), bf16[128,1,1,128,128]{4,3,2,1,0:T(8,128)(2,1)}, u32[]{:S(2)}, u32[]{:S(2)}) async-start(bf16[128,1,1,128,128]{4,3,2,1,0:T(8,128)(2,1)} %shard_map.136), calls=%async_computation | async-start | bytes 8388608 | tf_op jit(solution)/shard_map/all_to_all | solution.py:225
  74.9 0.7 compare_select_fusion.1
  75.7 0.0 copy-done.14
  75.7 0.7 gather_fusion
  76.3 0.0 copy-done.16
  76.3 0.2 copy.21.refs_2_
  76.6 0.0 copy-start.5
  76.6 0.0 copy-done.17
  76.6 0.2 copy.22.refs_4_
  76.8 0.0 copy-start.7
  76.8 0.7 compare_select_fusion
  77.6 0.0 copy-done
  77.6 0.7 gather_fusion.1
  78.2 0.7 multiply_bitcast_fusion
  78.9 0.1 add_convert_fusion
  79.1 0.1 compare_convert_fusion
  79.2 0.7 dynamic-slice_bitcast_fusion.pos_ref
  79.9 0.1 multiply_divide_fusion.refs_3_
  80.0 0.0 copy-done.15
  80.0 0.0 copy-start.9
  80.1 2.4 %fusion = (bf16[1024,1024]{1,0:T(8,128)(2,1)S(1)}, bf16[1024,1024]{1,0:T(8,128)(2,1)S(1)}) fusion(bf16[1024,1024]{1,0:T(8,128)(2,1)S(1)} %copy-done.15, bf16[1024,1024]{1,0:T(8,128)(2,1)} %param.23), kind=kLoop, calls=%fused_computation.4 | loop fusion | flops 8388608 | bytes 8388608 | tf_op jit(solution)/shard_map/convert_element_type | solution.py:247
  82.5 0.0 copy-done.5
  82.5 0.0 copy-done.7
  82.5 0.0 copy-done.9
  82.5 33.8 %shard_map.139 = bf16[8,1,13,128,128]{4,3,2,1,0:T(8,128)(2,1)} custom-call(s32[13]{0:T(128)S(1)} %dynamic-slice_bitcast_fusion.pos_ref, bf16[16,8,1,1,128,128]{5,4,3,2,1,0:T(8,128)(2,1)} %bitcast.5.refs_0_, f32[13,8,128]{2,1,0:T(8,128)S(1)} %scatter.9.refs_1_, f32[1024,1]{1,0:T(8,128)S(1)} %copy.21.refs_2_, f32[1024,1]{1,0:T(8,128)S(1)} %multiply_divide_fusion.refs_3_, ...), custom_call_target="tpu_custom_call" | custom-call | flops 6979321856 | bytes 11010048 | tf_op jit(solution)/shard_map/pallas_call | solution.py:141
  116.3 0.0 copy-start.1
  116.3 1.3 copy-done.1
  117.6 0.0 copy-start.3
  117.6 1.4 copy-done.3
  119.0 8.8 %all-to-all-done = bf16[128,1,1,128,128]{4,3,2,1,0:T(8,128)(2,1)} async-done(((bf16[128,1,1,128,128]{4,3,2,1,0:T(8,128)(2,1)}), bf16[128,1,1,128,128]{4,3,2,1,0:T(8,128)(2,1)}, u32[]{:S(2)}, u32[]{:S(2)}) %all-to-all-start) | async-done | bytes 4194336 | tf_op jit(solution)/shard_map/all_to_all | solution.py:225
  127.8 4.5 %all-to-all-start.3 = ((bf16[8,1,13,128,128]{4,3,2,1,0:T(8,128)(2,1)}), bf16[8,1,13,128,128]{4,3,2,1,0:T(8,128)(2,1)S(1)}, u32[]{:S(2)}, u32[]{:S(2)}) async-start(bf16[8,1,13,128,128]{4,3,2,1,0:T(8,128)(2,1)} %shard_map.139), calls=%async_computation.3 | async-start | bytes 6815744 | tf_op jit(solution)/shard_map/all_to_all | solution.py:252
  132.3 0.0 copy-start.2
  132.3 1.6 copy-done.2
  133.9 0.0 copy-start.4
  133.9 1.6 copy-done.4
  135.5 0.0 copy-start.6
  135.5 1.0 copy-done.6
  136.5 0.0 copy-start.8
  136.5 1.0 copy-done.8
  137.5 0.0 copy-start.10
  137.5 1.0 copy-done.10
  138.6 33.7 %shard_map.137 = bf16[8,1,13,128,128]{4,3,2,1,0:T(8,128)(2,1)} custom-call(s32[13]{0:T(128)S(1)} %dynamic-slice_bitcast_fusion.pos_ref, bf16[16,8,1,1,128,128]{5,4,3,2,1,0:T(8,128)(2,1)} %bitcast.1.refs_0_, f32[13,8,128]{2,1,0:T(8,128)S(1)} %scatter.9.refs_1_, f32[1024,1]{1,0:T(8,128)S(1)} %copy-done.6, f32[1024,1]{1,0:T(8,128)S(1)} %copy-done.10, ...), custom_call_target="tpu_custom_call" | custom-call | flops 6979321856 | bytes 11010048 | tf_op jit(solution)/shard_map/pallas_call | solution.py:141
  172.3 0.0 copy-start.11
  172.3 0.0 copy-start.12
  172.3 0.0 copy-start.13
  172.3 0.3 all-to-all-done.3.x_ref
  172.6 5.3 %all-to-all-start.1 = ((bf16[8,1,13,128,128]{4,3,2,1,0:T(8,128)(2,1)}), bf16[8,1,13,128,128]{4,3,2,1,0:T(8,128)(2,1)}, u32[]{:S(2)}, u32[]{:S(2)}) async-start(bf16[8,1,13,128,128]{4,3,2,1,0:T(8,128)(2,1)} %shard_map.137), calls=%async_computation.1 | async-start | bytes 6815744 | tf_op jit(solution)/shard_map/all_to_all | solution.py:252
  177.9 0.0 copy-done.11
  177.9 0.0 copy-done.12
  177.9 0.0 copy-done.13
  177.9 3.3 %shard_map.140.refs_0_ = bf16[2,16,128,1024]{3,2,1,0:T(8,128)(2,1)} custom-call(s32[128]{0:T(128)S(1)} %copy-done.13, s32[128]{0:T(128)S(1)} %copy-done.12, s32[128]{0:T(128)S(1)} %copy-done.11, bf16[8,1,13,128,128]{4,3,2,1,0:T(8,128)(2,1)S(1)} %all-to-all-done.3.x_ref), custom_call_target="tpu_custom_call" | custom-call | tf_op jit(solution)/shard_map/pallas_call | solution.py:191
  181.2 37.1 %all-to-all-done.1.x_ref = bf16[8,1,13,128,128]{4,3,2,1,0:T(8,128)(2,1)} async-done(((bf16[8,1,13,128,128]{4,3,2,1,0:T(8,128)(2,1)}), bf16[8,1,13,128,128]{4,3,2,1,0:T(8,128)(2,1)}, u32[]{:S(2)}, u32[]{:S(2)}) %all-to-all-start.1) | async-done | bytes 3407904 | tf_op jit(solution)/shard_map/all_to_all | solution.py:252
  218.3 5.2 %shard_map.141 = bf16[2,16,128,1024]{3,2,1,0:T(8,128)(2,1)} custom-call(s32[128]{0:T(128)S(1)} %copy-done.13, s32[128]{0:T(128)S(1)} %copy-done.12, s32[128]{0:T(128)S(1)} %copy-done.11, bf16[8,1,13,128,128]{4,3,2,1,0:T(8,128)(2,1)} %all-to-all-done.1.x_ref, bf16[2,16,128,1024]{3,2,1,0:T(8,128)(2,1)} %shard_map.140.refs_0_), custom_call_target="tpu_custom_call", output_to_operand_aliasing={{}: (4, {})} | custom-call | tf_op jit(solution)/shard_map/pallas_call | solution.py:191
  (5 shorter events, 0.1 us)
Async XLA Ops:
  0.0 77.6 %copy-start = (s32[256]{0:T(256)S(1)}, s32[256]{0:T(256)}, u32[]{:S(2)}) copy-start(s32[256]{0:T(256)} %param.25) | copy-start | bytes 3076
  4.8 64.7 %all-to-all-start.2 = ((bf16[128,1,1,128,128]{4,3,2,1,0:T(8,128)(2,1)}), bf16[128,1,1,128,128]{4,3,2,1,0:T(8,128)(2,1)}, u32[]{:S(2)}, u32[]{:S(2)}) async-start(bf16[128,1,1,128,128]{4,3,2,1,0:T(8,128)(2,1)} %shard_map.138), calls=%async_computation.2 | async-start | bytes 8388608 | tf_op jit(solution)/shard_map/all_to_all | solution.py:225
  21.4 54.2 %copy-start.14 = (s32[256]{0:T(256)S(1)}, s32[256]{0:T(256)}, u32[]{:S(2)}) copy-start(s32[256]{0:T(256)} %order_ref.3) | copy-start | bytes 3076
  21.4 54.9 %copy-start.16 = (f32[1024]{0:T(1024)S(1)}, f32[1024]{0:T(1024)}, u32[]{:S(2)}) copy-start(f32[1024]{0:T(1024)} %param.21) | copy-start | bytes 12292
  21.4 55.1 %copy-start.17 = (f32[1024]{0:T(1024)S(1)}, f32[1024]{0:T(1024)}, u32[]{:S(2)}) copy-start(f32[1024]{0:T(1024)} %param.22) | copy-start | bytes 12292
  21.4 58.6 %copy-start.15 = (bf16[1024,1024]{1,0:T(8,128)(2,1)S(1)}, bf16[1024,1024]{1,0:T(8,128)(2,1)}, u32[]{:S(2)}) copy-start(bf16[1024,1024]{1,0:T(8,128)(2,1)} %param.24) | copy-start | bytes 6291460
  69.5 58.3 %all-to-all-start = ((bf16[128,1,1,128,128]{4,3,2,1,0:T(8,128)(2,1)}), bf16[128,1,1,128,128]{4,3,2,1,0:T(8,128)(2,1)}, u32[]{:S(2)}, u32[]{:S(2)}) async-start(bf16[128,1,1,128,128]{4,3,2,1,0:T(8,128)(2,1)} %shard_map.136), calls=%async_computation | async-start | bytes 8388608 | tf_op jit(solution)/shard_map/all_to_all | solution.py:225
  76.6 5.9 %copy-start.5 = (f32[1024,1]{1,0:T(8,128)}, f32[1024,1]{1,0:T(8,128)S(1)}, u32[]{:S(2)}) copy-start(f32[1024,1]{1,0:T(8,128)S(1)} %copy.21.refs_2_) | copy-start | bytes 12292
  76.8 5.7 %copy-start.7 = (f32[1024,1]{1,0:T(8,128)}, f32[1024,1]{1,0:T(8,128)S(1)}, u32[]{:S(2)}) copy-start(f32[1024,1]{1,0:T(8,128)S(1)} %copy.22.refs_4_) | copy-start | bytes 12292
  80.0 2.5 %copy-start.9 = (f32[1024,1]{1,0:T(8,128)}, f32[1024,1]{1,0:T(8,128)S(1)}, u32[]{:S(2)}) copy-start(f32[1024,1]{1,0:T(8,128)S(1)} %multiply_divide_fusion.refs_3_) | copy-start | bytes 12292
  116.3 1.4 copy-start.1
  117.6 1.4 copy-start.3
  127.8 44.8 %all-to-all-start.3 = ((bf16[8,1,13,128,128]{4,3,2,1,0:T(8,128)(2,1)}), bf16[8,1,13,128,128]{4,3,2,1,0:T(8,128)(2,1)S(1)}, u32[]{:S(2)}, u32[]{:S(2)}) async-start(bf16[8,1,13,128,128]{4,3,2,1,0:T(8,128)(2,1)} %shard_map.139), calls=%async_computation.3 | async-start | bytes 6815744 | tf_op jit(solution)/shard_map/all_to_all | solution.py:252
  132.3 1.6 copy-start.2
  133.9 1.6 copy-start.4
  135.5 1.0 copy-start.6
  136.5 1.0 copy-start.8
  137.5 1.0 copy-start.10
  172.3 5.6 %copy-start.11 = (s32[128]{0:T(128)S(1)}, s32[128]{0:T(128)}, u32[]{:S(2)}) copy-start(s32[128]{0:T(128)} %constant.127.clone.ok_ref) | copy-start | bytes 1540
  172.3 5.6 %copy-start.12 = (s32[128]{0:T(128)S(1)}, s32[128]{0:T(128)}, u32[]{:S(2)}) copy-start(s32[128]{0:T(128)} %constant.126.clone.j_ref) | copy-start | bytes 1540
  172.3 5.6 %copy-start.13 = (s32[128]{0:T(128)S(1)}, s32[128]{0:T(128)}, u32[]{:S(2)}) copy-start(s32[128]{0:T(128)} %constant.125.clone.r_ref) | copy-start | bytes 1540
  172.6 45.7 %all-to-all-start.1 = ((bf16[8,1,13,128,128]{4,3,2,1,0:T(8,128)(2,1)}), bf16[8,1,13,128,128]{4,3,2,1,0:T(8,128)(2,1)}, u32[]{:S(2)}, u32[]{:S(2)}) async-start(bf16[8,1,13,128,128]{4,3,2,1,0:T(8,128)(2,1)} %shard_map.137), calls=%async_computation.1 | async-start | bytes 6815744 | tf_op jit(solution)/shard_map/all_to_all | solution.py:252

commit v12 on v11

--- a/solution.py
+++ b/solution.py
@@ -60,7 +60,7 @@
             o_ref[i * nrad + (w + turn) % nrad] = x_ref[:, 0:1, :, w * window:(w + 1) * window]
 
 
-def pack(spectra, order_slot, shifts, comp, groups, nrad, per_group, step=8):
+def pack(spectra, order_slot, shifts, comp, groups, nrad, per_group, step=16):
     comps, rows_here, shells_here, slots_total = spectra.shape
     window = slots_total // nrad
     picks_total = groups * per_group
@@ -178,7 +178,7 @@
             )
 
 
-def unpack(got, comp, comps, prev, src_r, src_j, src_ok, rows_here, step=8):
+def unpack(got, comp, comps, prev, src_r, src_j, src_ok, rows_here, step=16):
     nrad, _, count, sh, window = got.shape
     shape = (comps, rows_here, sh, nrad * window)
     in_specs = [pl.BlockSpec((nrad, 1, count, sh, window), lambda s, a, b, c: (0, 0, 0, 0, 0))]

time: 224 us -> 226 us (level)
  Pallas kernels: 85.4 us -> 88.3 us
where the time goes in v12:
time: 226 us; the launch traced here: 225 us
  waiting for transfers between devices  92.7 us (41%)
  Pallas kernels  88.3 us (39%)
  starting transfers between devices  27.2 us (12%)
  local copies, waits for them, and re-layouts  11.6 us (5%)
  other arithmetic  4.88 us (2%)
    pallas_call x2, Pallas kernels, solve(): pl.pallas_call(solve_kernel, out_shape=jax.ShapeDtypeStruct((nrad, 1, cou...  67.4 us
    all_to_all x2, waiting for transfers between devices, on_device(): recvs.append(lax.all_to_all(send, ('mode', 'rad'), 0, 0, tiled=True))  55.9 us
    all_to_all x2, waiting for transfers between devices, on_device(): gots.append(lax.all_to_all(back, 'rad', 0, 0, tiled=True))  36.8 us
    all_to_all x2, starting transfers between devices, on_device(): recvs.append(lax.all_to_all(send, ('mode', 'rad'), 0, 0, tiled=True))  17.4 us
    pallas_call x2, Pallas kernels, pack(): pl.pallas_call(pack_kernel, out_shape=jax.ShapeDtypeStruct((groups * nrad...  11.3 us
    all_to_all x2, starting transfers between devices, on_device(): gots.append(lax.all_to_all(back, 'rad', 0, 0, tiled=True))  9.82 us
    pallas_call x2, Pallas kernels, unpack(): pl.pallas_call(unpack_kernel, out_shape=jax.ShapeDtypeStruct(shape, got.d...  9.65 us
    unnamed x36, local copies, waits for them, and re-layouts  9.11 us
  transfers between devices with their start and end apart: 4, of which 4 were waited for; matrix products, arithmetic and copies ran while one was open for 3% of the time, Pallas kernels for 34%

profile of v12, /device:TPU:1, one launch (start us, length us, event | category | flops | bytes accessed | tf_op | source)
XLA Modules:
  0.0 225.0 jit_solution(13708966398806305651)
XLA Ops:
  0.0 0.0 copy-start
  0.0 5.6 %shard_map.138 = bf16[128,1,1,128,128]{4,3,2,1,0:T(8,128)(2,1)} custom-call(s32[256]{0:T(256)} %order_ref.3, s32[16]{0:T(128)} %constant.121.clone.shift_ref, bf16[2,16,128,1024]{3,2,1,0:T(8,128)(2,1)} %refs_15_.3, bf16[2,16,128,1024]{3,2,1,0:T(8,128)(2,1)} %refs_15_.3, bf16[2,16,128,1024]{3,2,1,0:T(8,128)(2,1)} %refs_15_.3, ...), custom_call_target="tpu_custom_call" | custom-call | tf_op jit(solution)/shard_map/pallas_call | solution.py:79
  5.7 11.9 %all-to-all-start.2 = ((bf16[128,1,1,128,128]{4,3,2,1,0:T(8,128)(2,1)}), bf16[128,1,1,128,128]{4,3,2,1,0:T(8,128)(2,1)}, u32[]{:S(2)}, u32[]{:S(2)}) async-start(bf16[128,1,1,128,128]{4,3,2,1,0:T(8,128)(2,1)} %shard_map.138), calls=%async_computation.2 | async-start | bytes 8388608 | tf_op jit(solution)/shard_map/all_to_all | solution.py:225
  17.6 5.6 %shard_map.136 = bf16[128,1,1,128,128]{4,3,2,1,0:T(8,128)(2,1)} custom-call(s32[256]{0:T(256)} %order_ref.3, s32[16]{0:T(128)} %constant.121.clone.shift_ref, bf16[2,16,128,1024]{3,2,1,0:T(8,128)(2,1)} %refs_15_.3, bf16[2,16,128,1024]{3,2,1,0:T(8,128)(2,1)} %refs_15_.3, bf16[2,16,128,1024]{3,2,1,0:T(8,128)(2,1)} %refs_15_.3, ...), custom_call_target="tpu_custom_call" | custom-call | tf_op jit(solution)/shard_map/pallas_call | solution.py:79
  23.2 0.0 copy-start.14
  23.2 0.0 copy-start.16
  23.2 0.0 copy-start.17
  23.2 0.0 copy-start.15
  23.2 47.1 %all-to-all-done.2 = bf16[128,1,1,128,128]{4,3,2,1,0:T(8,128)(2,1)} async-done(((bf16[128,1,1,128,128]{4,3,2,1,0:T(8,128)(2,1)}), bf16[128,1,1,128,128]{4,3,2,1,0:T(8,128)(2,1)}, u32[]{:S(2)}, u32[]{:S(2)}) %all-to-all-start.2) | async-done | bytes 4194336 | tf_op jit(solution)/shard_map/all_to_all | solution.py:225
  70.3 5.5 %all-to-all-start = ((bf16[128,1,1,128,128]{4,3,2,1,0:T(8,128)(2,1)}), bf16[128,1,1,128,128]{4,3,2,1,0:T(8,128)(2,1)}, u32[]{:S(2)}, u32[]{:S(2)}) async-start(bf16[128,1,1,128,128]{4,3,2,1,0:T(8,128)(2,1)} %shard_map.136), calls=%async_computation | async-start | bytes 8388608 | tf_op jit(solution)/shard_map/all_to_all | solution.py:225
  75.8 0.7 compare_select_fusion.1
  76.5 0.0 copy-done.14
  76.5 0.7 gather_fusion
  77.2 0.0 copy-done.16
  77.2 0.2 copy.21.refs_2_
  77.4 0.0 copy-start.5
  77.4 0.0 copy-done.17
  77.5 0.2 copy.22.refs_4_
  77.7 0.0 copy-start.7
  77.7 0.7 compare_select_fusion
  78.4 0.0 copy-done
  78.4 0.7 gather_fusion.1
  79.1 0.7 multiply_bitcast_fusion
  79.8 0.1 add_convert_fusion
  79.9 0.1 compare_convert_fusion
  80.1 0.7 dynamic-slice_bitcast_fusion.pos_ref
  80.8 0.1 multiply_divide_fusion.refs_3_
  80.9 0.0 copy-done.15
  80.9 0.0 copy-start.9
  80.9 2.4 %fusion = (bf16[1024,1024]{1,0:T(8,128)(2,1)S(1)}, bf16[1024,1024]{1,0:T(8,128)(2,1)S(1)}) fusion(bf16[1024,1024]{1,0:T(8,128)(2,1)S(1)} %copy-done.15, bf16[1024,1024]{1,0:T(8,128)(2,1)} %param.23), kind=kLoop, calls=%fused_computation.4 | loop fusion | flops 8388608 | bytes 8388608 | tf_op jit(solution)/shard_map/convert_element_type | solution.py:247
  83.4 0.0 copy-done.5
  83.4 0.0 copy-done.7
  83.4 0.0 copy-done.9
  83.4 33.8 %shard_map.139 = bf16[8,1,13,128,128]{4,3,2,1,0:T(8,128)(2,1)} custom-call(s32[13]{0:T(128)S(1)} %dynamic-slice_bitcast_fusion.pos_ref, bf16[16,8,1,1,128,128]{5,4,3,2,1,0:T(8,128)(2,1)} %bitcast.5.refs_0_, f32[13,8,128]{2,1,0:T(8,128)S(1)} %scatter.9.refs_1_, f32[1024,1]{1,0:T(8,128)S(1)} %copy.21.refs_2_, f32[1024,1]{1,0:T(8,128)S(1)} %multiply_divide_fusion.refs_3_, ...), custom_call_target="tpu_custom_call" | custom-call | flops 6979321856 | bytes 11010048 | tf_op jit(solution)/shard_map/pallas_call | solution.py:141
  117.1 0.0 copy-start.1
  117.1 1.3 copy-done.1
  118.5 0.0 copy-start.3
  118.5 1.4 copy-done.3
  119.9 8.8 %all-to-all-done = bf16[128,1,1,128,128]{4,3,2,1,0:T(8,128)(2,1)} async-done(((bf16[128,1,1,128,128]{4,3,2,1,0:T(8,128)(2,1)}), bf16[128,1,1,128,128]{4,3,2,1,0:T(8,128)(2,1)}, u32[]{:S(2)}, u32[]{:S(2)}) %all-to-all-start) | async-done | bytes 4194336 | tf_op jit(solution)/shard_map/all_to_all | solution.py:225
  128.7 4.5 %all-to-all-start.3 = ((bf16[8,1,13,128,128]{4,3,2,1,0:T(8,128)(2,1)}), bf16[8,1,13,128,128]{4,3,2,1,0:T(8,128)(2,1)S(1)}, u32[]{:S(2)}, u32[]{:S(2)}) async-start(bf16[8,1,13,128,128]{4,3,2,1,0:T(8,128)(2,1)} %shard_map.139), calls=%async_computation.3 | async-start | bytes 6815744 | tf_op jit(solution)/shard_map/all_to_all | solution.py:252
  133.2 0.0 copy-start.2
  133.2 1.6 copy-done.2
  134.7 0.0 copy-start.4
  134.7 1.6 copy-done.4
  136.3 0.0 copy-start.6
  136.3 1.0 copy-done.6
  137.4 0.0 copy-start.8
  137.4 1.0 copy-done.8
  138.4 0.0 copy-start.10
  138.4 1.0 copy-done.10
  139.5 33.7 %shard_map.137 = bf16[8,1,13,128,128]{4,3,2,1,0:T(8,128)(2,1)} custom-call(s32[13]{0:T(128)S(1)} %dynamic-slice_bitcast_fusion.pos_ref, bf16[16,8,1,1,128,128]{5,4,3,2,1,0:T(8,128)(2,1)} %bitcast.1.refs_0_, f32[13,8,128]{2,1,0:T(8,128)S(1)} %scatter.9.refs_1_, f32[1024,1]{1,0:T(8,128)S(1)} %copy-done.6, f32[1024,1]{1,0:T(8,128)S(1)} %copy-done.10, ...), custom_call_target="tpu_custom_call" | custom-call | flops 6979321856 | bytes 11010048 | tf_op jit(solution)/shard_map/pallas_call | solution.py:141
  173.1 0.0 copy-start.11
  173.1 0.0 copy-start.12
  173.1 0.0 copy-start.13
  173.1 0.3 all-to-all-done.3.x_ref
  173.4 5.3 %all-to-all-start.1 = ((bf16[8,1,13,128,128]{4,3,2,1,0:T(8,128)(2,1)}), bf16[8,1,13,128,128]{4,3,2,1,0:T(8,128)(2,1)}, u32[]{:S(2)}, u32[]{:S(2)}) async-start(bf16[8,1,13,128,128]{4,3,2,1,0:T(8,128)(2,1)} %shard_map.137), calls=%async_computation.1 | async-start | bytes 6815744 | tf_op jit(solution)/shard_map/all_to_all | solution.py:252
  178.8 0.0 copy-done.11
  178.8 0.0 copy-done.12
  178.8 0.0 copy-done.13
  178.8 3.8 %shard_map.140.refs_0_ = bf16[2,16,128,1024]{3,2,1,0:T(8,128)(2,1)} custom-call(s32[128]{0:T(128)S(1)} %copy-done.13, s32[128]{0:T(128)S(1)} %copy-done.12, s32[128]{0:T(128)S(1)} %copy-done.11, bf16[8,1,13,128,128]{4,3,2,1,0:T(8,128)(2,1)S(1)} %all-to-all-done.3.x_ref), custom_call_target="tpu_custom_call" | custom-call | tf_op jit(solution)/shard_map/pallas_call | solution.py:191
  182.6 36.5 %all-to-all-done.1.x_ref = bf16[8,1,13,128,128]{4,3,2,1,0:T(8,128)(2,1)} async-done(((bf16[8,1,13,128,128]{4,3,2,1,0:T(8,128)(2,1)}), bf16[8,1,13,128,128]{4,3,2,1,0:T(8,128)(2,1)}, u32[]{:S(2)}, u32[]{:S(2)}) %all-to-all-start.1) | async-done | bytes 3407904 | tf_op jit(solution)/shard_map/all_to_all | solution.py:252
  219.1 5.8 %shard_map.141 = bf16[2,16,128,1024]{3,2,1,0:T(8,128)(2,1)} custom-call(s32[128]{0:T(128)S(1)} %copy-done.13, s32[128]{0:T(128)S(1)} %copy-done.12, s32[128]{0:T(128)S(1)} %copy-done.11, bf16[8,1,13,128,128]{4,3,2,1,0:T(8,128)(2,1)} %all-to-all-done.1.x_ref, bf16[2,16,128,1024]{3,2,1,0:T(8,128)(2,1)} %shard_map.140.refs_0_), custom_call_target="tpu_custom_call", output_to_operand_aliasing={{}: (4, {})} | custom-call | tf_op jit(solution)/shard_map/pallas_call | solution.py:191
  (5 shorter events, 0.1 us)
Async XLA Ops:
  0.0 78.4 %copy-start = (s32[256]{0:T(256)S(1)}, s32[256]{0:T(256)}, u32[]{:S(2)}) copy-start(s32[256]{0:T(256)} %param.25) | copy-start | bytes 3076
  5.7 64.7 %all-to-all-start.2 = ((bf16[128,1,1,128,128]{4,3,2,1,0:T(8,128)(2,1)}), bf16[128,1,1,128,128]{4,3,2,1,0:T(8,128)(2,1)}, u32[]{:S(2)}, u32[]{:S(2)}) async-start(bf16[128,1,1,128,128]{4,3,2,1,0:T(8,128)(2,1)} %shard_map.138), calls=%async_computation.2 | async-start | bytes 8388608 | tf_op jit(solution)/shard_map/all_to_all | solution.py:225
  23.2 53.3 %copy-start.14 = (s32[256]{0:T(256)S(1)}, s32[256]{0:T(256)}, u32[]{:S(2)}) copy-start(s32[256]{0:T(256)} %order_ref.3) | copy-start | bytes 3076
  23.2 54.0 %copy-start.16 = (f32[1024]{0:T(1024)S(1)}, f32[1024]{0:T(1024)}, u32[]{:S(2)}) copy-start(f32[1024]{0:T(1024)} %param.21) | copy-start | bytes 12292
  23.2 54.2 %copy-start.17 = (f32[1024]{0:T(1024)S(1)}, f32[1024]{0:T(1024)}, u32[]{:S(2)}) copy-start(f32[1024]{0:T(1024)} %param.22) | copy-start | bytes 12292
  23.2 57.7 %copy-start.15 = (bf16[1024,1024]{1,0:T(8,128)(2,1)S(1)}, bf16[1024,1024]{1,0:T(8,128)(2,1)}, u32[]{:S(2)}) copy-start(bf16[1024,1024]{1,0:T(8,128)(2,1)} %param.24) | copy-start | bytes 6291460
  70.3 58.3 %all-to-all-start = ((bf16[128,1,1,128,128]{4,3,2,1,0:T(8,128)(2,1)}), bf16[128,1,1,128,128]{4,3,2,1,0:T(8,128)(2,1)}, u32[]{:S(2)}, u32[]{:S(2)}) async-start(bf16[128,1,1,128,128]{4,3,2,1,0:T(8,128)(2,1)} %shard_map.136), calls=%async_computation | async-start | bytes 8388608 | tf_op jit(solution)/shard_map/all_to_all | solution.py:225
  77.4 5.9 %copy-start.5 = (f32[1024,1]{1,0:T(8,128)}, f32[1024,1]{1,0:T(8,128)S(1)}, u32[]{:S(2)}) copy-start(f32[1024,1]{1,0:T(8,128)S(1)} %copy.21.refs_2_) | copy-start | bytes 12292
  77.7 5.7 %copy-start.7 = (f32[1024,1]{1,0:T(8,128)}, f32[1024,1]{1,0:T(8,128)S(1)}, u32[]{:S(2)}) copy-start(f32[1024,1]{1,0:T(8,128)S(1)} %copy.22.refs_4_) | copy-start | bytes 12292
  80.9 2.5 %copy-start.9 = (f32[1024,1]{1,0:T(8,128)}, f32[1024,1]{1,0:T(8,128)S(1)}, u32[]{:S(2)}) copy-start(f32[1024,1]{1,0:T(8,128)S(1)} %multiply_divide_fusion.refs_3_) | copy-start | bytes 12292
  117.1 1.4 copy-start.1
  118.5 1.4 copy-start.3
  128.7 44.8 %all-to-all-start.3 = ((bf16[8,1,13,128,128]{4,3,2,1,0:T(8,128)(2,1)}), bf16[8,1,13,128,128]{4,3,2,1,0:T(8,128)(2,1)S(1)}, u32[]{:S(2)}, u32[]{:S(2)}) async-start(bf16[8,1,13,128,128]{4,3,2,1,0:T(8,128)(2,1)} %shard_map.139), calls=%async_computation.3 | async-start | bytes 6815744 | tf_op jit(solution)/shard_map/all_to_all | solution.py:252
  133.2 1.6 copy-start.2
  134.7 1.6 copy-start.4
  136.3 1.0 copy-start.6
  137.4 1.0 copy-start.8
  138.4 1.0 copy-start.10
  173.1 5.6 %copy-start.11 = (s32[128]{0:T(128)S(1)}, s32[128]{0:T(128)}, u32[]{:S(2)}) copy-start(s32[128]{0:T(128)} %constant.127.clone.ok_ref) | copy-start | bytes 1540
  173.1 5.6 %copy-start.12 = (s32[128]{0:T(128)S(1)}, s32[128]{0:T(128)}, u32[]{:S(2)}) copy-start(s32[128]{0:T(128)} %constant.126.clone.j_ref) | copy-start | bytes 1540
  173.1 5.6 %copy-start.13 = (s32[128]{0:T(128)S(1)}, s32[128]{0:T(128)}, u32[]{:S(2)}) copy-start(s32[128]{0:T(128)} %constant.125.clone.r_ref) | copy-start | bytes 1540
  173.4 45.7 %all-to-all-start.1 = ((bf16[8,1,13,128,128]{4,3,2,1,0:T(8,128)(2,1)}), bf16[8,1,13,128,128]{4,3,2,1,0:T(8,128)(2,1)}, u32[]{:S(2)}, u32[]{:S(2)}) async-start(bf16[8,1,13,128,128]{4,3,2,1,0:T(8,128)(2,1)} %shard_map.137), calls=%async_computation.1 | async-start | bytes 6815744 | tf_op jit(solution)/shard_map/all_to_all | solution.py:252

commit v13 on v11

--- a/solution.py
+++ b/solution.py
@@ -53,11 +53,11 @@
 
 def pack_kernel(order_ref, shift_ref, *refs):
     x_refs, o_ref = refs[:-1], refs[-1]
-    nrad, window = o_ref.shape[0] // len(x_refs), o_ref.shape[-1]
+    nrad, window = o_ref.shape[0], o_ref.shape[-1]
     turn = shift_ref[lax.axis_index("mode")]
     for i, x_ref in enumerate(x_refs):
         for w in range(nrad):
-            o_ref[i * nrad + (w + turn) % nrad] = x_ref[:, 0:1, :, w * window:(w + 1) * window]
+            o_ref[(w + turn) % nrad, i] = x_ref[:, 0:1, :, w * window:(w + 1) * window]
 
 
 def pack(spectra, order_slot, shifts, comp, groups, nrad, per_group, step=8):
@@ -73,13 +73,13 @@
         return index
 
     def out_map(q, p, d):
-        return (q, 0, 0, 0, 0)
+        return (0, q, 0, 0, 0, 0)
 
     assert per_group == 1 and picks_total % step == 0
     return pl.pallas_call(
         pack_kernel,
         out_shape=jax.ShapeDtypeStruct(
-            (groups * nrad, 1, per_group, shells_here, window), spectra.dtype
+            (nrad, groups, 1, per_group, shells_here, window), spectra.dtype
         ),
         grid_spec=pltpu.PrefetchScalarGridSpec(
             num_scalar_prefetch=2,
@@ -88,7 +88,7 @@
                 pl.BlockSpec((1, 1, shells_here, slots_total), in_map(i))
                 for i in range(step)
             ],
-            out_specs=pl.BlockSpec((step * nrad, 1, per_group, shells_here, window), out_map),
+            out_specs=pl.BlockSpec((nrad, step, 1, per_group, shells_here, window), out_map),
         ),
     )(order_slot, shifts, *([spectra] * step))
 
@@ -97,10 +97,10 @@
     npos = len(refs) - 8
     x_refs = refs[:npos]
     info_ref, kappa_ref, invden_ref, eig_ref, d_ref, b_ref, o_ref, pad_ref = refs[npos:]
-    nrad = x_refs[0].shape[1]
+    nrad = x_refs[0].shape[0]
     sh, window = x_refs[0].shape[4], x_refs[0].shape[5]
     nr = nrad * sh
-    cols = [x_ref[0, :, 0, 0].reshape(nr, window) for x_ref in x_refs]
+    cols = [x_ref[:, 0, 0, 0].reshape(nr, window) for x_ref in x_refs]
     f = jnp.concatenate(cols, axis=1).astype(jnp.float32)
     width = f.shape[1]
     pad_ref[0:PAD, :] = jnp.zeros((PAD, width), jnp.float32)
@@ -132,11 +132,11 @@
     nr = nrad * sh
     count = pos.shape[0]
     assert per_group == 1 and count % npos == 0
-    x = recv.reshape(groups, nrad, 1, per_group, sh, window)
+    x = recv.reshape(nrad, groups, 1, per_group, sh, window)
     flops = 2 * 2 * nr * nr * window * count
 
     def x_map(j):
-        return lambda q, p: (p[q * npos + j], 0, 0, 0, 0, 0)
+        return lambda q, p: (0, p[q * npos + j], 0, 0, 0, 0)
 
     return pl.pallas_call(
         solve_kernel,
@@ -145,7 +145,7 @@
             num_scalar_prefetch=1,
             grid=(count // npos,),
             in_specs=[
-                pl.BlockSpec((1, nrad, 1, 1, sh, window), x_map(j)) for j in range(npos)
+                pl.BlockSpec((nrad, 1, 1, 1, sh, window), x_map(j)) for j in range(npos)
             ] + [
                 pl.BlockSpec((npos, 8, window), lambda q, p: (q, 0, 0)),
                 pl.BlockSpec((nr, 1), lambda q, p: (0, 0)),
@@ -222,7 +222,8 @@
     recvs = []
     for comp in range(comps):
         send = pack(spectra, order_slot, shifts, comp, groups, nrad, per_group)
-        recvs.append(lax.all_to_all(send, ("mode", "rad"), 0, 0, tiled=True))
+        send = send.reshape((nrad * groups,) + send.shape[2:])
+        recvs.append(lax.all_to_all(send, ("rad", "mode"), 0, 0, tiled=True))
 
     pos = jnp.asarray(tab["pos"], jnp.int32)[me_rad]
     win = jnp.asarray(tab["win"], jnp.int32)[me_rad]

time: 224 us -> 221 us (0.987)
  waiting for transfers between devices: 94.2 us -> 90.8 us
    all_to_all x2, waiting for transfers between devices: 56.8 us -> 53.5 us  [on_device(): recvs.append(lax.all_to_all(send, ('rad', 'mode'), 0, 0, tiled=True))]
where the time goes in v13:
time: 221 us; the launch traced here: 220 us
  waiting for transfers between devices  90.8 us (41%)
  Pallas kernels  85.5 us (39%)
  starting transfers between devices  27.1 us (12%)
  local copies, waits for them, and re-layouts  11.6 us (5%)
  other arithmetic  4.88 us (2%)
    pallas_call x2, Pallas kernels, solve(): pl.pallas_call(solve_kernel, out_shape=jax.ShapeDtypeStruct((nrad, 1, cou...  67.5 us
    all_to_all x2, waiting for transfers between devices, on_device(): recvs.append(lax.all_to_all(send, ('rad', 'mode'), 0, 0, tiled=True))  53.5 us
    all_to_all x2, waiting for transfers between devices, on_device(): gots.append(lax.all_to_all(back, 'rad', 0, 0, tiled=True))  37.4 us
    all_to_all x2, starting transfers between devices, on_device(): recvs.append(lax.all_to_all(send, ('rad', 'mode'), 0, 0, tiled=True))  17.5 us
    all_to_all x2, starting transfers between devices, on_device(): gots.append(lax.all_to_all(back, 'rad', 0, 0, tiled=True))  9.6 us
    pallas_call x2, Pallas kernels, pack(): pl.pallas_call(pack_kernel, out_shape=jax.ShapeDtypeStruct((nrad, groups,...  9.52 us
    unnamed x36, local copies, waits for them, and re-layouts  9.1 us
    pallas_call x2, Pallas kernels, unpack(): pl.pallas_call(unpack_kernel, out_shape=jax.ShapeDtypeStruct(shape, got.d...  8.48 us
  transfers between devices with their start and end apart: 4, of which 4 were waited for; matrix products, arithmetic and copies ran while one was open for 3% of the time, Pallas kernels for 34%

profile of v13, /device:TPU:1, one launch (start us, length us, event | category | flops | bytes accessed | tf_op | source)
XLA Modules:
  0.0 220.2 jit_solution(15705757979432130633)
XLA Ops:
  0.0 0.0 copy-start
  0.0 4.8 %shard_map.138 = bf16[8,16,1,1,128,128]{5,4,3,2,1,0:T(8,128)(2,1)} custom-call(s32[256]{0:T(256)} %order_ref.3, s32[16]{0:T(128)} %constant.121.clone.shift_ref, bf16[2,16,128,1024]{3,2,1,0:T(8,128)(2,1)} %refs_7_.3, bf16[2,16,128,1024]{3,2,1,0:T(8,128)(2,1)} %refs_7_.3, bf16[2,16,128,1024]{3,2,1,0:T(8,128)(2,1)} %refs_7_.3, ...), custom_call_target="tpu_custom_call" | custom-call | tf_op jit(solution)/shard_map/pallas_call | solution.py:79
  4.8 11.9 %all-to-all-start.2 = ((bf16[128,1,1,128,128]{4,3,2,1,0:T(8,128)(2,1)}), bf16[128,1,1,128,128]{4,3,2,1,0:T(8,128)(2,1)}, u32[]{:S(2)}, u32[]{:S(2)}) async-start(bf16[128,1,1,128,128]{4,3,2,1,0:T(8,128)(2,1)} %bitcast.19), calls=%async_computation.2 | async-start | bytes 8388608 | tf_op jit(solution)/shard_map/all_to_all | solution.py:226
  16.8 4.7 %shard_map.136 = bf16[8,16,1,1,128,128]{5,4,3,2,1,0:T(8,128)(2,1)} custom-call(s32[256]{0:T(256)} %order_ref.3, s32[16]{0:T(128)} %constant.121.clone.shift_ref, bf16[2,16,128,1024]{3,2,1,0:T(8,128)(2,1)} %refs_7_.3, bf16[2,16,128,1024]{3,2,1,0:T(8,128)(2,1)} %refs_7_.3, bf16[2,16,128,1024]{3,2,1,0:T(8,128)(2,1)} %refs_7_.3, ...), custom_call_target="tpu_custom_call" | custom-call | tf_op jit(solution)/shard_map/pallas_call | solution.py:79
  21.5 46.5 %all-to-all-done.2 = bf16[128,1,1,128,128]{4,3,2,1,0:T(8,128)(2,1)} async-done(((bf16[128,1,1,128,128]{4,3,2,1,0:T(8,128)(2,1)}), bf16[128,1,1,128,128]{4,3,2,1,0:T(8,128)(2,1)}, u32[]{:S(2)}, u32[]{:S(2)}) %all-to-all-start.2) | async-done | bytes 4194336 | tf_op jit(solution)/shard_map/all_to_all | solution.py:226
  67.9 0.0 copy-start.14
  67.9 0.0 copy-start.16
  67.9 0.0 copy-start.17
  67.9 0.0 copy-start.15
  68.0 5.6 %all-to-all-start = ((bf16[128,1,1,128,128]{4,3,2,1,0:T(8,128)(2,1)}), bf16[128,1,1,128,128]{4,3,2,1,0:T(8,128)(2,1)}, u32[]{:S(2)}, u32[]{:S(2)}) async-start(bf16[128,1,1,128,128]{4,3,2,1,0:T(8,128)(2,1)} %bitcast.18), calls=%async_computation | async-start | bytes 8388608 | tf_op jit(solution)/shard_map/all_to_all | solution.py:226
  73.5 0.7 compare_select_fusion.1
  74.2 0.0 copy-done.14
  74.2 0.7 gather_fusion
  74.9 0.0 copy-done.16
  74.9 0.2 copy.28.refs_2_
  75.1 0.0 copy-start.5
  75.2 0.0 copy-done.17
  75.2 0.2 copy.29.refs_4_
  75.4 0.0 copy-start.7
  75.4 0.7 compare_select_fusion
  76.1 0.0 copy-done
  76.1 0.7 gather_fusion.1
  76.8 0.7 multiply_bitcast_fusion
  77.5 0.1 add_convert_fusion
  77.6 0.1 compare_convert_fusion
  77.8 0.7 dynamic-slice_bitcast_fusion.pos_ref
  78.5 0.1 multiply_divide_fusion.refs_3_
  78.6 0.0 copy-done.15
  78.6 0.0 copy-start.9
  78.6 2.4 %fusion = (bf16[1024,1024]{1,0:T(8,128)(2,1)S(1)}, bf16[1024,1024]{1,0:T(8,128)(2,1)S(1)}) fusion(bf16[1024,1024]{1,0:T(8,128)(2,1)S(1)} %copy-done.15, bf16[1024,1024]{1,0:T(8,128)(2,1)} %param.23), kind=kLoop, calls=%fused_computation.4 | loop fusion | flops 8388608 | bytes 8388608 | tf_op jit(solution)/shard_map/convert_element_type | solution.py:248
  81.1 0.0 copy-done.5
  81.1 0.0 copy-done.7
  81.1 0.0 copy-done.9
  81.1 33.8 %shard_map.139 = bf16[8,1,13,128,128]{4,3,2,1,0:T(8,128)(2,1)} custom-call(s32[13]{0:T(128)S(1)} %dynamic-slice_bitcast_fusion.pos_ref, bf16[8,16,1,1,128,128]{5,4,3,2,1,0:T(8,128)(2,1)} %bitcast.9.refs_0_, f32[13,8,128]{2,1,0:T(8,128)S(1)} %scatter.9.refs_1_, f32[1024,1]{1,0:T(8,128)S(1)} %copy.28.refs_2_, f32[1024,1]{1,0:T(8,128)S(1)} %multiply_divide_fusion.refs_3_, ...), custom_call_target="tpu_custom_call" | custom-call | flops 6979321856 | bytes 11010048 | tf_op jit(solution)/shard_map/pallas_call | solution.py:141
  114.9 0.0 copy-start.1
  114.9 1.3 copy-done.1
  116.2 0.0 copy-start.3
  116.2 1.4 copy-done.3
  117.6 7.0 %all-to-all-done = bf16[128,1,1,128,128]{4,3,2,1,0:T(8,128)(2,1)} async-done(((bf16[128,1,1,128,128]{4,3,2,1,0:T(8,128)(2,1)}), bf16[128,1,1,128,128]{4,3,2,1,0:T(8,128)(2,1)}, u32[]{:S(2)}, u32[]{:S(2)}) %all-to-all-start) | async-done | bytes 4194336 | tf_op jit(solution)/shard_map/all_to_all | solution.py:226
  124.7 4.3 %all-to-all-start.3 = ((bf16[8,1,13,128,128]{4,3,2,1,0:T(8,128)(2,1)}), bf16[8,1,13,128,128]{4,3,2,1,0:T(8,128)(2,1)S(1)}, u32[]{:S(2)}, u32[]{:S(2)}) async-start(bf16[8,1,13,128,128]{4,3,2,1,0:T(8,128)(2,1)} %shard_map.139), calls=%async_computation.3 | async-start | bytes 6815744 | tf_op jit(solution)/shard_map/all_to_all | solution.py:253
  128.9 0.0 copy-start.2
  128.9 1.6 copy-done.2
  130.5 0.0 copy-start.4
  130.5 1.6 copy-done.4
  132.1 0.0 copy-start.6
  132.1 1.0 copy-done.6
  133.2 0.0 copy-start.8
  133.2 1.0 copy-done.8
  134.2 0.0 copy-start.10
  134.2 1.0 copy-done.10
  135.3 33.7 %shard_map.137 = bf16[8,1,13,128,128]{4,3,2,1,0:T(8,128)(2,1)} custom-call(s32[13]{0:T(128)S(1)} %dynamic-slice_bitcast_fusion.pos_ref, bf16[8,16,1,1,128,128]{5,4,3,2,1,0:T(8,128)(2,1)} %bitcast.3.refs_0_, f32[13,8,128]{2,1,0:T(8,128)S(1)} %scatter.9.refs_1_, f32[1024,1]{1,0:T(8,128)S(1)} %copy-done.6, f32[1024,1]{1,0:T(8,128)S(1)} %copy-done.10, ...), custom_call_target="tpu_custom_call" | custom-call | flops 6979321856 | bytes 11010048 | tf_op jit(solution)/shard_map/pallas_call | solution.py:141
  169.0 0.0 copy-start.11
  169.0 0.0 copy-start.12
  169.0 0.0 copy-start.13
  169.0 0.2 all-to-all-done.3.x_ref
  169.2 5.3 %all-to-all-start.1 = ((bf16[8,1,13,128,128]{4,3,2,1,0:T(8,128)(2,1)}), bf16[8,1,13,128,128]{4,3,2,1,0:T(8,128)(2,1)}, u32[]{:S(2)}, u32[]{:S(2)}) async-start(bf16[8,1,13,128,128]{4,3,2,1,0:T(8,128)(2,1)} %shard_map.137), calls=%async_computation.1 | async-start | bytes 6815744 | tf_op jit(solution)/shard_map/all_to_all | solution.py:253
  174.6 0.0 copy-done.11
  174.6 0.0 copy-done.12
  174.6 0.0 copy-done.13
  174.6 3.3 %shard_map.140.refs_0_ = bf16[2,16,128,1024]{3,2,1,0:T(8,128)(2,1)} custom-call(s32[128]{0:T(128)S(1)} %copy-done.13, s32[128]{0:T(128)S(1)} %copy-done.12, s32[128]{0:T(128)S(1)} %copy-done.11, bf16[8,1,13,128,128]{4,3,2,1,0:T(8,128)(2,1)S(1)} %all-to-all-done.3.x_ref), custom_call_target="tpu_custom_call" | custom-call | tf_op jit(solution)/shard_map/pallas_call | solution.py:191
  177.8 37.1 %all-to-all-done.1.x_ref = bf16[8,1,13,128,128]{4,3,2,1,0:T(8,128)(2,1)} async-done(((bf16[8,1,13,128,128]{4,3,2,1,0:T(8,128)(2,1)}), bf16[8,1,13,128,128]{4,3,2,1,0:T(8,128)(2,1)}, u32[]{:S(2)}, u32[]{:S(2)}) %all-to-all-start.1) | async-done | bytes 3407904 | tf_op jit(solution)/shard_map/all_to_all | solution.py:253
  214.9 5.2 %shard_map.141 = bf16[2,16,128,1024]{3,2,1,0:T(8,128)(2,1)} custom-call(s32[128]{0:T(128)S(1)} %copy-done.13, s32[128]{0:T(128)S(1)} %copy-done.12, s32[128]{0:T(128)S(1)} %copy-done.11, bf16[8,1,13,128,128]{4,3,2,1,0:T(8,128)(2,1)} %all-to-all-done.1.x_ref, bf16[2,16,128,1024]{3,2,1,0:T(8,128)(2,1)} %shard_map.140.refs_0_), custom_call_target="tpu_custom_call", output_to_operand_aliasing={{}: (4, {})} | custom-call | tf_op jit(solution)/shard_map/pallas_call | solution.py:191
  (5 shorter events, 0.1 us)
Async XLA Ops:
  0.0 76.1 %copy-start = (s32[256]{0:T(256)S(1)}, s32[256]{0:T(256)}, u32[]{:S(2)}) copy-start(s32[256]{0:T(256)} %param.25) | copy-start | bytes 3076
  4.8 63.1 %all-to-all-start.2 = ((bf16[128,1,1,128,128]{4,3,2,1,0:T(8,128)(2,1)}), bf16[128,1,1,128,128]{4,3,2,1,0:T(8,128)(2,1)}, u32[]{:S(2)}, u32[]{:S(2)}) async-start(bf16[128,1,1,128,128]{4,3,2,1,0:T(8,128)(2,1)} %bitcast.19), calls=%async_computation.2 | async-start | bytes 8388608 | tf_op jit(solution)/shard_map/all_to_all | solution.py:226
  67.9 6.3 %copy-start.14 = (s32[256]{0:T(256)S(1)}, s32[256]{0:T(256)}, u32[]{:S(2)}) copy-start(s32[256]{0:T(256)} %order_ref.3) | copy-start | bytes 3076
  67.9 7.0 %copy-start.16 = (f32[1024]{0:T(1024)S(1)}, f32[1024]{0:T(1024)}, u32[]{:S(2)}) copy-start(f32[1024]{0:T(1024)} %param.21) | copy-start | bytes 12292
  67.9 7.2 %copy-start.17 = (f32[1024]{0:T(1024)S(1)}, f32[1024]{0:T(1024)}, u32[]{:S(2)}) copy-start(f32[1024]{0:T(1024)} %param.22) | copy-start | bytes 12292
  67.9 10.7 %copy-start.15 = (bf16[1024,1024]{1,0:T(8,128)(2,1)S(1)}, bf16[1024,1024]{1,0:T(8,128)(2,1)}, u32[]{:S(2)}) copy-start(bf16[1024,1024]{1,0:T(8,128)(2,1)} %param.24) | copy-start | bytes 6291460
  68.0 56.7 %all-to-all-start = ((bf16[128,1,1,128,128]{4,3,2,1,0:T(8,128)(2,1)}), bf16[128,1,1,128,128]{4,3,2,1,0:T(8,128)(2,1)}, u32[]{:S(2)}, u32[]{:S(2)}) async-start(bf16[128,1,1,128,128]{4,3,2,1,0:T(8,128)(2,1)} %bitcast.18), calls=%async_computation | async-start | bytes 8388608 | tf_op jit(solution)/shard_map/all_to_all | solution.py:226
  75.1 5.9 %copy-start.5 = (f32[1024,1]{1,0:T(8,128)}, f32[1024,1]{1,0:T(8,128)S(1)}, u32[]{:S(2)}) copy-start(f32[1024,1]{1,0:T(8,128)S(1)} %copy.28.refs_2_) | copy-start | bytes 12292
  75.4 5.7 %copy-start.7 = (f32[1024,1]{1,0:T(8,128)}, f32[1024,1]{1,0:T(8,128)S(1)}, u32[]{:S(2)}) copy-start(f32[1024,1]{1,0:T(8,128)S(1)} %copy.29.refs_4_) | copy-start | bytes 12292
  78.6 2.5 %copy-start.9 = (f32[1024,1]{1,0:T(8,128)}, f32[1024,1]{1,0:T(8,128)S(1)}, u32[]{:S(2)}) copy-start(f32[1024,1]{1,0:T(8,128)S(1)} %multiply_divide_fusion.refs_3_) | copy-start | bytes 12292
  114.9 1.4 copy-start.1
  116.2 1.4 copy-start.3
  124.7 44.5 %all-to-all-start.3 = ((bf16[8,1,13,128,128]{4,3,2,1,0:T(8,128)(2,1)}), bf16[8,1,13,128,128]{4,3,2,1,0:T(8,128)(2,1)S(1)}, u32[]{:S(2)}, u32[]{:S(2)}) async-start(bf16[8,1,13,128,128]{4,3,2,1,0:T(8,128)(2,1)} %shard_map.139), calls=%async_computation.3 | async-start | bytes 6815744 | tf_op jit(solution)/shard_map/all_to_all | solution.py:253
  128.9 1.6 copy-start.2
  130.5 1.6 copy-start.4
  132.1 1.0 copy-start.6
  133.2 1.0 copy-start.8
  134.2 1.0 copy-start.10
  169.0 5.6 %copy-start.11 = (s32[128]{0:T(128)S(1)}, s32[128]{0:T(128)}, u32[]{:S(2)}) copy-start(s32[128]{0:T(128)} %constant.127.clone.ok_ref) | copy-start | bytes 1540
  169.0 5.6 %copy-start.12 = (s32[128]{0:T(128)S(1)}, s32[128]{0:T(128)}, u32[]{:S(2)}) copy-start(s32[128]{0:T(128)} %constant.126.clone.j_ref) | copy-start | bytes 1540
  169.0 5.6 %copy-start.13 = (s32[128]{0:T(128)S(1)}, s32[128]{0:T(128)}, u32[]{:S(2)}) copy-start(s32[128]{0:T(128)} %constant.125.clone.r_ref) | copy-start | bytes 1540
  169.2 45.7 %all-to-all-start.1 = ((bf16[8,1,13,128,128]{4,3,2,1,0:T(8,128)(2,1)}), bf16[8,1,13,128,128]{4,3,2,1,0:T(8,128)(2,1)}, u32[]{:S(2)}, u32[]{:S(2)}) async-start(bf16[8,1,13,128,128]{4,3,2,1,0:T(8,128)(2,1)} %shard_map.137), calls=%async_computation.1 | async-start | bytes 6815744 | tf_op jit(solution)/shard_map/all_to_all | solution.py:253

commit v14 on v13

--- a/solution.py
+++ b/solution.py
@@ -94,9 +94,12 @@
 
 
 def solve_kernel(pos_ref, *refs):
-    npos = len(refs) - 8
+    npos = len(refs) - 6
     x_refs = refs[:npos]
-    info_ref, kappa_ref, invden_ref, eig_ref, d_ref, b_ref, o_ref, pad_ref = refs[npos:]
+    info_ref, shell_ref, d_ref, b_ref, o_ref, pad_ref = refs[npos:]
+    kappa = shell_ref[:, 0:1]
+    invden = shell_ref[:, 1:2]
+    eig = shell_ref[:, 2:3]
     nrad = x_refs[0].shape[0]
     sh, window = x_refs[0].shape[4], x_refs[0].shape[5]
     nr = nrad * sh
@@ -114,11 +117,11 @@
     deg = jnp.concatenate([info_ref[j, 0:1, :] for j in range(npos)], axis=1)
     live = jnp.concatenate([info_ref[j, 1:2, :] for j in range(npos)], axis=1) > 0.5
     lterm = deg * (deg + 1.0)
-    damping = lterm * invden_ref[...]
-    updated = f + 0.5 * kappa_ref[...] * (second - damping * f)
+    damping = lterm * invden
+    updated = f + 0.5 * kappa * (second - damping * f)
     updated = jnp.where(live, updated, 0.0).astype(jnp.bfloat16)
     projected = jnp.dot(d_ref[...], updated, preferred_element_type=jnp.float32)
-    divisor = eig_ref[...] + 0.5 * lterm / float(nr * nr)
+    divisor = eig + 0.5 * lterm / float(nr * nr)
     scaled = (projected / divisor).astype(jnp.bfloat16)
     restored = jnp.dot(b_ref[...], scaled, preferred_element_type=jnp.float32)
     solved = jnp.where(live, restored, 0.0).astype(jnp.bfloat16)
@@ -126,7 +129,7 @@
         o_ref[:, 0, j] = solved[:, j * window:(j + 1) * window].reshape(nrad, sh, window)
 
 
-def solve(recv, pos, info, kappa, invden, eig, dual_full, basis_full, groups, nrad, per_group,
+def solve(recv, pos, info, shell, dual_full, basis_full, groups, nrad, per_group,
           npos=1):
     _, _, _, sh, window = recv.shape
     nr = nrad * sh
@@ -148,9 +151,7 @@
                 pl.BlockSpec((nrad, 1, 1, 1, sh, window), x_map(j)) for j in range(npos)
             ] + [
                 pl.BlockSpec((npos, 8, window), lambda q, p: (q, 0, 0)),
-                pl.BlockSpec((nr, 1), lambda q, p: (0, 0)),
-                pl.BlockSpec((nr, 1), lambda q, p: (0, 0)),
-                pl.BlockSpec((nr, 1), lambda q, p: (0, 0)),
+                pl.BlockSpec((nr, 3), lambda q, p: (0, 0)),
                 pl.BlockSpec((nr, nr), lambda q, p: (0, 0)),
                 pl.BlockSpec((nr, nr), lambda q, p: (0, 0)),
             ],
@@ -161,7 +162,7 @@
         cost_estimate=pl.CostEstimate(
             flops=flops, transcendentals=0, bytes_accessed=4 * count * nr * window + 4 * nr * nr
         ),
-    )(pos, *([x] * npos), info, kappa, invden, eig, dual_full, basis_full)
+    )(pos, *([x] * npos), info, shell, dual_full, basis_full)
 
 
 def unpack_kernel(r_ref, j_ref, ok_ref, x_ref, *refs):
@@ -242,13 +243,14 @@
     invden = (1.0 / ((shells_total * radius) ** 2)).reshape(shells_total, 1)
     kappa = diffusivity.reshape(shells_total, 1)
     eig = eigenvalues.reshape(shells_total, 1)
+    shell = jnp.concatenate([kappa, invden, eig], axis=1)
 
     identity = jnp.eye(shells_total, dtype=jnp.float32)
     basis_full = (identity + radial_basis.astype(jnp.float32)).astype(jnp.bfloat16)
     dual_full = (identity + dual_basis.astype(jnp.float32)).astype(jnp.bfloat16)
     gots = []
     for recv in recvs:
-        back = solve(recv, pos, info, kappa, invden, eig, dual_full, basis_full, groups, nrad,
+        back = solve(recv, pos, info, shell, dual_full, basis_full, groups, nrad,
                      per_group)
         gots.append(lax.all_to_all(back, "rad", 0, 0, tiled=True))
     src_r = jnp.asarray(tab["src_r"], jnp.int32)

time: 221 us -> 221 us (level)
  local copies, waits for them, and re-layouts: 11.6 us -> 9.26 us
    unnamed x36 -> x28, local copies, waits for them, and re-layouts: 9.1 us -> 6.96 us
  transfers between devices with their start and end apart: 4 -> 4, of which waited for: 4 -> 4; matrix products, arithmetic and copies ran while one was open for 3% -> 3% of each run, Pallas kernels for 34% -> 35%
where the time goes in v14:
time: 221 us; the launch traced here: 220 us
  waiting for transfers between devices  92.6 us (42%)
  Pallas kernels  86.4 us (39%)
  starting transfers between devices  27.1 us (12%)
  local copies, waits for them, and re-layouts  9.26 us (4%)
  other arithmetic  4.6 us (2%)
    pallas_call x2, Pallas kernels, solve(): pl.pallas_call(solve_kernel, out_shape=jax.ShapeDtypeStruct((nrad, 1, cou...  68.4 us
    all_to_all x2, waiting for transfers between devices, on_device(): recvs.append(lax.all_to_all(send, ('rad', 'mode'), 0, 0, tiled=True))  53.7 us
    all_to_all x2, waiting for transfers between devices, on_device(): gots.append(lax.all_to_all(back, 'rad', 0, 0, tiled=True))  39 us
    all_to_all x2, starting transfers between devices, on_device(): recvs.append(lax.all_to_all(send, ('rad', 'mode'), 0, 0, tiled=True))  17.5 us
    all_to_all x2, starting transfers between devices, on_device(): gots.append(lax.all_to_all(back, 'rad', 0, 0, tiled=True))  9.59 us
    pallas_call x2, Pallas kernels, pack(): pl.pallas_call(pack_kernel, out_shape=jax.ShapeDtypeStruct((nrad, groups,...  9.49 us
    pallas_call x2, Pallas kernels, unpack(): pl.pallas_call(unpack_kernel, out_shape=jax.ShapeDtypeStruct(shape, got.d...  8.48 us
    unnamed x28, local copies, waits for them, and re-layouts  6.96 us
  transfers between devices with their start and end apart: 4, of which 4 were waited for; matrix products, arithmetic and copies ran while one was open for 3% of the time, Pallas kernels for 35%

profile of v14, /device:TPU:1, one launch (start us, length us, event | category | flops | bytes accessed | tf_op | source)
XLA Modules:
  0.0 220.1 jit_solution(10631137702025963585)
XLA Ops:
  0.0 0.0 copy-start
  0.0 4.8 %shard_map.138 = bf16[8,16,1,1,128,128]{5,4,3,2,1,0:T(8,128)(2,1)} custom-call(s32[256]{0:T(256)} %order_ref.3, s32[16]{0:T(128)} %constant.121.clone.shift_ref, bf16[2,16,128,1024]{3,2,1,0:T(8,128)(2,1)} %refs_7_.3, bf16[2,16,128,1024]{3,2,1,0:T(8,128)(2,1)} %refs_7_.3, bf16[2,16,128,1024]{3,2,1,0:T(8,128)(2,1)} %refs_7_.3, ...), custom_call_target="tpu_custom_call" | custom-call | tf_op jit(solution)/shard_map/pallas_call | solution.py:79
  4.8 11.9 %all-to-all-start.2 = ((bf16[128,1,1,128,128]{4,3,2,1,0:T(8,128)(2,1)}), bf16[128,1,1,128,128]{4,3,2,1,0:T(8,128)(2,1)}, u32[]{:S(2)}, u32[]{:S(2)}) async-start(bf16[128,1,1,128,128]{4,3,2,1,0:T(8,128)(2,1)} %bitcast.19), calls=%async_computation.2 | async-start | bytes 8388608 | tf_op jit(solution)/shard_map/all_to_all | solution.py:227
  16.7 4.7 %shard_map.136 = bf16[8,16,1,1,128,128]{5,4,3,2,1,0:T(8,128)(2,1)} custom-call(s32[256]{0:T(256)} %order_ref.3, s32[16]{0:T(128)} %constant.121.clone.shift_ref, bf16[2,16,128,1024]{3,2,1,0:T(8,128)(2,1)} %refs_7_.3, bf16[2,16,128,1024]{3,2,1,0:T(8,128)(2,1)} %refs_7_.3, bf16[2,16,128,1024]{3,2,1,0:T(8,128)(2,1)} %refs_7_.3, ...), custom_call_target="tpu_custom_call" | custom-call | tf_op jit(solution)/shard_map/pallas_call | solution.py:79
  21.4 46.5 %all-to-all-done.2 = bf16[128,1,1,128,128]{4,3,2,1,0:T(8,128)(2,1)} async-done(((bf16[128,1,1,128,128]{4,3,2,1,0:T(8,128)(2,1)}), bf16[128,1,1,128,128]{4,3,2,1,0:T(8,128)(2,1)}, u32[]{:S(2)}, u32[]{:S(2)}) %all-to-all-start.2) | async-done | bytes 4194336 | tf_op jit(solution)/shard_map/all_to_all | solution.py:227
  67.9 0.0 copy-start.10
  67.9 0.0 copy-start.12
  67.9 0.0 copy-start.13
  67.9 0.0 copy-start.11
  67.9 5.6 %all-to-all-start = ((bf16[128,1,1,128,128]{4,3,2,1,0:T(8,128)(2,1)}), bf16[128,1,1,128,128]{4,3,2,1,0:T(8,128)(2,1)}, u32[]{:S(2)}, u32[]{:S(2)}) async-start(bf16[128,1,1,128,128]{4,3,2,1,0:T(8,128)(2,1)} %bitcast.18), calls=%async_computation | async-start | bytes 8388608 | tf_op jit(solution)/shard_map/all_to_all | solution.py:227
  73.5 0.7 compare_select_fusion.1
  74.2 0.0 copy-done.10
  74.2 0.7 gather_fusion
  74.9 0.0 copy-done.12
  74.9 0.0 copy-done.13
  74.9 0.2 copy.19.refs_2_
  75.2 0.0 copy-start.5
  75.2 0.7 compare_select_fusion
  75.9 0.0 copy-done
  75.9 0.7 gather_fusion.1
  76.6 0.7 multiply_bitcast_fusion
  77.3 0.1 add_convert_fusion
  77.4 0.1 compare_convert_fusion
  77.6 0.7 dynamic-slice_bitcast_fusion.pos_ref
  78.3 0.0 copy-done.11
  78.3 2.2 %fusion = (bf16[1024,1024]{1,0:T(8,128)(2,1)S(1)}, bf16[1024,1024]{1,0:T(8,128)(2,1)S(1)}) fusion(bf16[1024,1024]{1,0:T(8,128)(2,1)S(1)} %copy-done.11, bf16[1024,1024]{1,0:T(8,128)(2,1)} %param.23), kind=kLoop, calls=%fused_computation.4 | loop fusion | flops 8388608 | bytes 8388608 | tf_op jit(solution)/shard_map/convert_element_type | solution.py:250
  80.5 0.0 copy-done.5
  80.5 34.2 %shard_map.139 = bf16[8,1,13,128,128]{4,3,2,1,0:T(8,128)(2,1)} custom-call(s32[13]{0:T(128)S(1)} %dynamic-slice_bitcast_fusion.pos_ref, bf16[8,16,1,1,128,128]{5,4,3,2,1,0:T(8,128)(2,1)} %bitcast.9.refs_0_, f32[13,8,128]{2,1,0:T(8,128)S(1)} %scatter.9.refs_1_, f32[1024,3]{1,0:T(8,128)S(1)} %copy.19.refs_2_, ...), custom_call_target="tpu_custom_call" | custom-call | flops 6979321856 | bytes 11010048 | tf_op jit(solution)/shard_map/pallas_call | solution.py:144
  114.7 0.0 copy-start.1
  114.7 1.3 copy-done.1
  116.0 0.0 copy-start.3
  116.0 1.4 copy-done.3
  117.4 7.2 %all-to-all-done = bf16[128,1,1,128,128]{4,3,2,1,0:T(8,128)(2,1)} async-done(((bf16[128,1,1,128,128]{4,3,2,1,0:T(8,128)(2,1)}), bf16[128,1,1,128,128]{4,3,2,1,0:T(8,128)(2,1)}, u32[]{:S(2)}, u32[]{:S(2)}) %all-to-all-start) | async-done | bytes 4194336 | tf_op jit(solution)/shard_map/all_to_all | solution.py:227
  124.6 4.3 %all-to-all-start.3 = ((bf16[8,1,13,128,128]{4,3,2,1,0:T(8,128)(2,1)}), bf16[8,1,13,128,128]{4,3,2,1,0:T(8,128)(2,1)S(1)}, u32[]{:S(2)}, u32[]{:S(2)}) async-start(bf16[8,1,13,128,128]{4,3,2,1,0:T(8,128)(2,1)} %shard_map.139), calls=%async_computation.3 | async-start | bytes 6815744 | tf_op jit(solution)/shard_map/all_to_all | solution.py:255
  128.9 0.0 copy-start.2
  128.9 1.6 copy-done.2
  130.5 0.0 copy-start.4
  130.5 1.6 copy-done.4
  132.1 0.0 copy-start.6
  132.1 1.0 copy-done.6
  133.1 34.2 %shard_map.137 = bf16[8,1,13,128,128]{4,3,2,1,0:T(8,128)(2,1)} custom-call(s32[13]{0:T(128)S(1)} %dynamic-slice_bitcast_fusion.pos_ref, bf16[8,16,1,1,128,128]{5,4,3,2,1,0:T(8,128)(2,1)} %bitcast.3.refs_0_, f32[13,8,128]{2,1,0:T(8,128)S(1)} %scatter.9.refs_1_, f32[1024,3]{1,0:T(8,128)S(1)} %copy-done.6, bf16[1024,1024]{1,0:T(8,128)(2,1)S(1)} %copy-done.2, ...), custom_call_target="tpu_custom_call" | custom-call | flops 6979321856 | bytes 11010048 | tf_op jit(solution)/shard_map/pallas_call | solution.py:144
  167.3 0.0 copy-start.7
  167.3 0.0 copy-start.8
  167.3 0.0 copy-start.9
  167.3 1.8 all-to-all-done.3.x_ref
  169.2 5.3 %all-to-all-start.1 = ((bf16[8,1,13,128,128]{4,3,2,1,0:T(8,128)(2,1)}), bf16[8,1,13,128,128]{4,3,2,1,0:T(8,128)(2,1)}, u32[]{:S(2)}, u32[]{:S(2)}) async-start(bf16[8,1,13,128,128]{4,3,2,1,0:T(8,128)(2,1)} %shard_map.137), calls=%async_computation.1 | async-start | bytes 6815744 | tf_op jit(solution)/shard_map/all_to_all | solution.py:255
  174.5 0.0 copy-done.7
  174.5 0.0 copy-done.8
  174.5 0.0 copy-done.9
  174.5 3.3 %shard_map.140.refs_0_ = bf16[2,16,128,1024]{3,2,1,0:T(8,128)(2,1)} custom-call(s32[128]{0:T(128)S(1)} %copy-done.9, s32[128]{0:T(128)S(1)} %copy-done.8, s32[128]{0:T(128)S(1)} %copy-done.7, bf16[8,1,13,128,128]{4,3,2,1,0:T(8,128)(2,1)S(1)} %all-to-all-done.3.x_ref), custom_call_target="tpu_custom_call" | custom-call | tf_op jit(solution)/shard_map/pallas_call | solution.py:192
  177.8 37.1 %all-to-all-done.1.x_ref = bf16[8,1,13,128,128]{4,3,2,1,0:T(8,128)(2,1)} async-done(((bf16[8,1,13,128,128]{4,3,2,1,0:T(8,128)(2,1)}), bf16[8,1,13,128,128]{4,3,2,1,0:T(8,128)(2,1)}, u32[]{:S(2)}, u32[]{:S(2)}) %all-to-all-start.1) | async-done | bytes 3407904 | tf_op jit(solution)/shard_map/all_to_all | solution.py:255
  214.9 5.2 %shard_map.141 = bf16[2,16,128,1024]{3,2,1,0:T(8,128)(2,1)} custom-call(s32[128]{0:T(128)S(1)} %copy-done.9, s32[128]{0:T(128)S(1)} %copy-done.8, s32[128]{0:T(128)S(1)} %copy-done.7, bf16[8,1,13,128,128]{4,3,2,1,0:T(8,128)(2,1)} %all-to-all-done.1.x_ref, bf16[2,16,128,1024]{3,2,1,0:T(8,128)(2,1)} %shard_map.140.refs_0_), custom_call_target="tpu_custom_call", output_to_operand_aliasing={{}: (4, {})} | custom-call | tf_op jit(solution)/shard_map/pallas_call | solution.py:192
  (7 shorter events, 0.1 us)
Async XLA Ops:
  0.0 75.9 %copy-start = (s32[256]{0:T(256)S(1)}, s32[256]{0:T(256)}, u32[]{:S(2)}) copy-start(s32[256]{0:T(256)} %param.25) | copy-start | bytes 3076
  4.8 63.1 %all-to-all-start.2 = ((bf16[128,1,1,128,128]{4,3,2,1,0:T(8,128)(2,1)}), bf16[128,1,1,128,128]{4,3,2,1,0:T(8,128)(2,1)}, u32[]{:S(2)}, u32[]{:S(2)}) async-start(bf16[128,1,1,128,128]{4,3,2,1,0:T(8,128)(2,1)} %bitcast.19), calls=%async_computation.2 | async-start | bytes 8388608 | tf_op jit(solution)/shard_map/all_to_all | solution.py:227
  67.9 6.3 %copy-start.10 = (s32[256]{0:T(256)S(1)}, s32[256]{0:T(256)}, u32[]{:S(2)}) copy-start(s32[256]{0:T(256)} %order_ref.3) | copy-start | bytes 3076
  67.9 7.0 %copy-start.12 = (f32[1024]{0:T(1024)S(1)}, f32[1024]{0:T(1024)}, u32[]{:S(2)}) copy-start(f32[1024]{0:T(1024)} %param.22) | copy-start | bytes 12292
  67.9 7.0 %copy-start.13 = (f32[1024]{0:T(1024)S(1)}, f32[1024]{0:T(1024)}, u32[]{:S(2)}) copy-start(f32[1024]{0:T(1024)} %param.21) | copy-start | bytes 12292
  67.9 10.4 %copy-start.11 = (bf16[1024,1024]{1,0:T(8,128)(2,1)S(1)}, bf16[1024,1024]{1,0:T(8,128)(2,1)}, u32[]{:S(2)}) copy-start(bf16[1024,1024]{1,0:T(8,128)(2,1)} %param.24) | copy-start | bytes 6291460
  67.9 56.7 %all-to-all-start = ((bf16[128,1,1,128,128]{4,3,2,1,0:T(8,128)(2,1)}), bf16[128,1,1,128,128]{4,3,2,1,0:T(8,128)(2,1)}, u32[]{:S(2)}, u32[]{:S(2)}) async-start(bf16[128,1,1,128,128]{4,3,2,1,0:T(8,128)(2,1)} %bitcast.18), calls=%async_computation | async-start | bytes 8388608 | tf_op jit(solution)/shard_map/all_to_all | solution.py:227
  75.2 5.3 %copy-start.5 = (f32[1024,3]{1,0:T(8,128)}, f32[1024,3]{1,0:T(8,128)S(1)}, u32[]{:S(2)}) copy-start(f32[1024,3]{1,0:T(8,128)S(1)} %copy.19.refs_2_) | copy-start | bytes 36868
  114.7 1.3 copy-start.1
  116.0 1.4 copy-start.3
  124.6 44.5 %all-to-all-start.3 = ((bf16[8,1,13,128,128]{4,3,2,1,0:T(8,128)(2,1)}), bf16[8,1,13,128,128]{4,3,2,1,0:T(8,128)(2,1)S(1)}, u32[]{:S(2)}, u32[]{:S(2)}) async-start(bf16[8,1,13,128,128]{4,3,2,1,0:T(8,128)(2,1)} %shard_map.139), calls=%async_computation.3 | async-start | bytes 6815744 | tf_op jit(solution)/shard_map/all_to_all | solution.py:255
  128.9 1.6 copy-start.2
  130.5 1.6 copy-start.4
  132.1 1.0 copy-start.6
  167.3 7.2 %copy-start.7 = (s32[128]{0:T(128)S(1)}, s32[128]{0:T(128)}, u32[]{:S(2)}) copy-start(s32[128]{0:T(128)} %constant.127.clone.ok_ref) | copy-start | bytes 1540
  167.3 7.2 %copy-start.8 = (s32[128]{0:T(128)S(1)}, s32[128]{0:T(128)}, u32[]{:S(2)}) copy-start(s32[128]{0:T(128)} %constant.126.clone.j_ref) | copy-start | bytes 1540
  167.3 7.2 %copy-start.9 = (s32[128]{0:T(128)S(1)}, s32[128]{0:T(128)}, u32[]{:S(2)}) copy-start(s32[128]{0:T(128)} %constant.125.clone.r_ref) | copy-start | bytes 1540
  169.2 45.7 %all-to-all-start.1 = ((bf16[8,1,13,128,128]{4,3,2,1,0:T(8,128)(2,1)}), bf16[8,1,13,128,128]{4,3,2,1,0:T(8,128)(2,1)}, u32[]{:S(2)}, u32[]{:S(2)}) async-start(bf16[8,1,13,128,128]{4,3,2,1,0:T(8,128)(2,1)} %shard_map.137), calls=%async_computation.1 | async-start | bytes 6815744 | tf_op jit(solution)/shard_map/all_to_all | solution.py:255
